TPU v7x, 512 devices: a whole 4x4x16 slice. The times are simulated.
512 devices in a mesh: seq: 64 (over z, y), tp: 8 (over x, core).
Axes of the slice: x: 4, y: 4, z: 16, core: 2. Of those that a mesh axis runs over, the one named last changes fastest.
Arguments:
- queries: bfloat16 [64, 32, 4096], P('seq', None, 'tp'), may hold values from -15 to 15
- tree_keys: bfloat16 [64, 32, 1024], P('seq', None, 'tp'), may hold values from -15 to 15
- tree_values: bfloat16 [64, 32, 1024], P('seq', None, 'tp'), may hold values from -6 to 6
- cache_keys: bfloat16 [36864, 1024], P('seq', 'tp'), may hold values from -15 to 15
- cache_values: bfloat16 [36864, 1024], P('seq', 'tp'), may hold values from -6 to 6
- residual: bfloat16 [64, 32, 4096], P('seq', None, 'tp'), may hold values from -6 to 6
- out_weight: bfloat16 [4096, 4096], P('tp'), may hold values from -0.125 to 0.125
- cache_len: int32 [64], replicated, may hold values from 88 to 1720, as said below
- parents: int32 [64, 32], P('seq'), may hold values from -1 to 30, as said below
- accept_rows: int32 [64, 8], P('seq'), may hold values from 0 to 31, as said below
- accept_len: int32 [64], replicated, may hold values from 1 to 8
Outputs:
- mixed: bfloat16 [64, 32, 4096], P('seq', None, 'tp')
- new_cache_keys: bfloat16 [36864, 1024], P('seq', 'tp')
- new_cache_values: bfloat16 [36864, 1024], P('seq', 'tp')
Inputs may be any that keep to these rules, and one draw needn't show every extreme that they name: Requests form aligned groups of 4 (requests 4 g to 4 g + 3). Request r owns cache_len[r] + 8 pool positions, these regions follow one another in request order from position 0, and the regions of one group fill exactly 2304 positions, so that group g's caches lie in pool positions 4 * 576 * g to 4 * 576 * (g + 1) - 1. parents[r, 0] = -1, and 0 <= parents[r, i] < i for i > 0. `accept_rows`: entries 0 to accept_len[r] - 1 are a chain of tree tokens that starts at token 0, each entry's parent being the entry before it; later entries are 31 and are not used.
All inputs are finite; a program needn't handle non-finite values.
Results may differ from a plain program's by a relative error of at most 0.009.
Values may be sent and summed in bfloat16 or wider, within the bound.
No kernel may reach another device: no remote copies, remote signals or barrier semaphores. Data moves between devices by JAX's collectives and lax.ppermute only.
A program may use at most 64 MiB of HBM per device.

v0:
```python
import math

import jax
import jax.numpy as jnp
from jax import lax
from jax.sharding import PartitionSpec as P

HD = 128
TREE = 32
A_MAX = 8
GROUP = 4


NEG = -1e30


def partner_2(block, axis, stride):
    count = lax.axis_size(axis)
    route = []
    for low in range(count):
        high = low | 1 << stride
        if high != low and high < count:
            route += [(low, high), (high, low)]
    return lax.ppermute(block, axis, route)


def ancestry(parents):
    length = parents.shape[-1]
    members = jnp.arange(length, dtype=jnp.int32)
    ancestors = members[:, None] == members[None, :]
    current = parents
    for repeat in range(length - 1):
        ancestors = ancestors | (current[..., None] == members)
        hopped = jnp.take_along_axis(parents, jnp.maximum(current, 0), axis=-1)
        current = jnp.where(current >= 0, hopped, -1)
    return ancestors


def scale_heads(values, factors):
    return (values.reshape(factors.shape + (HD,)) * factors[..., None]).reshape(values.shape)


def combine(first_set, second_set):
    first_out, first_top, first_total = first_set
    second_out, second_top, second_total = second_set
    joint_top = jnp.maximum(first_top, second_top)
    first_factor = jnp.exp(first_top - joint_top)
    second_factor = jnp.exp(second_top - joint_top)
    joint_out = scale_heads(first_out, first_factor) + scale_heads(second_out, second_factor)
    return (joint_out, joint_top, first_total * first_factor + second_total * second_factor)


def on_device(
    queries,
    tree_keys,
    tree_values,
    cache_keys,
    cache_values,
    residual,
    out_weight,
    cache_len,
    parents,
    accept_rows,
    accept_len,
):
    seq_rank = lax.axis_index("seq")
    positions = cache_keys.shape[0]
    channels = cache_keys.shape[1]
    kv_local = channels // HD
    q_width = queries.shape[2]
    heads_local = q_width // HD
    sharing = heads_local // kv_local
    factor = 1.0 / math.sqrt(HD)
    regions = cache_len + A_MAX
    starts = jnp.cumsum(regions) - regions
    low_edge = seq_rank * positions
    places = low_edge + jnp.arange(positions, dtype=jnp.int32)
    keys_local = cache_keys.reshape(positions, kv_local, HD)
    values_local = cache_values.reshape(positions, kv_local, HD)
    tree_pair = jnp.concatenate([tree_keys[0], tree_values[0]], axis=-1)
    mine_rows = jnp.take(tree_pair, accept_rows[0], axis=0)[None]
    group_base = seq_rank // GROUP * GROUP
    levels = GROUP.bit_length() - 1
    gathered_q = queries
    for level in range(levels):
        partner = partner_2(gathered_q, "seq", level)
        upper_half = seq_rank // 2**level % 2 == 1
        gathered_q = jnp.where(
            upper_half,
            jnp.concatenate([partner, gathered_q], 0),
            jnp.concatenate([gathered_q, partner], 0),
        )
    number = gathered_q.shape[0]
    begin = lax.dynamic_slice_in_dim(starts, group_base, number)
    length = lax.dynamic_slice_in_dim(cache_len, group_base, number)
    inside = (places[None, :] >= begin[:, None]) & (places[None, :] < (begin + length)[:, None])
    shaped = gathered_q.reshape(number, TREE, kv_local, sharing, HD)
    scores = (
        jnp.einsum("rtkgd,pkd->rkgtp", shaped, keys_local, preferred_element_type=jnp.float32)
        * factor
    )
    valid = inside[:, None, None, None, :]
    top_score = jnp.max(jnp.where(valid, scores, NEG), axis=-1)
    raised = jnp.where(valid, jnp.exp(scores - top_score[..., None]), 0.0)
    total = jnp.sum(raised, axis=-1)
    summed = jnp.einsum(
        "rkgtp,pkd->rtkgd",
        raised.astype(jnp.bfloat16),
        values_local,
        preferred_element_type=jnp.float32,
    )
    top_rows = jnp.transpose(top_score, (0, 3, 1, 2)).reshape(number, TREE, heads_local)
    total_rows = jnp.transpose(total, (0, 3, 1, 2)).reshape(number, TREE, heads_local)
    partial_set = (summed.reshape(number, TREE, q_width), top_rows, total_rows)
    within = seq_rank - group_base
    for level in range(levels):
        partner_set = partner_2((partial_set[0], partial_set[1], partial_set[2]), "seq", level)
        partial_set = combine(partial_set, partner_set)
    cache_part = tuple((lax.dynamic_slice_in_dim(member, within, 1, 0) for member in partial_set))
    row_block = mine_rows
    for level in range(levels):
        partner_rows = partner_2(row_block, "seq", level)
        upper_half = seq_rank // 2**level % 2 == 1
        row_block = jnp.where(
            upper_half,
            jnp.concatenate([partner_rows, row_block], 0),
            jnp.concatenate([row_block, partner_rows], 0),
        )
    linked = ancestry(parents[0])
    shaped_q = queries[0].reshape(TREE, kv_local, sharing, HD)
    own_keys = tree_keys[0].reshape(TREE, kv_local, HD)
    own_values = tree_values[0].reshape(TREE, kv_local, HD)
    drafted = (
        jnp.einsum("tkgd,jkd->kgtj", shaped_q, own_keys, preferred_element_type=jnp.float32)
        * factor
    )
    tree_top = jnp.max(jnp.where(linked, drafted, NEG), axis=-1)
    tree_raised = jnp.where(linked, jnp.exp(drafted - tree_top[..., None]), 0.0)
    tree_total = jnp.sum(tree_raised, axis=-1)
    tree_out = jnp.einsum(
        "kgtj,jkd->tkgd",
        tree_raised.astype(jnp.bfloat16),
        own_values,
        preferred_element_type=jnp.float32,
    )
    tree_part = (
        tree_out.reshape(1, TREE, q_width),
        jnp.transpose(tree_top, (2, 0, 1)).reshape(1, TREE, heads_local),
        jnp.transpose(tree_total, (2, 0, 1)).reshape(1, TREE, heads_local),
    )
    joint_out, joint_top, joint_total = combine(cache_part, tree_part)
    attention = scale_heads(joint_out, 1.0 / joint_total).astype(jnp.bfloat16)[0]
    summed_heads = lax.psum_scatter(
        lax.dot_general(
            out_weight, attention, (((0,), (1,)), ((), ())), preferred_element_type=jnp.float32
        ).astype(jnp.bfloat16),
        "tp",
        scatter_dimension=0,
        tiled=True,
    ).astype(jnp.float32)
    mixed = (residual[0].astype(jnp.float32) + summed_heads.T).astype(jnp.bfloat16)[None]
    row_count = row_block.shape[0]
    row_begin = lax.dynamic_slice_in_dim(starts, group_base, row_count)
    row_length = lax.dynamic_slice_in_dim(cache_len, group_base, row_count)
    row_accepted = lax.dynamic_slice_in_dim(accept_len, group_base, row_count)
    column = jnp.arange(A_MAX, dtype=jnp.int32)
    targets = row_begin[:, None] + row_length[:, None] + column[None, :] - low_edge
    keep_row = (column[None, :] < row_accepted[:, None]) & (targets >= 0) & (targets < positions)
    targets = jnp.where(keep_row, targets, positions).reshape(-1)
    joined = jnp.concatenate([cache_keys, cache_values], axis=-1)
    joined = joined.at[targets].set(row_block.reshape(-1, 2 * channels), mode="drop")
    return (mixed, joined[:, :channels], joined[:, channels:])


def solution(mesh):
    return jax.shard_map(
        on_device,
        mesh=mesh,
        in_specs=(
            P("seq", None, "tp"),
            P("seq", None, "tp"),
            P("seq", None, "tp"),
            P("seq", "tp"),
            P("seq", "tp"),
            P("seq", None, "tp"),
            P("tp", None),
            P(),
            P("seq", None),
            P("seq", None),
            P(),
        ),
        out_specs=(P("seq", None, "tp"), P("seq", "tp"), P("seq", "tp")),
        check_vma=False,
    )
```

profile of v0, /device:TPU:1, one launch (start us, length us, event | category | flops | bytes accessed | tf_op | source)
XLA Modules:
  0.0 134.4 jit_solution(12056536933621213473)
XLA Ops:
  7.2 4.0 %collective-permute-start = (bf16[1,32,512]{2,1,0:T(8,128)(2,1)}, bf16[1,32,512]{2,1,0:T(8,128)(2,1)S(1)}, u32[]{:S(2)}, u32[]{:S(2)}) collective-permute-start(bf16[1,32,512]{2,1,0:T(8,128)(2,1)} %param.13), channel_id=1, source_target_pairs={{0,8},{8,0},{16,24},{24,16},{32,40},{40,32},{48,56},{56,48},{64,72... | collective-permute-start | bytes 98312 | tf_op jit(solution)/shard_map/ppermute | solution.py:24
  12.6 0.7 pad_maximum_fusion.1
  13.9 1.9 %collective-permute-start.8 = (bf16[1,8,256]{2,1,0:T(8,128)(2,1)S(1)}, bf16[1,8,256]{2,1,0:T(8,128)(2,1)S(1)}, u32[]{:S(2)}, u32[]{:S(2)}) collective-permute-start(bf16[1,8,256]{2,1,0:T(8,128)(2,1)S(1)} %bitcast_select_fusion), channel_id=1, source_target_pairs={{0,8},{8,0},{16,24},{24,16},{32,40},{40,32},{48,56},{56,48},{64,72... | collective-permute-start | bytes 12296 | tf_op jit(solution)/shard_map/ppermute | solution.py:24
  15.9 0.8 reshape.410
  16.6 0.8 copy_bitcast_fusion.1
  18.1 1.4 %gather_fusion.1 = s32[32]{0:T(128)S(1)} fusion(s32[32]{0:T(128)} %bitcast.155, s32[1024]{0:T(1024)S(1)} %pad_clamp_fusion.30), kind=kCustom, calls=%fused_computation.clone | custom fusion | bytes 384 | tf_op jit(solution)/shard_map/jit(take_along_axis)/gather | solution.py:34
  20.1 1.4 %gather_fusion.2 = s32[32]{0:T(128)S(1)} fusion(s32[32]{0:T(128)} %bitcast.156, s32[1024]{0:T(1024)S(1)} %pad_clamp_fusion.29), kind=kCustom, calls=%fused_computation.1.clone | custom fusion | bytes 384 | tf_op jit(solution)/shard_map/jit(take_along_axis)/gather | solution.py:34
  21.5 0.7 gather_fusion.3
  22.2 0.7 gather_fusion.4
  22.9 0.7 gather_fusion.5
  23.7 0.7 gather_fusion.6
  24.4 0.7 gather_fusion.7
  25.1 0.7 gather_fusion.8
  25.8 0.7 gather_fusion.9
  26.6 0.7 gather_fusion.10
  27.3 0.7 gather_fusion.11
  28.0 0.7 gather_fusion.12
  28.7 0.7 gather_fusion.13
  29.5 0.7 gather_fusion.14
  30.2 0.7 gather_fusion.15
  30.9 0.7 gather_fusion.16
  32.4 0.7 gather_fusion.18
  33.1 0.7 gather_fusion.19
  33.8 0.7 gather_fusion.20
  34.5 0.7 gather_fusion.21
  36.0 0.7 gather_fusion.23
  36.7 0.7 gather_fusion.24
  37.4 0.7 gather_fusion.25
  38.2 0.7 gather_fusion.26
  38.9 0.7 gather_fusion.27
  39.7 0.7 gather_fusion.28
  40.4 0.7 gather_fusion.29
  43.1 5.0 %collective-permute-start.1 = (bf16[2,32,512]{2,1,0:T(8,128)(2,1)S(1)}, bf16[2,32,512]{2,1,0:T(8,128)(2,1)S(1)}, u32[]{:S(2)}, u32[]{:S(2)}) collective-permute-start(bf16[2,32,512]{2,1,0:T(8,128)(2,1)S(1)} %maximum_select_fusion.2), channel_id=1, source_target_pairs={{0,16},{16,0},{8,24},{24,8},{32,48},{48,32},{40,56},{56,40},{64,80... | collective-permute-start | bytes 196616 | tf_op jit(solution)/shard_map/ppermute | solution.py:24
  48.1 1.6 %collective-permute-done.1 = bf16[2,32,512]{2,1,0:T(8,128)(2,1)S(1)} collective-permute-done((bf16[2,32,512]{2,1,0:T(8,128)(2,1)S(1)}, bf16[2,32,512]{2,1,0:T(8,128)(2,1)S(1)}, u32[]{:S(2)}, u32[]{:S(2)}) %collective-permute-start.1) | collective-permute-done | bytes 65568 | tf_op jit(solution)/shard_map/ppermute | solution.py:24
  50.6 3.2 %collective-permute-start.6 = (f32[4,32,4]{1,2,0:T(4,128)S(1)}, f32[4,32,4]{1,2,0:T(4,128)S(1)}, u32[]{:S(2)}, u32[]{:S(2)}) collective-permute-start(f32[4,32,4]{1,2,0:T(4,128)S(1)} %bitcast.193), channel_id=1, source_target_pairs={{0,8},{8,0},{16,24},{24,16},{32,40},{40,32},{48,56},{56,48},{64,72... | collective-permute-start | bytes 6152 | tf_op jit(solution)/shard_map/ppermute | solution.py:24
  53.9 2.0 %collective-permute-start.2 = (f32[4,32,4]{1,2,0:T(4,128)S(1)}, f32[4,32,4]{1,2,0:T(4,128)S(1)}, u32[]{:S(2)}, u32[]{:S(2)}) collective-permute-start(f32[4,32,4]{1,2,0:T(4,128)S(1)} %bitcast.192), channel_id=1, source_target_pairs={{0,8},{8,0},{16,24},{24,16},{32,40},{40,32},{48,56},{56,48},{64,72... | collective-permute-start | bytes 6152 | tf_op jit(solution)/shard_map/ppermute | solution.py:24
  56.7 3.2 %collective-permute-start.3 = (f32[4,32,512]{2,1,0:T(8,128)S(1)}, f32[4,32,512]{2,1,0:T(8,128)S(1)}, u32[]{:S(2)}, u32[]{:S(2)}) collective-permute-start(f32[4,32,512]{2,1,0:T(8,128)S(1)} %reshape_reshape.6), channel_id=1, source_target_pairs={{0,8},{8,0},{16,24},{24,16},{32,40},{40,32},{48,56},{56,48},{64,72... | collective-permute-start | bytes 786440 | tf_op jit(solution)/shard_map/ppermute | solution.py:24
  60.0 4.5 %collective-permute-start.4 = (f32[4,32,4]{1,2,0:T(4,128)S(1)}, f32[4,32,4]{1,2,0:T(4,128)S(1)}, u32[]{:S(2)}, u32[]{:S(2)}) collective-permute-start(f32[4,32,4]{1,2,0:T(4,128)S(1)} %get-tuple-element.9), channel_id=1, source_target_pairs={{0,16},{16,0},{8,24},{24,8},{32,48},{48,32},{40,56},{56,40},{64,80... | collective-permute-start | bytes 6152 | tf_op jit(solution)/shard_map/ppermute | solution.py:24
  65.7 2.3 %collective-permute-start.7 = (f32[4,32,4]{1,2,0:T(4,128)S(1)}, f32[4,32,4]{1,2,0:T(4,128)S(1)}, u32[]{:S(2)}, u32[]{:S(2)}) collective-permute-start(f32[4,32,4]{1,2,0:T(4,128)S(1)} %get-tuple-element.6), channel_id=1, source_target_pairs={{0,16},{16,0},{8,24},{24,8},{32,48},{48,32},{40,56},{56,40},{64,80... | collective-permute-start | bytes 6152 | tf_op jit(solution)/shard_map/ppermute | solution.py:24
  68.1 4.5 %collective-permute-start.5 = (f32[4,32,512]{2,1,0:T(8,128)S(1)}, f32[4,32,512]{2,1,0:T(8,128)S(1)}, u32[]{:S(2)}, u32[]{:S(2)}) collective-permute-start(f32[4,32,512]{2,1,0:T(8,128)S(1)} %multiply_add_fusion), channel_id=1, source_target_pairs={{0,16},{16,0},{8,24},{24,8},{32,48},{48,32},{40,56},{56,40},{64,80... | collective-permute-start | bytes 786440 | tf_op jit(solution)/shard_map/ppermute | solution.py:24
  74.2 2.5 %collective-permute-done.5 = f32[4,32,512]{2,1,0:T(8,128)S(1)} collective-permute-done((f32[4,32,512]{2,1,0:T(8,128)S(1)}, f32[4,32,512]{2,1,0:T(8,128)S(1)}, u32[]{:S(2)}, u32[]{:S(2)}) %collective-permute-start.5) | collective-permute-done | bytes 262176 | tf_op jit(solution)/shard_map/ppermute | solution.py:24
  76.7 3.7 %fusion = bf16[4096,32]{0,1:T(8,128)(2,1)} fusion(bf16[512,4096]{1,0:T(8,128)(2,1)} %param.19, f32[1,32,512]{2,1,0:T(8,128)S(1)} %mul.188, f32[1,32,512]{2,1,0:T(8,128)S(1)} %mul.174, f32[4,32,512]{2,1,0:T(8,128)S(1)} %mul.166, s32[]{:T(128)S(6)} %select_n.253, f32[4,32,512]{2,1,0:T(8,128)S(1)} %collective-permute-done.5, f32[4,32,512]{2,1,0:T(8,128)S(1)} %mul.163, ...), kind=kOutput, calls=%fused_computation.33 | convolution fusion | flops 134479872 | bytes 4980740 | tf_op jit(solution)/shard_map/dot_general | solution.py:154
  80.4 4.5 %collective-permute-start.9 = (bf16[2,8,256]{2,1,0:T(8,128)(2,1)S(1)}, bf16[2,8,256]{2,1,0:T(8,128)(2,1)S(1)}, u32[]{:S(2)}, u32[]{:S(2)}) collective-permute-start(bf16[2,8,256]{2,1,0:T(8,128)(2,1)S(1)} %maximum_select_fusion.5), channel_id=1, source_target_pairs={{0,16},{16,0},{8,24},{24,8},{32,48},{48,32},{40,56},{56,40},{64,80... | collective-permute-start | bytes 24584 | tf_op jit(solution)/shard_map/ppermute | solution.py:24
  85.0 1.3 collective-permute-done.9
  86.3 0.9 scatter_custom_fusion
  87.3 0.7 fusion.94
  88.0 38.2 %reduce-scatter.2.cloned.1.call-done = bf16[512,32]{0,1:T(8,128)(2,1)} async-done(((bf16[4096,32]{0,1:T(8,128)(2,1)}), bf16[512,32]{0,1:T(8,128)(2,1)}) %reduce-scatter.2.cloned.1.call-update) | async-done | bytes 32784 | tf_op jit(solution)/shard_map/reduce_scatter | solution.py:153
  126.1 1.4 %fusion.28 = bf16[1,32,512]{2,1,0:T(8,128)(2,1)} fusion(bf16[512,32]{0,1:T(8,128)(2,1)} %reduce-scatter.2.cloned.1.call-done, bf16[1,32,512]{2,1,0:T(8,128)(2,1)S(1)} %copy-done.4), kind=kLoop, calls=%fused_computation.77 | loop fusion | flops 65536 | bytes 98304 | tf_op jit(solution)/shard_map/broadcast_in_dim | solution.py:161
  (152 shorter events, 11.5 us)
Async XLA Ops:
  7.2 14.3 %copy-start = (s32[1,32]{1,0:T(1,128)S(1)}, s32[1,32]{1,0:T(1,128)}, u32[]{:S(2)}) copy-start(s32[1,32]{1,0:T(1,128)} %param.21) | copy-start | bytes 388
  7.2 119.0 %reduce-scatter.2.cloned.1.call-start = ((), (), s32[]{:S(2)}) async-start(), calls=%async_computation.1 | async-start | bytes 294912 | tf_op jit(solution)/shard_map/reduce_scatter | solution.py:153
  7.2 35.9 %collective-permute-start = (bf16[1,32,512]{2,1,0:T(8,128)(2,1)}, bf16[1,32,512]{2,1,0:T(8,128)(2,1)S(1)}, u32[]{:S(2)}, u32[]{:S(2)}) collective-permute-start(bf16[1,32,512]{2,1,0:T(8,128)(2,1)} %param.13), channel_id=1, source_target_pairs={{0,8},{8,0},{16,24},{24,16},{32,40},{40,32},{48,56},{56,48},{64,72... | collective-permute-start | bytes 98312 | tf_op jit(solution)/shard_map/ppermute | solution.py:24
  13.9 66.5 %collective-permute-start.8 = (bf16[1,8,256]{2,1,0:T(8,128)(2,1)S(1)}, bf16[1,8,256]{2,1,0:T(8,128)(2,1)S(1)}, u32[]{:S(2)}, u32[]{:S(2)}) collective-permute-start(bf16[1,8,256]{2,1,0:T(8,128)(2,1)S(1)} %bitcast_select_fusion), channel_id=1, source_target_pairs={{0,8},{8,0},{16,24},{24,16},{32,40},{40,32},{48,56},{56,48},{64,72... | collective-permute-start | bytes 12296 | tf_op jit(solution)/shard_map/ppermute | solution.py:24
  38.1 3.8 %copy-start.7 = (s32[64]{0:T(128)S(1)}, s32[64]{0:T(128)}, u32[]{:S(2)}) copy-start(s32[64]{0:T(128)} %param.20) | copy-start | bytes 772
  38.2 4.3 %copy-start.8 = (s32[64]{0:T(128)S(1)}, s32[64]{0:T(128)}, u32[]{:S(2)}) copy-start(s32[64]{0:T(128)} %param.23) | copy-start | bytes 772
  38.2 4.4 %copy-start.5 = (bf16[1,32,128]{2,1,0:T(8,128)(2,1)S(1)}, bf16[1,32,128]{2,1,0:T(8,128)(2,1)}, u32[]{:S(2)}) copy-start(bf16[1,32,128]{2,1,0:T(8,128)(2,1)} %param.14) | copy-start | bytes 24580
  38.9 4.0 %copy-start.6 = (bf16[1,32,128]{2,1,0:T(8,128)(2,1)S(1)}, bf16[1,32,128]{2,1,0:T(8,128)(2,1)}, u32[]{:S(2)}) copy-start(bf16[1,32,128]{2,1,0:T(8,128)(2,1)} %param.15) | copy-start | bytes 24580
  38.9 4.2 %copy-start.1 = (bf16[1,32,512]{2,1,0:T(8,128)(2,1)S(1)}, bf16[1,32,512]{2,1,0:T(8,128)(2,1)}, u32[]{:S(2)}) copy-start(bf16[1,32,512]{2,1,0:T(8,128)(2,1)} %param.13) | copy-start | bytes 98308
  39.6 10.1 %copy-start.2 = (bf16[576,128]{1,0:T(8,128)(2,1)S(1)}, bf16[576,128]{1,0:T(8,128)(2,1)}, u32[]{:S(2)}) copy-start(bf16[576,128]{1,0:T(8,128)(2,1)} %param.16) | copy-start | bytes 442372
  43.1 6.6 %collective-permute-start.1 = (bf16[2,32,512]{2,1,0:T(8,128)(2,1)S(1)}, bf16[2,32,512]{2,1,0:T(8,128)(2,1)S(1)}, u32[]{:S(2)}, u32[]{:S(2)}) collective-permute-start(bf16[2,32,512]{2,1,0:T(8,128)(2,1)S(1)} %maximum_select_fusion.2), channel_id=1, source_target_pairs={{0,16},{16,0},{8,24},{24,8},{32,48},{48,32},{40,56},{56,40},{64,80... | collective-permute-start | bytes 196616 | tf_op jit(solution)/shard_map/ppermute | solution.py:24
  49.8 6.2 %copy-start.3 = (bf16[576,128]{1,0:T(8,128)(2,1)S(1)}, bf16[576,128]{1,0:T(8,128)(2,1)}, u32[]{:S(2)}) copy-start(bf16[576,128]{1,0:T(8,128)(2,1)} %param.17) | copy-start | bytes 442372
  50.6 9.3 %collective-permute-start.6 = (f32[4,32,4]{1,2,0:T(4,128)S(1)}, f32[4,32,4]{1,2,0:T(4,128)S(1)}, u32[]{:S(2)}, u32[]{:S(2)}) collective-permute-start(f32[4,32,4]{1,2,0:T(4,128)S(1)} %bitcast.193), channel_id=1, source_target_pairs={{0,8},{8,0},{16,24},{24,16},{32,40},{40,32},{48,56},{56,48},{64,72... | collective-permute-start | bytes 6152 | tf_op jit(solution)/shard_map/ppermute | solution.py:24
  53.9 6.1 %collective-permute-start.2 = (f32[4,32,4]{1,2,0:T(4,128)S(1)}, f32[4,32,4]{1,2,0:T(4,128)S(1)}, u32[]{:S(2)}, u32[]{:S(2)}) collective-permute-start(f32[4,32,4]{1,2,0:T(4,128)S(1)} %bitcast.192), channel_id=1, source_target_pairs={{0,8},{8,0},{16,24},{24,16},{32,40},{40,32},{48,56},{56,48},{64,72... | collective-permute-start | bytes 6152 | tf_op jit(solution)/shard_map/ppermute | solution.py:24
  56.7 11.2 %collective-permute-start.3 = (f32[4,32,512]{2,1,0:T(8,128)S(1)}, f32[4,32,512]{2,1,0:T(8,128)S(1)}, u32[]{:S(2)}, u32[]{:S(2)}) collective-permute-start(f32[4,32,512]{2,1,0:T(8,128)S(1)} %reshape_reshape.6), channel_id=1, source_target_pairs={{0,8},{8,0},{16,24},{24,16},{32,40},{40,32},{48,56},{56,48},{64,72... | collective-permute-start | bytes 786440 | tf_op jit(solution)/shard_map/ppermute | solution.py:24
  60.0 7.9 %collective-permute-start.4 = (f32[4,32,4]{1,2,0:T(4,128)S(1)}, f32[4,32,4]{1,2,0:T(4,128)S(1)}, u32[]{:S(2)}, u32[]{:S(2)}) collective-permute-start(f32[4,32,4]{1,2,0:T(4,128)S(1)} %get-tuple-element.9), channel_id=1, source_target_pairs={{0,16},{16,0},{8,24},{24,8},{32,48},{48,32},{40,56},{56,40},{64,80... | collective-permute-start | bytes 6152 | tf_op jit(solution)/shard_map/ppermute | solution.py:24
  65.7 7.8 %collective-permute-start.7 = (f32[4,32,4]{1,2,0:T(4,128)S(1)}, f32[4,32,4]{1,2,0:T(4,128)S(1)}, u32[]{:S(2)}, u32[]{:S(2)}) collective-permute-start(f32[4,32,4]{1,2,0:T(4,128)S(1)} %get-tuple-element.6), channel_id=1, source_target_pairs={{0,16},{16,0},{8,24},{24,8},{32,48},{48,32},{40,56},{56,40},{64,80... | collective-permute-start | bytes 6152 | tf_op jit(solution)/shard_map/ppermute | solution.py:24
  68.1 8.6 %collective-permute-start.5 = (f32[4,32,512]{2,1,0:T(8,128)S(1)}, f32[4,32,512]{2,1,0:T(8,128)S(1)}, u32[]{:S(2)}, u32[]{:S(2)}) collective-permute-start(f32[4,32,512]{2,1,0:T(8,128)S(1)} %multiply_add_fusion), channel_id=1, source_target_pairs={{0,16},{16,0},{8,24},{24,8},{32,48},{48,32},{40,56},{56,40},{64,80... | collective-permute-start | bytes 786440 | tf_op jit(solution)/shard_map/ppermute | solution.py:24
  80.4 45.8 %copy-start.4 = (bf16[1,32,512]{2,1,0:T(8,128)(2,1)S(1)}, bf16[1,32,512]{2,1,0:T(8,128)(2,1)}, u32[]{:S(2)}) copy-start(bf16[1,32,512]{2,1,0:T(8,128)(2,1)} %param.18) | copy-start | bytes 98308
  80.4 5.9 %collective-permute-start.9 = (bf16[2,8,256]{2,1,0:T(8,128)(2,1)S(1)}, bf16[2,8,256]{2,1,0:T(8,128)(2,1)S(1)}, u32[]{:S(2)}, u32[]{:S(2)}) collective-permute-start(bf16[2,8,256]{2,1,0:T(8,128)(2,1)S(1)} %maximum_select_fusion.5), channel_id=1, source_target_pairs={{0,16},{16,0},{8,24},{24,8},{32,48},{48,32},{40,56},{56,40},{64,80... | collective-permute-start | bytes 24584 | tf_op jit(solution)/shard_map/ppermute | solution.py:24
Sparse Core Ops, SparseCore 0:
  80.5 45.5 reduce-scatter.1
where the time goes:
time: 136 us; the launch traced here: 134 us
  waiting for transfers between devices  43.6 us (32%)
  starting transfers between devices  35.3 us (26%)
  local copies, waits for them, and re-layouts  28.1 us (21%)
  between operations  14.8 us (11%)
  other arithmetic  7.54 us (6%)
  matrix products  4.97 us (4%)
    reduce_scatter x1, waiting for transfers between devices, on_device(): lax.psum_scatter(lax.dot_general(out_weight, attention, (((0,), (1,)), ((...  38.2 us
    ppermute x10, starting transfers between devices, partner_2(): return lax.ppermute(block, axis, route)  35.3 us
    gather x30, local copies, waits for them, and re-layouts, ancestry(): hopped = jnp.take_along_axis(parents, jnp.maximum(current, 0), axis=-1)  22.2 us
    ppermute x10, waiting for transfers between devices, partner_2(): return lax.ppermute(block, axis, route)  5.44 us
    dot_general x1, matrix products, on_device(): lax.dot_general(out_weight, attention, (((0,), (1,)), ((), ())), preferre...  3.7 us
  transfers between devices with their start and end apart: 11, of which 4 were waited for; matrix products, arithmetic and copies ran while one was open for 29% of the time, Pallas kernels for 0%

commit v1 on v0

v1 whole, which is shorter than its diff:
```python
import math

import jax
import jax.numpy as jnp
import numpy as np
from jax import lax
from jax.sharding import Mesh
from jax.sharding import PartitionSpec as P

HD = 128
TREE = 32
A_MAX = 8
GROUP = 4


NEG = -1e30


def ancestry(parents):
    length = parents.shape[-1]
    members = jnp.arange(length, dtype=jnp.int32)
    step = (members[:, None] == members[None, :]) | (parents[:, None] == members[None, :])
    reach = step.astype(jnp.bfloat16)
    covered = 1
    while covered < length - 1:
        reach = (
            jnp.dot(reach, reach, preferred_element_type=jnp.float32) > 0
        ).astype(jnp.bfloat16)
        covered *= 2
    return reach > 0


def scale_heads(values, factors):
    return (values.reshape(factors.shape + (HD,)) * factors[..., None]).reshape(values.shape)


def on_device(
    queries,
    tree_keys,
    tree_values,
    cache_keys,
    cache_values,
    residual,
    out_weight,
    cache_len,
    parents,
    accept_rows,
    accept_len,
):
    member = lax.axis_index("mem")
    seq_rank = lax.axis_index("grp") * GROUP + member
    positions = cache_keys.shape[0]
    channels = cache_keys.shape[1]
    kv_local = channels // HD
    q_width = queries.shape[2]
    heads_local = q_width // HD
    sharing = heads_local // kv_local
    factor = 1.0 / math.sqrt(HD)
    regions = cache_len + A_MAX
    starts = jnp.cumsum(regions) - regions
    low_edge = seq_rank * positions
    places = low_edge + jnp.arange(positions, dtype=jnp.int32)
    keys_local = cache_keys.reshape(positions, kv_local, HD)
    values_local = cache_values.reshape(positions, kv_local, HD)

    tree_pair = jnp.concatenate([tree_keys[0], tree_values[0]], axis=-1)
    mine_rows = jnp.take(tree_pair, accept_rows[0], axis=0)
    q_size = TREE * q_width
    packed = jnp.concatenate([queries[0].reshape(-1), mine_rows.reshape(-1)])
    sent = jnp.broadcast_to(packed[None], (GROUP, packed.shape[0]))
    got = lax.all_to_all(sent, "mem", 0, 0, tiled=True)
    gathered_q = got[:, :q_size].reshape(GROUP, TREE, q_width)
    row_block = got[:, q_size:].reshape(GROUP, A_MAX, 2 * channels)

    group_base = seq_rank - member
    begin = lax.dynamic_slice_in_dim(starts, group_base, GROUP)
    length = lax.dynamic_slice_in_dim(cache_len, group_base, GROUP)
    inside = (places[None, :] >= begin[:, None]) & (places[None, :] < (begin + length)[:, None])
    shaped = gathered_q.reshape(GROUP, TREE, kv_local, sharing, HD)
    scores = (
        jnp.einsum("rtkgd,pkd->rkgtp", shaped, keys_local, preferred_element_type=jnp.float32)
        * factor
    )
    valid = inside[:, None, None, None, :]
    top_score = jnp.max(jnp.where(valid, scores, NEG), axis=-1)
    raised = jnp.where(valid, jnp.exp(scores - top_score[..., None]), 0.0)
    total = jnp.sum(raised, axis=-1)
    summed = jnp.einsum(
        "rkgtp,pkd->rtkgd",
        raised.astype(jnp.bfloat16),
        values_local,
        preferred_element_type=jnp.float32,
    )
    top_rows = jnp.transpose(top_score, (0, 3, 1, 2)).reshape(GROUP, TREE, heads_local)
    total_rows = jnp.transpose(total, (0, 3, 1, 2)).reshape(GROUP, TREE, heads_local)
    partial = jnp.concatenate(
        [summed.reshape(GROUP, TREE, q_width), top_rows, total_rows], axis=-1
    )
    partials = lax.all_to_all(partial, "mem", 0, 0, tiled=True)
    part_out = partials[:, :, :q_width]
    part_top = partials[:, :, q_width : q_width + heads_local]
    part_total = partials[:, :, q_width + heads_local :]

    linked = ancestry(parents[0])
    shaped_q = queries[0].reshape(TREE, kv_local, sharing, HD)
    own_keys = tree_keys[0].reshape(TREE, kv_local, HD)
    own_values = tree_values[0].reshape(TREE, kv_local, HD)
    drafted = (
        jnp.einsum("tkgd,jkd->kgtj", shaped_q, own_keys, preferred_element_type=jnp.float32)
        * factor
    )
    tree_top = jnp.max(jnp.where(linked, drafted, NEG), axis=-1)
    tree_raised = jnp.where(linked, jnp.exp(drafted - tree_top[..., None]), 0.0)
    tree_total = jnp.sum(tree_raised, axis=-1)
    tree_out = jnp.einsum(
        "kgtj,jkd->tkgd",
        tree_raised.astype(jnp.bfloat16),
        own_values,
        preferred_element_type=jnp.float32,
    ).reshape(TREE, q_width)
    tree_top = jnp.transpose(tree_top, (2, 0, 1)).reshape(TREE, heads_local)
    tree_total = jnp.transpose(tree_total, (2, 0, 1)).reshape(TREE, heads_local)

    joint_top = jnp.maximum(jnp.max(part_top, axis=0), tree_top)
    part_factor = jnp.exp(part_top - joint_top[None])
    tree_factor = jnp.exp(tree_top - joint_top)
    joint_out = jnp.sum(scale_heads(part_out, part_factor), axis=0) + scale_heads(
        tree_out, tree_factor
    )
    joint_total = jnp.sum(part_total * part_factor, axis=0) + tree_total * tree_factor
    attention = scale_heads(joint_out, 1.0 / joint_total).astype(jnp.bfloat16)

    tp_size = lax.axis_size("tp")
    projected = jnp.dot(attention, out_weight, preferred_element_type=jnp.float32).astype(
        jnp.bfloat16
    )
    pieces = jnp.transpose(projected.reshape(TREE, tp_size, -1), (1, 0, 2))
    pieces = lax.all_to_all(pieces, "tp", 0, 0, tiled=True)
    summed_heads = jnp.sum(pieces.astype(jnp.float32), axis=0)
    mixed = (residual[0].astype(jnp.float32) + summed_heads).astype(jnp.bfloat16)[None]

    row_accepted = lax.dynamic_slice_in_dim(accept_len, group_base, GROUP)
    column = jnp.arange(A_MAX, dtype=jnp.int32)
    targets = begin[:, None] + length[:, None] + column[None, :] - low_edge
    keep_row = (column[None, :] < row_accepted[:, None]) & (targets >= 0) & (targets < positions)
    targets = jnp.where(keep_row, targets, positions).reshape(-1)
    rows = row_block.reshape(-1, 2 * channels)
    new_keys = cache_keys.at[targets].set(rows[:, :channels], mode="drop")
    new_values = cache_values.at[targets].set(rows[:, channels:], mode="drop")
    return (mixed, new_keys, new_values)


def solution(mesh):
    seq_size = mesh.shape["seq"]
    tp_size = mesh.shape["tp"]
    devices = np.asarray(mesh.devices).reshape(seq_size // GROUP, GROUP, tp_size)
    inner = Mesh(devices, ("grp", "mem", "tp"))
    seq = ("grp", "mem")
    return jax.shard_map(
        on_device,
        mesh=inner,
        in_specs=(
            P(seq, None, "tp"),
            P(seq, None, "tp"),
            P(seq, None, "tp"),
            P(seq, "tp"),
            P(seq, "tp"),
            P(seq, None, "tp"),
            P("tp", None),
            P(),
            P(seq, None),
            P(seq, None),
            P(),
        ),
        out_specs=(P(seq, None, "tp"), P(seq, "tp"), P(seq, "tp")),
        check_vma=False,
    )
```

time: 136 us -> 54.7 us (0.40)
  waiting for transfers between devices: 43.6 us -> 13.4 us
  local copies, waits for them, and re-layouts: 28.1 us -> 9.28 us
  starting transfers between devices: 35.3 us -> 19.2 us
  between operations: 14.8 us -> 0.98 us
    reduce_scatter x1 -> x0, waiting for transfers between devices: 38.2 us -> none  [on_device(): lax.psum_scatter(lax.dot_general(out_weight, attention, (((0,), (1,)), ((...]
    ppermute x10 -> x0, starting transfers between devices: 35.3 us -> none  [partner_2(): return lax.ppermute(block, axis, route)]
    gather x31 -> x1, local copies, waits for them, and re-layouts: 22.8 us -> 0.57 us  [on_device(): mine_rows = jnp.take(tree_pair, accept_rows[0], axis=0)]
    all_to_all x0 -> x3, starting transfers between devices: none -> 19.2 us  [the longest x1 10.8 us: on_device(): pieces = lax.all_to_all(pieces, 'tp', 0, 0, tiled=True)]
    all_to_all x0 -> x3, waiting for transfers between devices: none -> 13.4 us  [the longest x1 5.77 us: on_device(): partials = lax.all_to_all(partial, 'mem', 0, 0, tiled=True)]
    ppermute x10 -> x0, waiting for transfers between devices: 5.44 us -> none  [partner_2(): return lax.ppermute(block, axis, route)]
    unnamed x18 -> x25, local copies, waits for them, and re-layouts: 0.05 us -> 3.67 us
    max x30 -> x1, other arithmetic: 1.54 us -> 0.01 us  [on_device(): joint_top = jnp.maximum(jnp.max(part_top, axis=0), tree_top)]
  transfers between devices with their start and end apart: 11 -> 3, of which waited for: 4 -> 3; matrix products, arithmetic and copies ran while one was open for 29% -> 7% of each run, Pallas kernels for 0% -> 0%
where the time goes in v1:
time: 54.7 us; the launch traced here: 54.1 us
  starting transfers between devices  19.2 us (35%)
  waiting for transfers between devices  13.4 us (24%)
  local copies, waits for them, and re-layouts  9.28 us (17%)
  other arithmetic  6.27 us (11%)
  matrix products  4.95 us (9%)
  between operations  0.98 us (2%)
    all_to_all x1, starting transfers between devices, on_device(): pieces = lax.all_to_all(pieces, 'tp', 0, 0, tiled=True)  10.8 us
    all_to_all x1, waiting for transfers between devices, on_device(): partials = lax.all_to_all(partial, 'mem', 0, 0, tiled=True)  5.77 us
    all_to_all x1, starting transfers between devices, on_device(): got = lax.all_to_all(sent, 'mem', 0, 0, tiled=True)  5 us
    all_to_all x1, waiting for transfers between devices, on_device(): pieces = lax.all_to_all(pieces, 'tp', 0, 0, tiled=True)  4.64 us
    unnamed x25, local copies, waits for them, and re-layouts  3.67 us
    all_to_all x1, starting transfers between devices, on_device(): partials = lax.all_to_all(partial, 'mem', 0, 0, tiled=True)  3.45 us
    all_to_all x1, waiting for transfers between devices, on_device(): got = lax.all_to_all(sent, 'mem', 0, 0, tiled=True)  3.03 us
    dot_general x1, matrix products, on_device(): jnp.dot(attention, out_weight, preferred_element_type=jnp.float32)  3 us
  transfers between devices with their start and end apart: 3, of which 3 were waited for; matrix products, arithmetic and copies ran while one was open for 7% of the time, Pallas kernels for 0%

profile of v1, /device:TPU:1, one launch (start us, length us, event | category | flops | bytes accessed | tf_op | source)
XLA Modules:
  0.0 54.1 jit_solution(10262613137390350856)
XLA Ops:
  0.7 0.9 %copy.112 = bf16[576,128]{1,0:T(8,128)(2,1)S(1)} copy(bf16[576,128]{1,0:T(8,128)(2,1)} %param.14) | data formatting | bytes 294912
  1.6 0.9 %copy.113 = bf16[576,128]{1,0:T(8,128)(2,1)S(1)} copy(bf16[576,128]{1,0:T(8,128)(2,1)} %param.15) | data formatting | bytes 294912
  2.5 0.7 %fusion.42 = s32[8]{0:T(128)S(1)} fusion(s32[1,8]{1,0:T(1,128)} %param.20), kind=kLoop, calls=%fused_computation.84 | loop fusion | flops 24 | bytes 64 | tf_op jit(solution)/shard_map/jit(_take)/jit(_where)/select_n | solution.py:67
  3.2 0.7 %compare_and_fusion.1 = pred[8]{0:T(512)(128)(4,1)S(1)} fusion(s32[1,8]{1,0:T(1,128)} %param.20), kind=kLoop, calls=%fused_computation.83 | loop fusion | flops 48 | bytes 40 | tf_op jit(solution)/shard_map/jit(_take)/and | solution.py:67
  3.9 0.7 %pad_maximum_fusion.2 = bf16[32,256]{1,0:T(8,128)(2,1)S(1)} fusion(bf16[32,128]{1,0:T(8,128)(2,1)} %bitcast.152, bf16[32,128]{1,0:T(8,128)(2,1)} %bitcast.151), kind=kLoop, calls=%fused_computation.54 | loop fusion | flops 32768 | bytes 32768 | tf_op jit(solution)/shard_map/concatenate | solution.py:66
  4.6 0.6 %gather_fusion = bf16[8,256]{1,0:T(8,128)(2,1)S(1)} fusion(bf16[32,256]{1,0:T(8,128)(2,1)S(1)} %pad_maximum_fusion.2, s32[1024]{0:T(1024)S(1)} %pad_clamp_fusion), kind=kCustom, calls=%fused_computation | custom fusion | bytes 8224 | tf_op jit(solution)/shard_map/jit(_take)/gather | solution.py:67
  5.3 0.8 %copy.79 = bf16[4,4,8,128]{3,1,2,0:T(4,128)(2,1)S(1)} copy(bf16[4,4,8,128]{3,2,1,0:T(8,128)(2,1)} %bitcast.147) | data formatting | bytes 65536
  6.0 0.2 broadcast_in_dim.73
  6.2 0.5 broadcast.171
  6.7 1.5 %reduce.5 = bf16[4,18432]{1,0:T(4,128)(2,1)S(1)} reduce(bf16[4,1,18432]{2,1,0:T(2,128)(2,1)S(1)} %broadcast_in_dim.73, bf16[]{:T(256)} %broadcast.171), dimensions={1}, to_apply=%broadcast_in_dim.73.reduce_sub_computation | reduce | bytes 294914 | tf_op jit(solution)/shard_map/broadcast_in_dim | solution.py:70
  8.3 0.8 %reshape.361 = bf16[4,2,9216]{2,1,0:T(2,128)(2,1)} reshape(bf16[4,18432]{1,0:T(4,128)(2,1)S(1)} %reduce.5) | data formatting | bytes 294912
  9.0 5.0 %all-to-all-start = ((bf16[4,2,9216]{2,1,0:T(2,128)(2,1)}), bf16[4,2,9216]{2,1,0:T(2,128)(2,1)S(1)}, u32[]{:S(2)}, u32[]{:S(2)}) async-start(bf16[4,2,9216]{2,1,0:T(2,128)(2,1)} %reshape.361), calls=%async_computation | async-start | bytes 294912 | tf_op jit(solution)/shard_map/all_to_all | solution.py:71
  14.1 0.2 convolution_compare_fusion.4
  14.3 0.2 convolution_compare_fusion.2
  14.5 0.2 fusion.3
  14.8 0.1 copy.64
  14.9 0.1 copy.59
  15.0 0.1 reduce-window.9
  15.1 0.1 reduce.4
  15.4 0.2 select_reduce_fusion.1
  15.6 0.2 convolution_bitcast_fusion.1
  15.9 3.0 %all-to-all-done = bf16[4,2,9216]{2,1,0:T(2,128)(2,1)S(1)} async-done(((bf16[4,2,9216]{2,1,0:T(2,128)(2,1)}), bf16[4,2,9216]{2,1,0:T(2,128)(2,1)S(1)}, u32[]{:S(2)}, u32[]{:S(2)}) %all-to-all-start) | async-done | bytes 147488 | tf_op jit(solution)/shard_map/all_to_all | solution.py:71
  18.9 0.1 reshape.362
  19.1 0.1 copy.101
  19.2 0.2 reshape.318
  19.4 0.4 select_reduce_fusion
  19.8 0.4 fusion.4
  20.3 0.4 convolution_bitcast_fusion
  20.7 0.2 copy.61
  20.9 0.1 reshape.320
  21.0 0.1 copy.63
  21.1 0.1 copy.62
  21.2 0.8 %pad_maximum_fusion = f32[4,32,520]{2,1,0:T(8,128)} fusion(f32[4,32,4]{2,1,0:T(8,128)S(1)} %copy.63, f32[4,32,4]{2,1,0:T(8,128)S(1)} %copy.62, f32[4,32,512]{2,1,0:T(8,128)S(1)} %reshape.320), kind=kLoop, calls=%fused_computation.26 | loop fusion | flops 133120 | bytes 532480 | tf_op jit(solution)/shard_map/concatenate | solution.py:96
  22.0 3.5 %all-to-all-start.1 = ((f32[4,32,520]{2,1,0:T(8,128)}), f32[4,32,520]{2,1,0:T(8,128)S(1)}, u32[]{:S(2)}, u32[]{:S(2)}) async-start(f32[4,32,520]{2,1,0:T(8,128)} %pad_maximum_fusion), calls=%async_computation.1 | async-start | bytes 655360 | tf_op jit(solution)/shard_map/all_to_all | solution.py:99
  25.6 5.8 %all-to-all-done.1 = f32[4,32,520]{2,1,0:T(8,128)S(1)} async-done(((f32[4,32,520]{2,1,0:T(8,128)}), f32[4,32,520]{2,1,0:T(8,128)S(1)}, u32[]{:S(2)}, u32[]{:S(2)}) %all-to-all-start.1) | async-done | bytes 266272 | tf_op jit(solution)/shard_map/all_to_all | solution.py:99
  31.4 0.1 copy.67
  31.5 0.1 fusion.17
  31.7 0.1 copy.72
  31.9 0.2 mul.89
  32.1 0.1 mul.90
  32.4 0.1 mul.97
  32.5 3.0 %convolution_convert_fusion = bf16[32,4096]{1,0:T(8,128)(2,1)S(1)} fusion(bf16[512,4096]{1,0:T(8,128)(2,1)} %param.17, f32[4,8,4,128]{3,2,1,0:T(4,128)S(1)} %bitcast.145, f32[32,512]{1,0:T(8,128)S(1)} %fusion.11, f32[4,8,4,128]{3,2,1,0:T(4,128)S(1)} %bitcast.144, f32[4,8,4,128]{3,2,1,0:T(4,128)S(1)} %bitcast.146), kind=kOutput, calls=%fused_computation.3 | convolution fusion | flops 134414336 | bytes 4718592 | tf_op jit(solution)/shard_map/dot_general | solution.py:134
  35.5 0.7 %copy.100 = bf16[4,8,8,512]{3,2,0,1:T(8,128)(2,1)} copy(bf16[4,8,8,512]{3,2,1,0:T(8,128)(2,1)S(1)} %bitcast.141) | data formatting | bytes 524288 | tf_op jit(solution)/shard_map/reshape | solution.py:137
  36.2 10.8 %all-to-all-start.2 = ((bf16[8,32,512]{2,1,0:T(8,128)(2,1)}), bf16[8,32,512]{2,1,0:T(8,128)(2,1)S(1)}, u32[]{:S(2)}, u32[]{:S(2)}) async-start(bf16[8,32,512]{2,1,0:T(8,128)(2,1)} %bitcast.137), calls=%async_computation.2 | async-start | bytes 524288 | tf_op jit(solution)/shard_map/all_to_all | solution.py:138
  47.2 0.8 %scatter_custom_fusion = bf16[576,128]{1,0:T(8,128)(2,1)S(1)} fusion(bf16[576,128]{1,0:T(8,128)(2,1)S(1)} %copy.112, s32[32]{0:T(128)S(1)} %fusion.43, bf16[32,256]{1,0:T(8,128)(2,1)S(1)} %reshape_reshape.8), kind=kCustom, calls=%fused_computation.61 | custom fusion | bytes 155648 | tf_op jit(solution)/shard_map/scatter | solution.py:148
  48.0 0.8 %scatter_custom_fusion.1 = bf16[576,128]{1,0:T(8,128)(2,1)S(1)} fusion(bf16[576,128]{1,0:T(8,128)(2,1)S(1)} %copy.113, s32[32]{0:T(128)S(1)} %fusion.43, bf16[32,256]{1,0:T(8,128)(2,1)S(1)} %reshape_reshape.8), kind=kCustom, calls=%fused_computation.59 | custom fusion | bytes 155648 | tf_op jit(solution)/shard_map/scatter | solution.py:149
  48.8 4.6 %all-to-all-done.2 = bf16[8,32,512]{2,1,0:T(8,128)(2,1)S(1)} async-done(((bf16[8,32,512]{2,1,0:T(8,128)(2,1)}), bf16[8,32,512]{2,1,0:T(8,128)(2,1)S(1)}, u32[]{:S(2)}, u32[]{:S(2)}) %all-to-all-start.2) | async-done | bytes 262176 | tf_op jit(solution)/shard_map/all_to_all | solution.py:138
  53.5 0.6 %fusion.18 = bf16[1,32,512]{2,1,0:T(8,128)(2,1)} fusion(f32[32,512]{1,0:T(8,128)S(1)} %convert_reduce_fusion, bf16[1,32,512]{2,1,0:T(8,128)(2,1)S(1)} %copy-done.5), kind=kLoop, calls=%fused_computation.41 | loop fusion | flops 49152 | bytes 131072 | tf_op jit(solution)/shard_map/convert_element_type | solution.py:140
  (48 shorter events, 1.3 us)
Async XLA Ops:
  0.6 13.4 %copy-start.2 = (bf16[1,32,512]{2,1,0:T(8,128)(2,1)S(1)}, bf16[1,32,512]{2,1,0:T(8,128)(2,1)}, u32[]{:S(2)}) copy-start(bf16[1,32,512]{2,1,0:T(8,128)(2,1)} %param.11) | copy-start | bytes 98308
  0.6 14.7 %copy-start.3 = (bf16[1,32,128]{2,1,0:T(8,128)(2,1)S(1)}, bf16[1,32,128]{2,1,0:T(8,128)(2,1)}, u32[]{:S(2)}) copy-start(bf16[1,32,128]{2,1,0:T(8,128)(2,1)} %param.12) | copy-start | bytes 24580
  0.7 14.9 %copy-start.4 = (bf16[1,32,128]{2,1,0:T(8,128)(2,1)S(1)}, bf16[1,32,128]{2,1,0:T(8,128)(2,1)}, u32[]{:S(2)}) copy-start(bf16[1,32,128]{2,1,0:T(8,128)(2,1)} %param.13) | copy-start | bytes 24580
  0.7 13.4 %copy-start.6 = (s32[64]{0:T(128)S(1)}, s32[64]{0:T(128)}, u32[]{:S(2)}) copy-start(s32[64]{0:T(128)} %param.18) | copy-start | bytes 772
  0.7 13.4 %copy-start.7 = (s32[1,32]{1,0:T(1,128)S(1)}, s32[1,32]{1,0:T(1,128)}, u32[]{:S(2)}) copy-start(s32[1,32]{1,0:T(1,128)} %param.19) | copy-start | bytes 388
  0.7 14.5 %copy-start.8 = (s32[64]{0:T(128)S(1)}, s32[64]{0:T(128)}, u32[]{:S(2)}) copy-start(s32[64]{0:T(128)} %param.21) | copy-start | bytes 772
  9.0 9.9 %all-to-all-start = ((bf16[4,2,9216]{2,1,0:T(2,128)(2,1)}), bf16[4,2,9216]{2,1,0:T(2,128)(2,1)S(1)}, u32[]{:S(2)}, u32[]{:S(2)}) async-start(bf16[4,2,9216]{2,1,0:T(2,128)(2,1)} %reshape.361), calls=%async_computation | async-start | bytes 294912 | tf_op jit(solution)/shard_map/all_to_all | solution.py:71
  22.0 9.3 %all-to-all-start.1 = ((f32[4,32,520]{2,1,0:T(8,128)}), f32[4,32,520]{2,1,0:T(8,128)S(1)}, u32[]{:S(2)}, u32[]{:S(2)}) async-start(f32[4,32,520]{2,1,0:T(8,128)} %pad_maximum_fusion), calls=%async_computation.1 | async-start | bytes 655360 | tf_op jit(solution)/shard_map/all_to_all | solution.py:99
  35.5 18.0 %copy-start.5 = (bf16[1,32,512]{2,1,0:T(8,128)(2,1)S(1)}, bf16[1,32,512]{2,1,0:T(8,128)(2,1)}, u32[]{:S(2)}) copy-start(bf16[1,32,512]{2,1,0:T(8,128)(2,1)} %param.16) | copy-start | bytes 98308
  36.2 17.2 %all-to-all-start.2 = ((bf16[8,32,512]{2,1,0:T(8,128)(2,1)}), bf16[8,32,512]{2,1,0:T(8,128)(2,1)S(1)}, u32[]{:S(2)}, u32[]{:S(2)}) async-start(bf16[8,32,512]{2,1,0:T(8,128)(2,1)} %bitcast.137), calls=%async_computation.2 | async-start | bytes 524288 | tf_op jit(solution)/shard_map/all_to_all | solution.py:138
  48.0 6.1 %copy-start = (bf16[576,128]{1,0:T(8,128)(2,1)}, bf16[576,128]{1,0:T(8,128)(2,1)S(1)}, u32[]{:S(2)}) copy-start(bf16[576,128]{1,0:T(8,128)(2,1)S(1)} %scatter_custom_fusion) | copy-start | bytes 442372
  48.8 5.3 %copy-start.1 = (bf16[576,128]{1,0:T(8,128)(2,1)}, bf16[576,128]{1,0:T(8,128)(2,1)S(1)}, u32[]{:S(2)}) copy-start(bf16[576,128]{1,0:T(8,128)(2,1)S(1)} %scatter_custom_fusion.1) | copy-start | bytes 442372

commit v2 on v1

--- a/solution.py
+++ b/solution.py
@@ -63,14 +63,8 @@
     keys_local = cache_keys.reshape(positions, kv_local, HD)
     values_local = cache_values.reshape(positions, kv_local, HD)
 
-    tree_pair = jnp.concatenate([tree_keys[0], tree_values[0]], axis=-1)
-    mine_rows = jnp.take(tree_pair, accept_rows[0], axis=0)
-    q_size = TREE * q_width
-    packed = jnp.concatenate([queries[0].reshape(-1), mine_rows.reshape(-1)])
-    sent = jnp.broadcast_to(packed[None], (GROUP, packed.shape[0]))
-    got = lax.all_to_all(sent, "mem", 0, 0, tiled=True)
-    gathered_q = got[:, :q_size].reshape(GROUP, TREE, q_width)
-    row_block = got[:, q_size:].reshape(GROUP, A_MAX, 2 * channels)
+    sent = jnp.broadcast_to(queries, (GROUP,) + queries.shape[1:])
+    gathered_q = lax.all_to_all(sent, "mem", 0, 0, tiled=True)
 
     group_base = seq_rank - member
     begin = lax.dynamic_slice_in_dim(starts, group_base, GROUP)
@@ -96,7 +90,17 @@
     partial = jnp.concatenate(
         [summed.reshape(GROUP, TREE, q_width), top_rows, total_rows], axis=-1
     )
-    partials = lax.all_to_all(partial, "mem", 0, 0, tiled=True)
+    tree_pair = jnp.concatenate([tree_keys[0], tree_values[0]], axis=-1)
+    mine_rows = jnp.take(tree_pair, accept_rows[0], axis=0).astype(jnp.float32)
+    width = partial.shape[-1]
+    row_lines = mine_rows.reshape(-1, q_width)
+    row_lines = jnp.pad(row_lines, ((0, 0), (0, width - q_width)))
+    row_lines = jnp.broadcast_to(row_lines[None], (GROUP,) + row_lines.shape)
+    message = jnp.concatenate([partial, row_lines], axis=1)
+    partials = lax.all_to_all(message, "mem", 0, 0, tiled=True)
+    row_block = partials[:, TREE:, :q_width].reshape(GROUP, A_MAX, 2 * channels)
+    row_block = row_block.astype(jnp.bfloat16)
+    partials = partials[:, :TREE]
     part_out = partials[:, :, :q_width]
     part_top = partials[:, :, q_width : q_width + heads_local]
     part_total = partials[:, :, q_width + heads_local :]
@@ -131,13 +135,13 @@
     attention = scale_heads(joint_out, 1.0 / joint_total).astype(jnp.bfloat16)
 
     tp_size = lax.axis_size("tp")
-    projected = jnp.dot(attention, out_weight, preferred_element_type=jnp.float32).astype(
-        jnp.bfloat16
-    )
-    pieces = jnp.transpose(projected.reshape(TREE, tp_size, -1), (1, 0, 2))
+    projected = lax.dot_general(
+        out_weight, attention, (((0,), (1,)), ((), ())), preferred_element_type=jnp.float32
+    ).astype(jnp.bfloat16)
+    pieces = projected.reshape(tp_size, -1, TREE)
     pieces = lax.all_to_all(pieces, "tp", 0, 0, tiled=True)
     summed_heads = jnp.sum(pieces.astype(jnp.float32), axis=0)
-    mixed = (residual[0].astype(jnp.float32) + summed_heads).astype(jnp.bfloat16)[None]
+    mixed = (residual[0].astype(jnp.float32) + summed_heads.T).astype(jnp.bfloat16)[None]
 
     row_accepted = lax.dynamic_slice_in_dim(accept_len, group_base, GROUP)
     column = jnp.arange(A_MAX, dtype=jnp.int32)

time: 54.7 us -> 53 us (0.969)
  waiting for transfers between devices: 13.4 us -> 10.7 us
  matrix products: 4.95 us -> 5.68 us
    all_to_all x2, waiting for transfers between devices: 8.8 us -> 6.08 us  [the longest x1 6.08 us: on_device(): partials = lax.all_to_all(message, 'mem', 0, 0, tiled=True)]
    unnamed x25 -> x17, local copies, waits for them, and re-layouts: 3.67 us -> 2.39 us
    unnamed x1, other arithmetic: 0.07 us -> 1.32 us
    broadcast_in_dim x1, other arithmetic: 1.55 us -> 0.62 us  [on_device(): (residual[0].astype(jnp.float32) + summed_heads.T).astype(jnp.bfloat16)]
    broadcast_in_dim x2 -> x3, local copies, waits for them, and re-layouts: 0.67 us -> 1.5 us  [the longest x1 1.42 us: on_device(): sent = jnp.broadcast_to(queries, (GROUP,) + queries.shape[1:])]
    all_to_all x2, starting transfers between devices: 8.45 us -> 9.24 us  [the longest x1 5 us: on_device(): gathered_q = lax.all_to_all(sent, 'mem', 0, 0, tiled=True)]
    dot_general x3, matrix products: 0.69 us -> 1.42 us  [ancestry(): jnp.dot(reach, reach, preferred_element_type=jnp.float32) > 0]
    another operation x3, other arithmetic: 0.21 us -> 0.86 us
  transfers between devices with their start and end apart: 3 -> 3, of which waited for: 3 -> 2; matrix products, arithmetic and copies ran while one was open for 7% -> 19% of each run, Pallas kernels for 0% -> 0%
where the time goes in v2:
time: 53 us; the launch traced here: 52.3 us
  starting transfers between devices  19.4 us (37%)
  waiting for transfers between devices  10.7 us (20%)
  local copies, waits for them, and re-layouts  9.58 us (18%)
  other arithmetic  6.01 us (11%)
  matrix products  5.68 us (11%)
  between operations  0.89 us (2%)
    all_to_all x1, starting transfers between devices, on_device(): pieces = lax.all_to_all(pieces, 'tp', 0, 0, tiled=True)  10.2 us
    all_to_all x1, waiting for transfers between devices, on_device(): partials = lax.all_to_all(message, 'mem', 0, 0, tiled=True)  6.08 us
    all_to_all x1, starting transfers between devices, on_device(): gathered_q = lax.all_to_all(sent, 'mem', 0, 0, tiled=True)  5 us
    all_to_all x1, waiting for transfers between devices, on_device(): pieces = lax.all_to_all(pieces, 'tp', 0, 0, tiled=True)  4.65 us
    all_to_all x1, starting transfers between devices, on_device(): partials = lax.all_to_all(message, 'mem', 0, 0, tiled=True)  4.24 us
    dot_general x1, matrix products, on_device(): lax.dot_general(out_weight, attention, (((0,), (1,)), ((), ())), preferre...  3 us
    unnamed x17, local copies, waits for them, and re-layouts  2.39 us
    broadcast_in_dim x1, local copies, waits for them, and re-layouts, on_device(): sent = jnp.broadcast_to(queries, (GROUP,) + queries.shape[1:])  1.42 us
  transfers between devices with their start and end apart: 3, of which 2 were waited for; matrix products, arithmetic and copies ran while one was open for 19% of the time, Pallas kernels for 0%

profile of v2, /device:TPU:1, one launch (start us, length us, event | category | flops | bytes accessed | tf_op | source)
XLA Modules:
  0.0 52.3 jit_solution(15799228451935410677)
XLA Ops:
  0.7 0.9 %copy.100 = bf16[576,128]{1,0:T(8,128)(2,1)S(1)} copy(bf16[576,128]{1,0:T(8,128)(2,1)} %param.14) | data formatting | bytes 294912
  1.6 0.9 %copy.101 = bf16[576,128]{1,0:T(8,128)(2,1)S(1)} copy(bf16[576,128]{1,0:T(8,128)(2,1)} %param.15) | data formatting | bytes 294912
  2.5 1.4 %broadcast_in_dim.83 = bf16[4,32,512]{2,1,0:T(8,128)(2,1)} broadcast(bf16[32,512]{1,0:T(8,128)(2,1)} %bitcast.147), dimensions={1,2} | broadcast | bytes 163840 | tf_op jit(solution)/shard_map/broadcast_in_dim | solution.py:66
  3.9 5.0 %all-to-all-start = ((bf16[4,32,512]{2,1,0:T(8,128)(2,1)}), bf16[4,32,512]{2,1,0:T(8,128)(2,1)S(1)}, u32[]{:S(2)}, u32[]{:S(2)}) async-start(bf16[4,32,512]{2,1,0:T(8,128)(2,1)} %broadcast_in_dim.83), calls=%async_computation | async-start | bytes 262144 | tf_op jit(solution)/shard_map/all_to_all | solution.py:67
  8.9 0.8 %reshape.324 = bf16[32,4,128]{2,1,0:T(4,128)(2,1)S(1)} reshape(bf16[1,32,512]{2,1,0:T(8,128)(2,1)} %param.11) | data formatting | bytes 65536 | tf_op jit(solution)/shard_map/reshape.13
  9.7 0.7 %fusion.44 = s32[8]{0:T(128)S(1)} fusion(s32[1,8]{1,0:T(1,128)} %param.20), kind=kLoop, calls=%fused_computation.86 | loop fusion | flops 24 | bytes 64 | tf_op jit(solution)/shard_map/jit(_take)/jit(_where)/select_n | solution.py:94
  10.4 0.5 broadcast.174
  10.9 1.3 %reduce.8 = s32[8]{0:T(128)S(1)} reduce(s32[1,8]{1,0:T(1,128)} %param.20, s32[]{:T(128)} %broadcast.174), dimensions={0}, to_apply=%param.20.reduce_sub_computation.3 | reduce | bytes 68 | tf_op args[9]
  12.2 0.7 %add_bitcast_fusion = s32[64,1]{0,1:T(1,128)S(1)} fusion(s32[64]{0:T(128)} %param.18), kind=kLoop, calls=%fused_computation.90 | loop fusion | flops 64 | bytes 512 | tf_op jit(solution)/shard_map/reshape.275
  12.9 0.1 copy.53
  13.1 0.9 %convolution_compare_fusion.4 = pred[32,32]{1,0:T(32,128)(4,1)S(1)} fusion(s32[32]{0:T(128)} %bitcast.153), kind=kOutput, calls=%fused_computation.16 | convolution fusion | flops 69632 | bytes 1152 | tf_op jit(solution)/shard_map/dot_general | solution.py:27
  14.0 0.2 convolution_compare_fusion.2
  14.2 0.2 fusion.3
  14.5 0.1 copy.54
  14.6 0.7 %pad_maximum_fusion.1 = bf16[32,256]{1,0:T(8,128)(2,1)S(1)} fusion(bf16[32,128]{1,0:T(8,128)(2,1)} %bitcast.151, bf16[32,128]{1,0:T(8,128)(2,1)} %bitcast.150), kind=kLoop, calls=%fused_computation.55 | loop fusion | flops 32768 | bytes 32768 | tf_op jit(solution)/shard_map/concatenate | solution.py:93
  15.3 0.6 %gather_fusion = bf16[8,256]{1,0:T(8,128)(2,1)S(1)} fusion(bf16[32,256]{1,0:T(8,128)(2,1)S(1)} %pad_maximum_fusion.1, s32[1024]{0:T(1024)S(1)} %pad_clamp_fusion), kind=kCustom, calls=%fused_computation | custom fusion | bytes 8224 | tf_op jit(solution)/shard_map/jit(_take)/gather | solution.py:94
  15.9 0.1 copy.48
  16.0 0.1 reduce-window.9
  16.1 0.1 reduce.4
  16.4 0.2 select_reduce_fusion.1
  16.6 0.2 convolution_bitcast_fusion.1
  16.9 0.4 select_reduce_fusion
  17.3 0.4 fusion.4
  17.7 0.4 convolution_bitcast_fusion
  18.2 0.2 copy.50
  18.4 0.1 reshape.321
  18.5 0.1 copy.52
  18.6 0.1 copy.51
  18.7 0.8 %pad_maximum_fusion = f32[4,36,520]{2,1,0:T(8,128)} fusion(f32[4,4,520]{2,1,0:T(4,128)S(1)} %broadcast_in_dim.89, f32[4,32,4]{2,1,0:T(8,128)S(1)} %copy.52, f32[4,32,4]{2,1,0:T(8,128)S(1)} %copy.51, f32[4,32,512]{2,1,0:T(8,128)S(1)} %reshape.321), kind=kLoop, calls=%fused_computation.26 | loop fusion | flops 224640 | bytes 599040 | tf_op jit(solution)/shard_map/concatenate | solution.py:99
  19.5 4.2 %all-to-all-start.1 = ((f32[4,36,520]{2,1,0:T(8,128)}), f32[4,36,520]{2,1,0:T(8,128)S(1)}, u32[]{:S(2)}, u32[]{:S(2)}) async-start(f32[4,36,520]{2,1,0:T(8,128)} %pad_maximum_fusion), calls=%async_computation.1 | async-start | bytes 819200 | tf_op jit(solution)/shard_map/all_to_all | solution.py:100
  24.0 6.1 %all-to-all-done.1 = f32[4,36,520]{2,1,0:T(8,128)S(1)} async-done(((f32[4,36,520]{2,1,0:T(8,128)}), f32[4,36,520]{2,1,0:T(8,128)S(1)}, u32[]{:S(2)}, u32[]{:S(2)}) %all-to-all-start.1) | async-done | bytes 299552 | tf_op jit(solution)/shard_map/all_to_all | solution.py:100
  30.2 0.1 copy.57
  30.3 0.1 fusion.18
  30.5 0.1 copy.62
  30.6 0.1 copy.60
  30.6 0.2 mul.85
  30.9 0.1 mul.86
  31.0 0.1 mul.88
  31.1 0.1 mul.93
  31.2 3.0 %convolution_convert_fusion = bf16[32,4096]{1,0:T(8,128)(2,1)S(1)} fusion(bf16[512,4096]{1,0:T(8,128)(2,1)} %param.17, f32[4,8,4,128]{3,2,1,0:T(4,128)S(1)} %bitcast.145, f32[32,512]{1,0:T(8,128)S(1)} %fusion.11, f32[4,8,4,128]{3,2,1,0:T(4,128)S(1)} %bitcast.144, f32[4,8,4,128]{3,2,1,0:T(4,128)S(1)} %bitcast.146), kind=kOutput, calls=%fused_computation.3 | convolution fusion | flops 134414336 | bytes 4718592 | tf_op jit(solution)/shard_map/dot_general | solution.py:138
  34.2 0.7 %copy.89 = bf16[4,8,8,512]{3,2,0,1:T(8,128)(2,1)} copy(bf16[4,8,8,512]{3,2,1,0:T(8,128)(2,1)S(1)} %bitcast.143) | data formatting | bytes 524288 | tf_op jit(solution)/shard_map/reshape | solution.py:141
  35.0 10.2 %all-to-all-start.2 = ((bf16[8,512,32]{1,2,0:T(8,128)(2,1)}), bf16[8,512,32]{1,2,0:T(8,128)(2,1)S(1)}, u32[]{:S(2)}, u32[]{:S(2)}) async-start(bf16[8,512,32]{1,2,0:T(8,128)(2,1)} %bitcast.140), calls=%async_computation.2 | async-start | bytes 524288 | tf_op jit(solution)/shard_map/all_to_all | solution.py:142
  45.2 0.1 lt.95
  45.3 0.1 sub.65
  45.4 0.8 %scatter_custom_fusion.1 = bf16[576,128]{1,0:T(8,128)(2,1)S(1)} fusion(bf16[576,128]{1,0:T(8,128)(2,1)S(1)} %copy.101, s32[32]{0:T(128)S(1)} %fusion.45, bf16[32,256]{1,0:T(8,128)(2,1)S(1)} %convert_element_type.54), kind=kCustom, calls=%fused_computation.60 | custom fusion | bytes 155648 | tf_op jit(solution)/shard_map/scatter | solution.py:153
  46.2 0.8 %scatter_custom_fusion = bf16[576,128]{1,0:T(8,128)(2,1)S(1)} fusion(bf16[576,128]{1,0:T(8,128)(2,1)S(1)} %copy.100, s32[32]{0:T(128)S(1)} %fusion.45, bf16[32,256]{1,0:T(8,128)(2,1)S(1)} %convert_element_type.54), kind=kCustom, calls=%fused_computation.62 | custom fusion | bytes 155648 | tf_op jit(solution)/shard_map/scatter | solution.py:152
  47.0 4.6 %all-to-all-done.2 = bf16[8,512,32]{1,2,0:T(8,128)(2,1)S(1)} async-done(((bf16[8,512,32]{1,2,0:T(8,128)(2,1)}), bf16[8,512,32]{1,2,0:T(8,128)(2,1)S(1)}, u32[]{:S(2)}, u32[]{:S(2)}) %all-to-all-start.2) | async-done | bytes 262176 | tf_op jit(solution)/shard_map/all_to_all | solution.py:142
  51.7 0.6 %fusion.24 = bf16[1,32,512]{2,1,0:T(8,128)(2,1)} fusion(f32[512,32]{0,1:T(8,128)S(1)} %convert_reduce_fusion, bf16[1,32,512]{2,1,0:T(8,128)(2,1)S(1)} %copy-done.4), kind=kLoop, calls=%fused_computation.49 | loop fusion | flops 49152 | bytes 131072 | tf_op jit(solution)/shard_map/broadcast_in_dim | solution.py:144
  (42 shorter events, 1.0 us)
Async XLA Ops:
  0.6 15.8 %copy-start.2 = (bf16[1,32,128]{2,1,0:T(8,128)(2,1)S(1)}, bf16[1,32,128]{2,1,0:T(8,128)(2,1)}, u32[]{:S(2)}) copy-start(bf16[1,32,128]{2,1,0:T(8,128)(2,1)} %param.12) | copy-start | bytes 24580
  0.6 15.9 %copy-start.3 = (bf16[1,32,128]{2,1,0:T(8,128)(2,1)S(1)}, bf16[1,32,128]{2,1,0:T(8,128)(2,1)}, u32[]{:S(2)}) copy-start(bf16[1,32,128]{2,1,0:T(8,128)(2,1)} %param.13) | copy-start | bytes 24580
  0.7 15.5 %copy-start.5 = (s32[64]{0:T(128)S(1)}, s32[64]{0:T(128)}, u32[]{:S(2)}) copy-start(s32[64]{0:T(128)} %param.18) | copy-start | bytes 772
  3.9 12.9 %all-to-all-start = ((bf16[4,32,512]{2,1,0:T(8,128)(2,1)}), bf16[4,32,512]{2,1,0:T(8,128)(2,1)S(1)}, u32[]{:S(2)}, u32[]{:S(2)}) async-start(bf16[4,32,512]{2,1,0:T(8,128)(2,1)} %broadcast_in_dim.83), calls=%async_computation | async-start | bytes 262144 | tf_op jit(solution)/shard_map/all_to_all | solution.py:67
  18.4 5.5 %copy-start.6 = (s32[64]{0:T(128)S(1)}, s32[64]{0:T(128)}, u32[]{:S(2)}) copy-start(s32[64]{0:T(128)} %param.21) | copy-start | bytes 772
  19.5 10.6 %all-to-all-start.1 = ((f32[4,36,520]{2,1,0:T(8,128)}), f32[4,36,520]{2,1,0:T(8,128)S(1)}, u32[]{:S(2)}, u32[]{:S(2)}) async-start(f32[4,36,520]{2,1,0:T(8,128)} %pad_maximum_fusion), calls=%async_computation.1 | async-start | bytes 819200 | tf_op jit(solution)/shard_map/all_to_all | solution.py:100
  34.2 17.4 %copy-start.4 = (bf16[1,32,512]{2,1,0:T(8,128)(2,1)S(1)}, bf16[1,32,512]{2,1,0:T(8,128)(2,1)}, u32[]{:S(2)}) copy-start(bf16[1,32,512]{2,1,0:T(8,128)(2,1)} %param.16) | copy-start | bytes 98308
  35.0 16.7 %all-to-all-start.2 = ((bf16[8,512,32]{1,2,0:T(8,128)(2,1)}), bf16[8,512,32]{1,2,0:T(8,128)(2,1)S(1)}, u32[]{:S(2)}, u32[]{:S(2)}) async-start(bf16[8,512,32]{1,2,0:T(8,128)(2,1)} %bitcast.140), calls=%async_computation.2 | async-start | bytes 524288 | tf_op jit(solution)/shard_map/all_to_all | solution.py:142
  46.2 6.1 %copy-start.1 = (bf16[576,128]{1,0:T(8,128)(2,1)}, bf16[576,128]{1,0:T(8,128)(2,1)S(1)}, u32[]{:S(2)}) copy-start(bf16[576,128]{1,0:T(8,128)(2,1)S(1)} %scatter_custom_fusion.1) | copy-start | bytes 442372
  46.9 5.3 %copy-start = (bf16[576,128]{1,0:T(8,128)(2,1)}, bf16[576,128]{1,0:T(8,128)(2,1)S(1)}, u32[]{:S(2)}) copy-start(bf16[576,128]{1,0:T(8,128)(2,1)S(1)} %scatter_custom_fusion) | copy-start | bytes 442372

commit v3 on v2

--- a/solution.py
+++ b/solution.py
@@ -4,6 +4,7 @@
 import jax.numpy as jnp
 import numpy as np
 from jax import lax
+from jax.experimental import pallas as pl
 from jax.sharding import Mesh
 from jax.sharding import PartitionSpec as P
 
@@ -28,6 +29,29 @@
         ).astype(jnp.bfloat16)
         covered *= 2
     return reach > 0
+
+
+def project_kernel(attention_ref, weight_ref, out_ref):
+    result = jnp.dot(attention_ref[...], weight_ref[...], preferred_element_type=jnp.float32)
+    width = out_ref.shape[2]
+    for piece in range(out_ref.shape[0]):
+        out_ref[piece] = result[:, piece * width : (piece + 1) * width].astype(out_ref.dtype)
+
+
+def project(attention, weight, pieces):
+    rows, cols = weight.shape
+    width = cols // pieces
+    per_step = 2 if pieces % 2 == 0 else 1
+    return pl.pallas_call(
+        project_kernel,
+        grid=(pieces // per_step,),
+        in_specs=[
+            pl.BlockSpec((attention.shape[0], rows), lambda j: (0, 0)),
+            pl.BlockSpec((rows, width * per_step), lambda j: (0, j)),
+        ],
+        out_specs=pl.BlockSpec((per_step, attention.shape[0], width), lambda j: (j, 0, 0)),
+        out_shape=jax.ShapeDtypeStruct((pieces, attention.shape[0], width), jnp.bfloat16),
+    )(attention, weight)
 
 
 def scale_heads(values, factors):
@@ -85,25 +109,28 @@
         values_local,
         preferred_element_type=jnp.float32,
     )
-    top_rows = jnp.transpose(top_score, (0, 3, 1, 2)).reshape(GROUP, TREE, heads_local)
-    total_rows = jnp.transpose(total, (0, 3, 1, 2)).reshape(GROUP, TREE, heads_local)
-    partial = jnp.concatenate(
-        [summed.reshape(GROUP, TREE, q_width), top_rows, total_rows], axis=-1
-    )
+    stats = jnp.concatenate(
+        [top_score.reshape(GROUP, 1, -1), total.reshape(GROUP, 1, -1)], axis=-1
+    )
+    stats = jnp.pad(stats, ((0, 0), (0, 0), (0, q_width - stats.shape[-1])))
     tree_pair = jnp.concatenate([tree_keys[0], tree_values[0]], axis=-1)
     mine_rows = jnp.take(tree_pair, accept_rows[0], axis=0).astype(jnp.float32)
-    width = partial.shape[-1]
-    row_lines = mine_rows.reshape(-1, q_width)
-    row_lines = jnp.pad(row_lines, ((0, 0), (0, width - q_width)))
-    row_lines = jnp.broadcast_to(row_lines[None], (GROUP,) + row_lines.shape)
-    message = jnp.concatenate([partial, row_lines], axis=1)
+    row_lines = mine_rows.reshape(1, -1, q_width)
+    row_count = row_lines.shape[1]
+    row_lines = jnp.broadcast_to(row_lines, (GROUP,) + row_lines.shape[1:])
+    used = TREE + 1 + row_count
+    filler = jnp.zeros((GROUP, -used % 8, q_width), jnp.float32)
+    message = jnp.concatenate(
+        [summed.reshape(GROUP, TREE, q_width), stats, row_lines, filler], axis=1
+    )
     partials = lax.all_to_all(message, "mem", 0, 0, tiled=True)
-    row_block = partials[:, TREE:, :q_width].reshape(GROUP, A_MAX, 2 * channels)
+    row_block = partials[:, TREE + 1 : used].reshape(GROUP, A_MAX, 2 * channels)
     row_block = row_block.astype(jnp.bfloat16)
-    partials = partials[:, :TREE]
-    part_out = partials[:, :, :q_width]
-    part_top = partials[:, :, q_width : q_width + heads_local]
-    part_total = partials[:, :, q_width + heads_local :]
+    part_out = partials[:, :TREE]
+    stat_count = kv_local * sharing * TREE
+    part_stats = partials[:, TREE, : 2 * stat_count].reshape(GROUP, 2, heads_local, TREE)
+    part_top = jnp.transpose(part_stats[:, 0], (0, 2, 1))
+    part_total = jnp.transpose(part_stats[:, 1], (0, 2, 1))
 
     linked = ancestry(parents[0])
     shaped_q = queries[0].reshape(TREE, kv_local, sharing, HD)
@@ -135,13 +162,10 @@
     attention = scale_heads(joint_out, 1.0 / joint_total).astype(jnp.bfloat16)
 
     tp_size = lax.axis_size("tp")
-    projected = lax.dot_general(
-        out_weight, attention, (((0,), (1,)), ((), ())), preferred_element_type=jnp.float32
-    ).astype(jnp.bfloat16)
-    pieces = projected.reshape(tp_size, -1, TREE)
+    pieces = project(attention, out_weight, tp_size)
     pieces = lax.all_to_all(pieces, "tp", 0, 0, tiled=True)
     summed_heads = jnp.sum(pieces.astype(jnp.float32), axis=0)
-    mixed = (residual[0].astype(jnp.float32) + summed_heads.T).astype(jnp.bfloat16)[None]
+    mixed = (residual[0].astype(jnp.float32) + summed_heads).astype(jnp.bfloat16)[None]
 
     row_accepted = lax.dynamic_slice_in_dim(accept_len, group_base, GROUP)
     column = jnp.arange(A_MAX, dtype=jnp.int32)

time: 53 us -> 53.1 us (level)
  Pallas kernels: 0 us -> 4.36 us
  matrix products: 5.68 us -> 1.94 us
  local copies, waits for them, and re-layouts: 9.58 us -> 8.89 us
  other arithmetic: 6.01 us -> 6.57 us
    pallas_call x0 -> x1, Pallas kernels: none -> 4.36 us  [project(): pl.pallas_call(project_kernel, grid=(pieces // per_step,), in_specs=[pl.B...]
    dot_general x1 -> x0, matrix products: 3 us -> none  [on_device(): lax.dot_general(out_weight, attention, (((0,), (1,)), ((), ())), preferre...]
    convert_element_type x0 -> x3, other arithmetic: none -> 1.28 us  [the longest x1 0.64 us: on_device(): attention = scale_heads(joint_out, 1.0 / joint_total).astype(jnp.bfloat16)]
    reshape x3 -> x2, local copies, waits for them, and re-layouts: 0.93 us -> 0.17 us  [the longest x1 0.09 us: on_device(): top_score.reshape(GROUP, 1, -1)]
    dot_general x3, matrix products: 1.42 us -> 0.69 us  [ancestry(): jnp.dot(reach, reach, preferred_element_type=jnp.float32) > 0]
    sub x1, other arithmetic: 0.01 us -> 0.67 us  [on_device(): starts = jnp.cumsum(regions) - regions]
    unnamed x1, other arithmetic: 1.32 us -> 0.66 us
    broadcast_in_dim x1 -> x0, other arithmetic: 0.62 us -> none  [on_device(): (residual[0].astype(jnp.float32) + summed_heads.T).astype(jnp.bfloat16)]
  transfers between devices with their start and end apart: 3 -> 3, of which waited for: 2 -> 2; matrix products, arithmetic and copies ran while one was open for 19% -> 18% of each run, Pallas kernels for 0% -> 0%
where the time goes in v3:
time: 53.1 us; the launch traced here: 52.3 us
  starting transfers between devices  19.4 us (37%)
  waiting for transfers between devices  10.3 us (19%)
  local copies, waits for them, and re-layouts  8.89 us (17%)
  other arithmetic  6.57 us (12%)
  Pallas kernels  4.36 us (8%)
  matrix products  1.94 us (4%)
  between operations  0.9 us (2%)
    all_to_all x1, starting transfers between devices, on_device(): pieces = lax.all_to_all(pieces, 'tp', 0, 0, tiled=True)  10.2 us
    all_to_all x1, waiting for transfers between devices, on_device(): partials = lax.all_to_all(message, 'mem', 0, 0, tiled=True)  5.63 us
    all_to_all x1, starting transfers between devices, on_device(): gathered_q = lax.all_to_all(sent, 'mem', 0, 0, tiled=True)  5 us
    all_to_all x1, waiting for transfers between devices, on_device(): pieces = lax.all_to_all(pieces, 'tp', 0, 0, tiled=True)  4.65 us
    pallas_call x1, Pallas kernels, project(): pl.pallas_call(project_kernel, grid=(pieces // per_step,), in_specs=[pl.B...  4.36 us
    all_to_all x1, starting transfers between devices, on_device(): partials = lax.all_to_all(message, 'mem', 0, 0, tiled=True)  4.24 us
    unnamed x21, local copies, waits for them, and re-layouts  2.41 us
    broadcast_in_dim x1, local copies, waits for them, and re-layouts, on_device(): sent = jnp.broadcast_to(queries, (GROUP,) + queries.shape[1:])  1.42 us
  transfers between devices with their start and end apart: 3, of which 2 were waited for; matrix products, arithmetic and copies ran while one was open for 18% of the time, Pallas kernels for 0%

profile of v3, /device:TPU:1, one launch (start us, length us, event | category | flops | bytes accessed | tf_op | source)
XLA Modules:
  0.0 52.3 jit_solution(15995068464805883103)
XLA Ops:
  0.7 0.9 %copy.67 = bf16[576,128]{1,0:T(8,128)(2,1)S(1)} copy(bf16[576,128]{1,0:T(8,128)(2,1)} %param.14) | data formatting | bytes 294912
  1.6 0.9 %copy.68 = bf16[576,128]{1,0:T(8,128)(2,1)S(1)} copy(bf16[576,128]{1,0:T(8,128)(2,1)} %param.15) | data formatting | bytes 294912
  2.5 1.4 %broadcast_in_dim.83 = bf16[4,32,512]{2,1,0:T(8,128)(2,1)} broadcast(bf16[32,512]{1,0:T(8,128)(2,1)} %bitcast.139), dimensions={1,2} | broadcast | bytes 163840 | tf_op jit(solution)/shard_map/broadcast_in_dim | solution.py:90
  4.0 5.0 %all-to-all-start = ((bf16[4,32,512]{2,1,0:T(8,128)(2,1)}), bf16[4,32,512]{2,1,0:T(8,128)(2,1)S(1)}, u32[]{:S(2)}, u32[]{:S(2)}) async-start(bf16[4,32,512]{2,1,0:T(8,128)(2,1)} %broadcast_in_dim.83), calls=%async_computation | async-start | bytes 262144 | tf_op jit(solution)/shard_map/all_to_all | solution.py:91
  9.0 0.8 %reshape.332 = bf16[32,4,128]{2,1,0:T(4,128)(2,1)S(1)} reshape(bf16[1,32,512]{2,1,0:T(8,128)(2,1)} %param.11) | data formatting | bytes 65536 | tf_op jit(solution)/shard_map/reshape.13
  9.7 0.7 %add_bitcast_fusion = s32[64,1]{0,1:T(1,128)S(1)} fusion(s32[64]{0:T(128)} %param.18), kind=kLoop, calls=%fused_computation.92 | loop fusion | flops 64 | bytes 512 | tf_op jit(solution)/shard_map/reshape.287
  10.4 0.1 copy.24
  10.5 0.1 reduce-window.9
  10.6 0.1 reduce.4
  10.7 0.7 %add_subtract_fusion.1 = s32[64]{0:T(128)S(1)} fusion(s32[64]{0:T(128)S(1)} %reduce.4, s32[64]{0:T(128)} %param.18), kind=kLoop, calls=%fused_computation.91 | loop fusion | flops 128 | bytes 768 | tf_op jit(solution)/shard_map/sub | solution.py:84
  11.4 0.7 %fusion.45 = s32[8]{0:T(128)S(1)} fusion(s32[1,8]{1,0:T(1,128)} %param.20), kind=kLoop, calls=%fused_computation.88 | loop fusion | flops 24 | bytes 64 | tf_op jit(solution)/shard_map/jit(_take)/jit(_where)/select_n | solution.py:117
  12.0 0.7 %pad_maximum_fusion = bf16[32,256]{1,0:T(8,128)(2,1)S(1)} fusion(bf16[32,128]{1,0:T(8,128)(2,1)} %bitcast.141, bf16[32,128]{1,0:T(8,128)(2,1)} %bitcast.140), kind=kLoop, calls=%fused_computation.50 | loop fusion | flops 32768 | bytes 32768 | tf_op jit(solution)/shard_map/concatenate | solution.py:116
  12.8 0.6 %gather_fusion = bf16[8,256]{1,0:T(8,128)(2,1)S(1)} fusion(bf16[32,256]{1,0:T(8,128)(2,1)S(1)} %pad_maximum_fusion, s32[1024]{0:T(1024)S(1)} %pad_clamp_fusion), kind=kCustom, calls=%fused_computation | custom fusion | bytes 8224 | tf_op jit(solution)/shard_map/jit(_take)/gather | solution.py:117
  13.3 0.5 broadcast.187
  13.9 0.7 %reduce.10 = s32[8]{0:T(128)S(1)} reduce(s32[1,8]{1,0:T(1,128)S(1)} %copy-done.6, s32[]{:T(128)} %broadcast.187), dimensions={0}, to_apply=%param.20.reduce_sub_computation.3 | reduce | bytes 68 | tf_op args[9]
  14.6 0.1 copy.27
  14.7 0.2 convolution_compare_fusion.4
  14.9 0.2 convolution_compare_fusion.2
  15.2 0.2 fusion.3
  15.4 0.1 copy.29
  15.8 0.2 select_reduce_fusion.1
  16.1 0.2 convolution_bitcast_fusion.1
  16.2 0.4 select_reduce_fusion
  16.7 0.1 reshape.330
  16.8 0.4 fusion.4
  17.2 0.1 reshape.331
  17.3 0.4 convolution_bitcast_fusion
  17.7 0.2 copy.26
  17.9 0.1 reshape.329
  18.1 0.8 %maximum_maximum_fusion = f32[4,40,512]{2,1,0:T(8,128)} fusion(f32[4,4,512]{2,1,0:T(4,128)S(1)} %broadcast_in_dim.89, f32[4,1,512]{2,1,0:T(1,128)S(1)} %fusion.29, f32[4,32,512]{2,1,0:T(8,128)S(1)} %reshape.329, f32[40]{0:T(128)S(1)} %pad.8.clone), kind=kLoop, calls=%fused_computation.25 | loop fusion | flops 245760 | bytes 630944 | tf_op jit(solution)/shard_map/concatenate | solution.py:123
  18.9 4.2 %all-to-all-start.1 = ((f32[4,40,512]{2,1,0:T(8,128)}), f32[4,40,512]{2,1,0:T(8,128)S(1)}, u32[]{:S(2)}, u32[]{:S(2)}) async-start(f32[4,40,512]{2,1,0:T(8,128)} %maximum_maximum_fusion), calls=%async_computation.1 | async-start | bytes 655360 | tf_op jit(solution)/shard_map/all_to_all | solution.py:126
  23.4 5.6 %all-to-all-done.1 = f32[4,40,512]{2,1,0:T(8,128)S(1)} async-done(((f32[4,40,512]{2,1,0:T(8,128)}), f32[4,40,512]{2,1,0:T(8,128)S(1)}, u32[]{:S(2)}, u32[]{:S(2)}) %all-to-all-start.1) | async-done | bytes 327712 | tf_op jit(solution)/shard_map/all_to_all | solution.py:126
  29.0 0.1 reshape_squeeze.2
  29.1 0.1 copy.31
  29.3 0.2 mul.85
  29.5 0.1 mul.86
  29.6 0.1 copy.34
  29.7 0.1 copy.35
  29.8 0.1 mul.88
  29.9 0.1 mul.93
  30.0 0.6 %fusion.16.attention_ref = bf16[32,512]{1,0:T(8,128)(2,1)} fusion(f32[4,8,4,128]{3,2,1,0:T(4,128)S(1)} %bitcast.137, f32[32,512]{1,0:T(8,128)S(1)} %fusion.11, f32[4,8,4,128]{3,2,1,0:T(4,128)S(1)} %bitcast.136, f32[4,8,4,128]{3,2,1,0:T(4,128)S(1)} %bitcast.138), kind=kLoop, calls=%fused_computation.33 | loop fusion | flops 65536 | bytes 294912 | tf_op jit(solution)/shard_map/convert_element_type | solution.py:162
  30.6 4.4 %shard_map.130 = bf16[8,32,512]{2,1,0:T(8,128)(2,1)} custom-call(bf16[32,512]{1,0:T(8,128)(2,1)} %fusion.16.attention_ref, bf16[512,4096]{1,0:T(8,128)(2,1)} %weight_ref.1), custom_call_target="tpu_custom_call" | custom-call | tf_op jit(solution)/shard_map/pallas_call | solution.py:45
  35.0 10.2 %all-to-all-start.2 = ((bf16[8,32,512]{2,1,0:T(8,128)(2,1)}), bf16[8,32,512]{2,1,0:T(8,128)(2,1)S(1)}, u32[]{:S(2)}, u32[]{:S(2)}) async-start(bf16[8,32,512]{2,1,0:T(8,128)(2,1)} %shard_map.130), calls=%async_computation.2 | async-start | bytes 524288 | tf_op jit(solution)/shard_map/all_to_all | solution.py:166
  45.3 0.1 lt.95
  45.4 0.8 %scatter_custom_fusion = bf16[576,128]{1,0:T(8,128)(2,1)S(1)} fusion(bf16[576,128]{1,0:T(8,128)(2,1)S(1)} %copy.67, s32[32]{0:T(128)S(1)} %fusion.46, bf16[32,256]{1,0:T(8,128)(2,1)S(1)} %convert_element_type.50), kind=kCustom, calls=%fused_computation.58 | custom fusion | bytes 155648 | tf_op jit(solution)/shard_map/scatter | solution.py:176
  46.2 0.8 %scatter_custom_fusion.1 = bf16[576,128]{1,0:T(8,128)(2,1)S(1)} fusion(bf16[576,128]{1,0:T(8,128)(2,1)S(1)} %copy.68, s32[32]{0:T(128)S(1)} %fusion.46, bf16[32,256]{1,0:T(8,128)(2,1)S(1)} %convert_element_type.50), kind=kCustom, calls=%fused_computation.56 | custom fusion | bytes 155648 | tf_op jit(solution)/shard_map/scatter | solution.py:177
  47.0 4.6 %all-to-all-done.2 = bf16[8,32,512]{2,1,0:T(8,128)(2,1)S(1)} async-done(((bf16[8,32,512]{2,1,0:T(8,128)(2,1)}), bf16[8,32,512]{2,1,0:T(8,128)(2,1)S(1)}, u32[]{:S(2)}, u32[]{:S(2)}) %all-to-all-start.2) | async-done | bytes 262176 | tf_op jit(solution)/shard_map/all_to_all | solution.py:166
  51.7 0.6 %fusion.18 = bf16[1,32,512]{2,1,0:T(8,128)(2,1)} fusion(f32[32,512]{1,0:T(8,128)S(1)} %convert_reduce_fusion, bf16[1,32,512]{2,1,0:T(8,128)(2,1)S(1)} %copy-done.4), kind=kLoop, calls=%fused_computation.37 | loop fusion | flops 49152 | bytes 131072 | tf_op jit(solution)/shard_map/convert_element_type | solution.py:168
  (48 shorter events, 1.1 us)
Async XLA Ops:
  0.6 15.2 %copy-start.2 = (bf16[1,32,128]{2,1,0:T(8,128)(2,1)S(1)}, bf16[1,32,128]{2,1,0:T(8,128)(2,1)}, u32[]{:S(2)}) copy-start(bf16[1,32,128]{2,1,0:T(8,128)(2,1)} %param.12) | copy-start | bytes 24580
  0.6 15.4 %copy-start.3 = (bf16[1,32,128]{2,1,0:T(8,128)(2,1)S(1)}, bf16[1,32,128]{2,1,0:T(8,128)(2,1)}, u32[]{:S(2)}) copy-start(bf16[1,32,128]{2,1,0:T(8,128)(2,1)} %param.13) | copy-start | bytes 24580
  0.7 14.9 %copy-start.5 = (s32[64]{0:T(128)S(1)}, s32[64]{0:T(128)}, u32[]{:S(2)}) copy-start(s32[64]{0:T(128)} %param.18) | copy-start | bytes 772
  0.7 14.1 %copy-start.7 = (s32[1,32]{1,0:T(1,128)S(1)}, s32[1,32]{1,0:T(1,128)}, u32[]{:S(2)}) copy-start(s32[1,32]{1,0:T(1,128)} %param.19) | copy-start | bytes 388
  0.7 13.2 %copy-start.6 = (s32[1,8]{1,0:T(1,128)S(1)}, s32[1,8]{1,0:T(1,128)}, u32[]{:S(2)}) copy-start(s32[1,8]{1,0:T(1,128)} %param.20) | copy-start | bytes 100
  4.0 12.3 %all-to-all-start = ((bf16[4,32,512]{2,1,0:T(8,128)(2,1)}), bf16[4,32,512]{2,1,0:T(8,128)(2,1)S(1)}, u32[]{:S(2)}, u32[]{:S(2)}) async-start(bf16[4,32,512]{2,1,0:T(8,128)(2,1)} %broadcast_in_dim.83), calls=%async_computation | async-start | bytes 262144 | tf_op jit(solution)/shard_map/all_to_all | solution.py:91
  17.7 5.5 %copy-start.8 = (s32[64]{0:T(128)S(1)}, s32[64]{0:T(128)}, u32[]{:S(2)}) copy-start(s32[64]{0:T(128)} %param.21) | copy-start | bytes 772
  18.9 10.1 %all-to-all-start.1 = ((f32[4,40,512]{2,1,0:T(8,128)}), f32[4,40,512]{2,1,0:T(8,128)S(1)}, u32[]{:S(2)}, u32[]{:S(2)}) async-start(f32[4,40,512]{2,1,0:T(8,128)} %maximum_maximum_fusion), calls=%async_computation.1 | async-start | bytes 655360 | tf_op jit(solution)/shard_map/all_to_all | solution.py:126
  30.6 21.1 %copy-start.4 = (bf16[1,32,512]{2,1,0:T(8,128)(2,1)S(1)}, bf16[1,32,512]{2,1,0:T(8,128)(2,1)}, u32[]{:S(2)}) copy-start(bf16[1,32,512]{2,1,0:T(8,128)(2,1)} %param.16) | copy-start | bytes 98308
  35.0 16.6 %all-to-all-start.2 = ((bf16[8,32,512]{2,1,0:T(8,128)(2,1)}), bf16[8,32,512]{2,1,0:T(8,128)(2,1)S(1)}, u32[]{:S(2)}, u32[]{:S(2)}) async-start(bf16[8,32,512]{2,1,0:T(8,128)(2,1)} %shard_map.130), calls=%async_computation.2 | async-start | bytes 524288 | tf_op jit(solution)/shard_map/all_to_all | solution.py:166
  46.2 6.1 %copy-start = (bf16[576,128]{1,0:T(8,128)(2,1)}, bf16[576,128]{1,0:T(8,128)(2,1)S(1)}, u32[]{:S(2)}) copy-start(bf16[576,128]{1,0:T(8,128)(2,1)S(1)} %scatter_custom_fusion) | copy-start | bytes 442372
  47.0 5.3 %copy-start.1 = (bf16[576,128]{1,0:T(8,128)(2,1)}, bf16[576,128]{1,0:T(8,128)(2,1)S(1)}, u32[]{:S(2)}) copy-start(bf16[576,128]{1,0:T(8,128)(2,1)S(1)} %scatter_custom_fusion.1) | copy-start | bytes 442372

commit v4 on v3

--- a/solution.py
+++ b/solution.py
@@ -5,6 +5,7 @@
 import numpy as np
 from jax import lax
 from jax.experimental import pallas as pl
+from jax.experimental.pallas import tpu as pltpu
 from jax.sharding import Mesh
 from jax.sharding import PartitionSpec as P
 
@@ -31,6 +32,22 @@
     return reach > 0
 
 
+def load_kernel(weight_hbm, weight_vmem, done):
+    copy = pltpu.make_async_copy(weight_hbm, weight_vmem, done)
+    copy.start()
+    copy.wait()
+
+
+def load_weight(weight):
+    return pl.pallas_call(
+        load_kernel,
+        in_specs=[pl.BlockSpec(memory_space=pl.ANY)],
+        out_specs=pl.BlockSpec(memory_space=pltpu.VMEM),
+        out_shape=jax.ShapeDtypeStruct(weight.shape, weight.dtype),
+        scratch_shapes=[pltpu.SemaphoreType.DMA(())],
+    )(weight)
+
+
 def project_kernel(attention_ref, weight_ref, out_ref):
     result = jnp.dot(attention_ref[...], weight_ref[...], preferred_element_type=jnp.float32)
     width = out_ref.shape[2]
@@ -39,17 +56,14 @@
 
 
 def project(attention, weight, pieces):
-    rows, cols = weight.shape
-    width = cols // pieces
-    per_step = 2 if pieces % 2 == 0 else 1
+    width = weight.shape[1] // pieces
     return pl.pallas_call(
         project_kernel,
-        grid=(pieces // per_step,),
         in_specs=[
-            pl.BlockSpec((attention.shape[0], rows), lambda j: (0, 0)),
-            pl.BlockSpec((rows, width * per_step), lambda j: (0, j)),
+            pl.BlockSpec(memory_space=pltpu.VMEM),
+            pl.BlockSpec(memory_space=pltpu.VMEM),
         ],
-        out_specs=pl.BlockSpec((per_step, attention.shape[0], width), lambda j: (j, 0, 0)),
+        out_specs=pl.BlockSpec(memory_space=pltpu.VMEM),
         out_shape=jax.ShapeDtypeStruct((pieces, attention.shape[0], width), jnp.bfloat16),
     )(attention, weight)
 
@@ -162,7 +176,7 @@
     attention = scale_heads(joint_out, 1.0 / joint_total).astype(jnp.bfloat16)
 
     tp_size = lax.axis_size("tp")
-    pieces = project(attention, out_weight, tp_size)
+    pieces = project(attention, load_weight(out_weight), tp_size)
     pieces = lax.all_to_all(pieces, "tp", 0, 0, tiled=True)
     summed_heads = jnp.sum(pieces.astype(jnp.float32), axis=0)
     mixed = (residual[0].astype(jnp.float32) + summed_heads).astype(jnp.bfloat16)[None]

time: 53.1 us -> 53.1 us (level)
  waiting for transfers between devices: 10.3 us -> 6.15 us
  Pallas kernels: 4.36 us -> 7.86 us
  matrix products: 1.94 us -> 2.67 us
    all_to_all x1, waiting for transfers between devices: 5.63 us -> 1.51 us  [on_device(): partials = lax.all_to_all(message, 'mem', 0, 0, tiled=True)]
    pallas_call x1 -> x2, Pallas kernels: 4.36 us -> 7.86 us  [the longest x1 4.12 us: load_weight(): pl.pallas_call(load_kernel, in_specs=[pl.BlockSpec(memory_space=pl.ANY)],...]
    dot_general x3, matrix products: 0.69 us -> 1.42 us  [ancestry(): jnp.dot(reach, reach, preferred_element_type=jnp.float32) > 0]
    sub x1, other arithmetic: 0.67 us -> 0.01 us  [on_device(): starts = jnp.cumsum(regions) - regions]
    unnamed x1, other arithmetic: 0.66 us -> 1.32 us
    unnamed x21 -> x17, local copies, waits for them, and re-layouts: 2.41 us -> 2.39 us
  transfers between devices with their start and end apart: 3 -> 3, of which waited for: 2 -> 2; matrix products, arithmetic and copies ran while one was open for 18% -> 19% of each run, Pallas kernels for 0% -> 8%
where the time goes in v4:
time: 53.1 us; the launch traced here: 52.4 us
  starting transfers between devices  19.4 us (37%)
  local copies, waits for them, and re-layouts  8.86 us (17%)
  Pallas kernels  7.86 us (15%)
  other arithmetic  6.58 us (12%)
  waiting for transfers between devices  6.15 us (12%)
  matrix products  2.67 us (5%)
  between operations  0.9 us (2%)
    all_to_all x1, starting transfers between devices, on_device(): pieces = lax.all_to_all(pieces, 'tp', 0, 0, tiled=True)  10.2 us
    all_to_all x1, starting transfers between devices, on_device(): gathered_q = lax.all_to_all(sent, 'mem', 0, 0, tiled=True)  5 us
    all_to_all x1, waiting for transfers between devices, on_device(): pieces = lax.all_to_all(pieces, 'tp', 0, 0, tiled=True)  4.64 us
    all_to_all x1, starting transfers between devices, on_device(): partials = lax.all_to_all(message, 'mem', 0, 0, tiled=True)  4.24 us
    pallas_call x1, Pallas kernels, load_weight(): pl.pallas_call(load_kernel, in_specs=[pl.BlockSpec(memory_space=pl.ANY)],...  4.12 us
    pallas_call x1, Pallas kernels, project(): pl.pallas_call(project_kernel, in_specs=[pl.BlockSpec(memory_space=pltpu....  3.73 us
    unnamed x17, local copies, waits for them, and re-layouts  2.39 us
    all_to_all x1, waiting for transfers between devices, on_device(): partials = lax.all_to_all(message, 'mem', 0, 0, tiled=True)  1.51 us
  transfers between devices with their start and end apart: 3, of which 2 were waited for; matrix products, arithmetic and copies ran while one was open for 19% of the time, Pallas kernels for 8%

profile of v4, /device:TPU:1, one launch (start us, length us, event | category | flops | bytes accessed | tf_op | source)
XLA Modules:
  0.0 52.4 jit_solution(2512453578588746504)
XLA Ops:
  0.7 0.9 %copy.67 = bf16[576,128]{1,0:T(8,128)(2,1)S(1)} copy(bf16[576,128]{1,0:T(8,128)(2,1)} %param.14) | data formatting | bytes 294912
  1.6 0.9 %copy.68 = bf16[576,128]{1,0:T(8,128)(2,1)S(1)} copy(bf16[576,128]{1,0:T(8,128)(2,1)} %param.15) | data formatting | bytes 294912
  2.5 1.4 %broadcast_in_dim.83 = bf16[4,32,512]{2,1,0:T(8,128)(2,1)} broadcast(bf16[32,512]{1,0:T(8,128)(2,1)} %bitcast.141), dimensions={1,2} | broadcast | bytes 163840 | tf_op jit(solution)/shard_map/broadcast_in_dim | solution.py:104
  3.9 5.0 %all-to-all-start = ((bf16[4,32,512]{2,1,0:T(8,128)(2,1)}), bf16[4,32,512]{2,1,0:T(8,128)(2,1)S(1)}, u32[]{:S(2)}, u32[]{:S(2)}) async-start(bf16[4,32,512]{2,1,0:T(8,128)(2,1)} %broadcast_in_dim.83), calls=%async_computation | async-start | bytes 262144 | tf_op jit(solution)/shard_map/all_to_all | solution.py:105
  8.9 0.8 %reshape.332 = bf16[32,4,128]{2,1,0:T(4,128)(2,1)S(1)} reshape(bf16[1,32,512]{2,1,0:T(8,128)(2,1)} %param.11) | data formatting | bytes 65536 | tf_op jit(solution)/shard_map/reshape.13
  9.7 0.7 %fusion.45 = s32[8]{0:T(128)S(1)} fusion(s32[1,8]{1,0:T(1,128)} %param.20), kind=kLoop, calls=%fused_computation.88 | loop fusion | flops 24 | bytes 64 | tf_op jit(solution)/shard_map/jit(_take)/jit(_where)/select_n | solution.py:131
  10.4 0.5 broadcast.187
  10.9 1.3 %reduce.10 = s32[8]{0:T(128)S(1)} reduce(s32[1,8]{1,0:T(1,128)} %param.20, s32[]{:T(128)} %broadcast.187), dimensions={0}, to_apply=%param.20.reduce_sub_computation.3 | reduce | bytes 68 | tf_op args[9]
  12.2 0.7 %add_bitcast_fusion = s32[64,1]{0,1:T(1,128)S(1)} fusion(s32[64]{0:T(128)} %param.18), kind=kLoop, calls=%fused_computation.92 | loop fusion | flops 64 | bytes 512 | tf_op jit(solution)/shard_map/reshape.287
  12.9 0.1 copy.27
  13.1 0.9 %convolution_compare_fusion.4 = pred[32,32]{1,0:T(32,128)(4,1)S(1)} fusion(s32[32]{0:T(128)} %bitcast.145), kind=kOutput, calls=%fused_computation.15 | convolution fusion | flops 69632 | bytes 1152 | tf_op jit(solution)/shard_map/dot_general | solution.py:29
  14.0 0.2 convolution_compare_fusion.2
  14.2 0.2 fusion.3
  14.5 0.1 copy.29
  14.6 0.7 %pad_maximum_fusion = bf16[32,256]{1,0:T(8,128)(2,1)S(1)} fusion(bf16[32,128]{1,0:T(8,128)(2,1)} %bitcast.143, bf16[32,128]{1,0:T(8,128)(2,1)} %bitcast.142), kind=kLoop, calls=%fused_computation.50 | loop fusion | flops 32768 | bytes 32768 | tf_op jit(solution)/shard_map/concatenate | solution.py:130
  15.3 0.6 %gather_fusion = bf16[8,256]{1,0:T(8,128)(2,1)S(1)} fusion(bf16[32,256]{1,0:T(8,128)(2,1)S(1)} %pad_maximum_fusion, s32[1024]{0:T(1024)S(1)} %pad_clamp_fusion), kind=kCustom, calls=%fused_computation | custom fusion | bytes 8224 | tf_op jit(solution)/shard_map/jit(_take)/gather | solution.py:131
  15.9 0.1 copy.24
  16.0 0.1 reduce-window.9
  16.1 0.1 reduce.4
  16.5 0.2 select_reduce_fusion.1
  16.7 0.2 convolution_bitcast_fusion.1
  16.9 0.4 select_reduce_fusion
  17.4 0.1 reshape.330
  17.5 0.4 fusion.4
  17.9 0.4 convolution_bitcast_fusion
  18.3 0.1 reshape.331
  18.4 0.2 copy.26
  18.6 0.1 reshape.329
  18.7 0.8 %maximum_maximum_fusion = f32[4,40,512]{2,1,0:T(8,128)} fusion(f32[4,4,512]{2,1,0:T(4,128)S(1)} %broadcast_in_dim.89, f32[4,1,512]{2,1,0:T(1,128)S(1)} %fusion.29, f32[4,32,512]{2,1,0:T(8,128)S(1)} %reshape.329, f32[40]{0:T(128)S(1)} %pad.8.clone), kind=kLoop, calls=%fused_computation.25 | loop fusion | flops 245760 | bytes 630944 | tf_op jit(solution)/shard_map/concatenate | solution.py:137
  19.6 4.2 %all-to-all-start.1 = ((f32[4,40,512]{2,1,0:T(8,128)}), f32[4,40,512]{2,1,0:T(8,128)S(1)}, u32[]{:S(2)}, u32[]{:S(2)}) async-start(f32[4,40,512]{2,1,0:T(8,128)} %maximum_maximum_fusion), calls=%async_computation.1 | async-start | bytes 655360 | tf_op jit(solution)/shard_map/all_to_all | solution.py:140
  24.0 4.1 %shard_map.130.weight_ref = bf16[512,4096]{1,0:T(8,128)(2,1)} custom-call(bf16[512,4096]{1,0:T(8,128)(2,1)} %weight_hbm.1), custom_call_target="tpu_custom_call" | custom-call | tf_op jit(solution)/shard_map/pallas_call | solution.py:42
  28.2 1.5 %all-to-all-done.1 = f32[4,40,512]{2,1,0:T(8,128)S(1)} async-done(((f32[4,40,512]{2,1,0:T(8,128)}), f32[4,40,512]{2,1,0:T(8,128)S(1)}, u32[]{:S(2)}, u32[]{:S(2)}) %all-to-all-start.1) | async-done | bytes 327712 | tf_op jit(solution)/shard_map/all_to_all | solution.py:140
  29.7 0.1 reshape_squeeze.2
  29.9 0.1 copy.35
  29.9 0.1 copy.34
  30.0 0.1 copy.31
  30.1 0.2 mul.85
  30.4 0.1 mul.86
  30.5 0.1 mul.88
  30.6 0.1 mul.93
  30.7 0.6 %fusion.16.attention_ref = bf16[32,512]{1,0:T(8,128)(2,1)} fusion(f32[4,8,4,128]{3,2,1,0:T(4,128)S(1)} %bitcast.139, f32[32,512]{1,0:T(8,128)S(1)} %fusion.11, f32[4,8,4,128]{3,2,1,0:T(4,128)S(1)} %bitcast.138, f32[4,8,4,128]{3,2,1,0:T(4,128)S(1)} %bitcast.140), kind=kLoop, calls=%fused_computation.33 | loop fusion | flops 65536 | bytes 294912 | tf_op jit(solution)/shard_map/convert_element_type | solution.py:176
  31.4 3.7 %shard_map.131 = bf16[8,32,512]{2,1,0:T(8,128)(2,1)} custom-call(bf16[32,512]{1,0:T(8,128)(2,1)} %fusion.16.attention_ref, bf16[512,4096]{1,0:T(8,128)(2,1)} %shard_map.130.weight_ref), custom_call_target="tpu_custom_call" | custom-call | tf_op jit(solution)/shard_map/pallas_call | solution.py:60
  35.1 10.2 %all-to-all-start.2 = ((bf16[8,32,512]{2,1,0:T(8,128)(2,1)}), bf16[8,32,512]{2,1,0:T(8,128)(2,1)S(1)}, u32[]{:S(2)}, u32[]{:S(2)}) async-start(bf16[8,32,512]{2,1,0:T(8,128)(2,1)} %shard_map.131), calls=%async_computation.2 | async-start | bytes 524288 | tf_op jit(solution)/shard_map/all_to_all | solution.py:180
  45.3 0.1 lt.95
  45.5 0.8 %scatter_custom_fusion.1 = bf16[576,128]{1,0:T(8,128)(2,1)S(1)} fusion(bf16[576,128]{1,0:T(8,128)(2,1)S(1)} %copy.68, s32[32]{0:T(128)S(1)} %fusion.46, bf16[32,256]{1,0:T(8,128)(2,1)S(1)} %convert_element_type.50), kind=kCustom, calls=%fused_computation.56 | custom fusion | bytes 155648 | tf_op jit(solution)/shard_map/scatter | solution.py:191
  46.3 0.8 %scatter_custom_fusion = bf16[576,128]{1,0:T(8,128)(2,1)S(1)} fusion(bf16[576,128]{1,0:T(8,128)(2,1)S(1)} %copy.67, s32[32]{0:T(128)S(1)} %fusion.46, bf16[32,256]{1,0:T(8,128)(2,1)S(1)} %convert_element_type.50), kind=kCustom, calls=%fused_computation.58 | custom fusion | bytes 155648 | tf_op jit(solution)/shard_map/scatter | solution.py:190
  47.1 4.6 %all-to-all-done.2 = bf16[8,32,512]{2,1,0:T(8,128)(2,1)S(1)} async-done(((bf16[8,32,512]{2,1,0:T(8,128)(2,1)}), bf16[8,32,512]{2,1,0:T(8,128)(2,1)S(1)}, u32[]{:S(2)}, u32[]{:S(2)}) %all-to-all-start.2) | async-done | bytes 262176 | tf_op jit(solution)/shard_map/all_to_all | solution.py:180
  51.8 0.6 %fusion.18 = bf16[1,32,512]{2,1,0:T(8,128)(2,1)} fusion(f32[32,512]{1,0:T(8,128)S(1)} %convert_reduce_fusion, bf16[1,32,512]{2,1,0:T(8,128)(2,1)S(1)} %copy-done.4), kind=kLoop, calls=%fused_computation.37 | loop fusion | flops 49152 | bytes 131072 | tf_op jit(solution)/shard_map/convert_element_type | solution.py:182
  (45 shorter events, 1.1 us)
Async XLA Ops:
  0.6 15.8 %copy-start.2 = (bf16[1,32,128]{2,1,0:T(8,128)(2,1)S(1)}, bf16[1,32,128]{2,1,0:T(8,128)(2,1)}, u32[]{:S(2)}) copy-start(bf16[1,32,128]{2,1,0:T(8,128)(2,1)} %param.12) | copy-start | bytes 24580
  0.6 16.1 %copy-start.3 = (bf16[1,32,128]{2,1,0:T(8,128)(2,1)S(1)}, bf16[1,32,128]{2,1,0:T(8,128)(2,1)}, u32[]{:S(2)}) copy-start(bf16[1,32,128]{2,1,0:T(8,128)(2,1)} %param.13) | copy-start | bytes 24580
  0.7 15.5 %copy-start.5 = (s32[64]{0:T(128)S(1)}, s32[64]{0:T(128)}, u32[]{:S(2)}) copy-start(s32[64]{0:T(128)} %param.18) | copy-start | bytes 772
  3.9 13.0 %all-to-all-start = ((bf16[4,32,512]{2,1,0:T(8,128)(2,1)}), bf16[4,32,512]{2,1,0:T(8,128)(2,1)S(1)}, u32[]{:S(2)}, u32[]{:S(2)}) async-start(bf16[4,32,512]{2,1,0:T(8,128)(2,1)} %broadcast_in_dim.83), calls=%async_computation | async-start | bytes 262144 | tf_op jit(solution)/shard_map/all_to_all | solution.py:105
  18.3 5.5 %copy-start.6 = (s32[64]{0:T(128)S(1)}, s32[64]{0:T(128)}, u32[]{:S(2)}) copy-start(s32[64]{0:T(128)} %param.21) | copy-start | bytes 772
  19.6 10.1 %all-to-all-start.1 = ((f32[4,40,512]{2,1,0:T(8,128)}), f32[4,40,512]{2,1,0:T(8,128)S(1)}, u32[]{:S(2)}, u32[]{:S(2)}) async-start(f32[4,40,512]{2,1,0:T(8,128)} %maximum_maximum_fusion), calls=%async_computation.1 | async-start | bytes 655360 | tf_op jit(solution)/shard_map/all_to_all | solution.py:140
  31.3 20.4 %copy-start.4 = (bf16[1,32,512]{2,1,0:T(8,128)(2,1)S(1)}, bf16[1,32,512]{2,1,0:T(8,128)(2,1)}, u32[]{:S(2)}) copy-start(bf16[1,32,512]{2,1,0:T(8,128)(2,1)} %param.16) | copy-start | bytes 98308
  35.1 16.6 %all-to-all-start.2 = ((bf16[8,32,512]{2,1,0:T(8,128)(2,1)}), bf16[8,32,512]{2,1,0:T(8,128)(2,1)S(1)}, u32[]{:S(2)}, u32[]{:S(2)}) async-start(bf16[8,32,512]{2,1,0:T(8,128)(2,1)} %shard_map.131), calls=%async_computation.2 | async-start | bytes 524288 | tf_op jit(solution)/shard_map/all_to_all | solution.py:180
  46.3 6.1 %copy-start.1 = (bf16[576,128]{1,0:T(8,128)(2,1)}, bf16[576,128]{1,0:T(8,128)(2,1)S(1)}, u32[]{:S(2)}) copy-start(bf16[576,128]{1,0:T(8,128)(2,1)S(1)} %scatter_custom_fusion.1) | copy-start | bytes 442372
  47.1 5.3 %copy-start = (bf16[576,128]{1,0:T(8,128)(2,1)}, bf16[576,128]{1,0:T(8,128)(2,1)S(1)}, u32[]{:S(2)}) copy-start(bf16[576,128]{1,0:T(8,128)(2,1)S(1)} %scatter_custom_fusion) | copy-start | bytes 442372

commit v5 on v3

--- a/solution.py
+++ b/solution.py
@@ -5,6 +5,7 @@
 import numpy as np
 from jax import lax
 from jax.experimental import pallas as pl
+from jax.experimental.pallas import tpu as pltpu
 from jax.sharding import Mesh
 from jax.sharding import PartitionSpec as P
 
@@ -31,8 +32,29 @@
     return reach > 0
 
 
-def project_kernel(attention_ref, weight_ref, out_ref):
-    result = jnp.dot(attention_ref[...], weight_ref[...], preferred_element_type=jnp.float32)
+CHUNKS = 8
+
+
+def project_kernel(attention_ref, weight_hbm, out_ref, weight_vmem, landed):
+    rows = weight_vmem.shape[1]
+    copies = [
+        pltpu.make_async_copy(
+            weight_hbm.at[pl.ds(chunk * rows, rows)], weight_vmem.at[chunk], landed.at[chunk]
+        )
+        for chunk in range(CHUNKS)
+    ]
+    for copy in copies:
+        copy.start()
+    attention = attention_ref[...]
+    result = None
+    for chunk in range(CHUNKS):
+        copies[chunk].wait()
+        part = jnp.dot(
+            attention[:, chunk * rows : (chunk + 1) * rows],
+            weight_vmem[chunk],
+            preferred_element_type=jnp.float32,
+        )
+        result = part if result is None else result + part
     width = out_ref.shape[2]
     for piece in range(out_ref.shape[0]):
         out_ref[piece] = result[:, piece * width : (piece + 1) * width].astype(out_ref.dtype)
@@ -40,17 +62,18 @@
 
 def project(attention, weight, pieces):
     rows, cols = weight.shape
-    width = cols // pieces
-    per_step = 2 if pieces % 2 == 0 else 1
     return pl.pallas_call(
         project_kernel,
-        grid=(pieces // per_step,),
         in_specs=[
-            pl.BlockSpec((attention.shape[0], rows), lambda j: (0, 0)),
-            pl.BlockSpec((rows, width * per_step), lambda j: (0, j)),
+            pl.BlockSpec(memory_space=pltpu.VMEM),
+            pl.BlockSpec(memory_space=pl.ANY),
         ],
-        out_specs=pl.BlockSpec((per_step, attention.shape[0], width), lambda j: (j, 0, 0)),
-        out_shape=jax.ShapeDtypeStruct((pieces, attention.shape[0], width), jnp.bfloat16),
+        out_specs=pl.BlockSpec(memory_space=pltpu.VMEM),
+        out_shape=jax.ShapeDtypeStruct((pieces, attention.shape[0], cols // pieces), jnp.bfloat16),
+        scratch_shapes=[
+            pltpu.VMEM((CHUNKS, rows // CHUNKS, cols), weight.dtype),
+            pltpu.SemaphoreType.DMA((CHUNKS,)),
+        ],
     )(attention, weight)
 
 

time: 53.1 us -> 52.7 us (level)
  no operation moved by 1% of the time
where the time goes in v5:
time: 52.7 us; the launch traced here: 51.9 us
  starting transfers between devices  19.4 us (37%)
  waiting for transfers between devices  10.3 us (20%)
  local copies, waits for them, and re-layouts  8.89 us (17%)
  other arithmetic  6.57 us (12%)
  Pallas kernels  3.94 us (7%)
  matrix products  1.94 us (4%)
  between operations  0.91 us (2%)
    all_to_all x1, starting transfers between devices, on_device(): pieces = lax.all_to_all(pieces, 'tp', 0, 0, tiled=True)  10.2 us
    all_to_all x1, waiting for transfers between devices, on_device(): partials = lax.all_to_all(message, 'mem', 0, 0, tiled=True)  5.63 us
    all_to_all x1, starting transfers between devices, on_device(): gathered_q = lax.all_to_all(sent, 'mem', 0, 0, tiled=True)  5 us
    all_to_all x1, waiting for transfers between devices, on_device(): pieces = lax.all_to_all(pieces, 'tp', 0, 0, tiled=True)  4.65 us
    all_to_all x1, starting transfers between devices, on_device(): partials = lax.all_to_all(message, 'mem', 0, 0, tiled=True)  4.24 us
    pallas_call x1, Pallas kernels, project(): pl.pallas_call(project_kernel, in_specs=[pl.BlockSpec(memory_space=pltpu....  3.94 us
    unnamed x21, local copies, waits for them, and re-layouts  2.41 us
    broadcast_in_dim x1, local copies, waits for them, and re-layouts, on_device(): sent = jnp.broadcast_to(queries, (GROUP,) + queries.shape[1:])  1.42 us
  transfers between devices with their start and end apart: 3, of which 2 were waited for; matrix products, arithmetic and copies ran while one was open for 18% of the time, Pallas kernels for 0%

profile of v5, /device:TPU:1, one launch (start us, length us, event | category | flops | bytes accessed | tf_op | source)
XLA Modules:
  0.0 51.9 jit_solution(8538517541416023606)
XLA Ops:
  0.7 0.9 %copy.67 = bf16[576,128]{1,0:T(8,128)(2,1)S(1)} copy(bf16[576,128]{1,0:T(8,128)(2,1)} %param.14) | data formatting | bytes 294912
  1.6 0.9 %copy.68 = bf16[576,128]{1,0:T(8,128)(2,1)S(1)} copy(bf16[576,128]{1,0:T(8,128)(2,1)} %param.15) | data formatting | bytes 294912
  2.5 1.4 %broadcast_in_dim.83 = bf16[4,32,512]{2,1,0:T(8,128)(2,1)} broadcast(bf16[32,512]{1,0:T(8,128)(2,1)} %bitcast.139), dimensions={1,2} | broadcast | bytes 163840 | tf_op jit(solution)/shard_map/broadcast_in_dim | solution.py:113
  4.0 5.0 %all-to-all-start = ((bf16[4,32,512]{2,1,0:T(8,128)(2,1)}), bf16[4,32,512]{2,1,0:T(8,128)(2,1)S(1)}, u32[]{:S(2)}, u32[]{:S(2)}) async-start(bf16[4,32,512]{2,1,0:T(8,128)(2,1)} %broadcast_in_dim.83), calls=%async_computation | async-start | bytes 262144 | tf_op jit(solution)/shard_map/all_to_all | solution.py:114
  9.0 0.8 %reshape.332 = bf16[32,4,128]{2,1,0:T(4,128)(2,1)S(1)} reshape(bf16[1,32,512]{2,1,0:T(8,128)(2,1)} %param.11) | data formatting | bytes 65536 | tf_op jit(solution)/shard_map/reshape.13
  9.7 0.7 %add_bitcast_fusion = s32[64,1]{0,1:T(1,128)S(1)} fusion(s32[64]{0:T(128)} %param.18), kind=kLoop, calls=%fused_computation.92 | loop fusion | flops 64 | bytes 512 | tf_op jit(solution)/shard_map/reshape.287
  10.4 0.1 copy.24
  10.5 0.1 reduce-window.9
  10.6 0.1 reduce.4
  10.7 0.7 %add_subtract_fusion.1 = s32[64]{0:T(128)S(1)} fusion(s32[64]{0:T(128)S(1)} %reduce.4, s32[64]{0:T(128)} %param.18), kind=kLoop, calls=%fused_computation.91 | loop fusion | flops 128 | bytes 768 | tf_op jit(solution)/shard_map/sub | solution.py:107
  11.4 0.7 %fusion.45 = s32[8]{0:T(128)S(1)} fusion(s32[1,8]{1,0:T(1,128)} %param.20), kind=kLoop, calls=%fused_computation.88 | loop fusion | flops 24 | bytes 64 | tf_op jit(solution)/shard_map/jit(_take)/jit(_where)/select_n | solution.py:140
  12.0 0.7 %pad_maximum_fusion = bf16[32,256]{1,0:T(8,128)(2,1)S(1)} fusion(bf16[32,128]{1,0:T(8,128)(2,1)} %bitcast.141, bf16[32,128]{1,0:T(8,128)(2,1)} %bitcast.140), kind=kLoop, calls=%fused_computation.50 | loop fusion | flops 32768 | bytes 32768 | tf_op jit(solution)/shard_map/concatenate | solution.py:139
  12.8 0.6 %gather_fusion = bf16[8,256]{1,0:T(8,128)(2,1)S(1)} fusion(bf16[32,256]{1,0:T(8,128)(2,1)S(1)} %pad_maximum_fusion, s32[1024]{0:T(1024)S(1)} %pad_clamp_fusion), kind=kCustom, calls=%fused_computation | custom fusion | bytes 8224 | tf_op jit(solution)/shard_map/jit(_take)/gather | solution.py:140
  13.3 0.5 broadcast.187
  13.9 0.7 %reduce.10 = s32[8]{0:T(128)S(1)} reduce(s32[1,8]{1,0:T(1,128)S(1)} %copy-done.6, s32[]{:T(128)} %broadcast.187), dimensions={0}, to_apply=%param.20.reduce_sub_computation.3 | reduce | bytes 68 | tf_op args[9]
  14.6 0.1 copy.27
  14.7 0.2 convolution_compare_fusion.4
  14.9 0.2 convolution_compare_fusion.2
  15.2 0.2 fusion.3
  15.4 0.1 copy.29
  15.8 0.2 select_reduce_fusion.1
  16.1 0.2 convolution_bitcast_fusion.1
  16.2 0.4 select_reduce_fusion
  16.7 0.1 reshape.330
  16.8 0.4 fusion.4
  17.2 0.1 reshape.331
  17.3 0.4 convolution_bitcast_fusion
  17.7 0.2 copy.26
  17.9 0.1 reshape.329
  18.1 0.8 %maximum_maximum_fusion = f32[4,40,512]{2,1,0:T(8,128)} fusion(f32[4,4,512]{2,1,0:T(4,128)S(1)} %broadcast_in_dim.89, f32[4,1,512]{2,1,0:T(1,128)S(1)} %fusion.29, f32[4,32,512]{2,1,0:T(8,128)S(1)} %reshape.329, f32[40]{0:T(128)S(1)} %pad.8.clone), kind=kLoop, calls=%fused_computation.25 | loop fusion | flops 245760 | bytes 630944 | tf_op jit(solution)/shard_map/concatenate | solution.py:146
  18.9 4.2 %all-to-all-start.1 = ((f32[4,40,512]{2,1,0:T(8,128)}), f32[4,40,512]{2,1,0:T(8,128)S(1)}, u32[]{:S(2)}, u32[]{:S(2)}) async-start(f32[4,40,512]{2,1,0:T(8,128)} %maximum_maximum_fusion), calls=%async_computation.1 | async-start | bytes 655360 | tf_op jit(solution)/shard_map/all_to_all | solution.py:149
  23.4 5.6 %all-to-all-done.1 = f32[4,40,512]{2,1,0:T(8,128)S(1)} async-done(((f32[4,40,512]{2,1,0:T(8,128)}), f32[4,40,512]{2,1,0:T(8,128)S(1)}, u32[]{:S(2)}, u32[]{:S(2)}) %all-to-all-start.1) | async-done | bytes 327712 | tf_op jit(solution)/shard_map/all_to_all | solution.py:149
  29.0 0.1 reshape_squeeze.2
  29.1 0.1 copy.31
  29.3 0.2 mul.85
  29.5 0.1 mul.86
  29.6 0.1 copy.34
  29.7 0.1 copy.35
  29.8 0.1 mul.88
  29.9 0.1 mul.93
  30.0 0.6 %fusion.16.attention_ref = bf16[32,512]{1,0:T(8,128)(2,1)} fusion(f32[4,8,4,128]{3,2,1,0:T(4,128)S(1)} %bitcast.137, f32[32,512]{1,0:T(8,128)S(1)} %fusion.11, f32[4,8,4,128]{3,2,1,0:T(4,128)S(1)} %bitcast.136, f32[4,8,4,128]{3,2,1,0:T(4,128)S(1)} %bitcast.138), kind=kLoop, calls=%fused_computation.33 | loop fusion | flops 65536 | bytes 294912 | tf_op jit(solution)/shard_map/convert_element_type | solution.py:185
  30.6 3.9 %shard_map.130 = bf16[8,32,512]{2,1,0:T(8,128)(2,1)} custom-call(bf16[32,512]{1,0:T(8,128)(2,1)} %fusion.16.attention_ref, bf16[512,4096]{1,0:T(8,128)(2,1)} %weight_hbm.1), custom_call_target="tpu_custom_call" | custom-call | tf_op jit(solution)/shard_map/pallas_call | solution.py:65
  34.6 10.2 %all-to-all-start.2 = ((bf16[8,32,512]{2,1,0:T(8,128)(2,1)}), bf16[8,32,512]{2,1,0:T(8,128)(2,1)S(1)}, u32[]{:S(2)}, u32[]{:S(2)}) async-start(bf16[8,32,512]{2,1,0:T(8,128)(2,1)} %shard_map.130), calls=%async_computation.2 | async-start | bytes 524288 | tf_op jit(solution)/shard_map/all_to_all | solution.py:189
  44.9 0.1 lt.95
  45.0 0.8 %scatter_custom_fusion = bf16[576,128]{1,0:T(8,128)(2,1)S(1)} fusion(bf16[576,128]{1,0:T(8,128)(2,1)S(1)} %copy.67, s32[32]{0:T(128)S(1)} %fusion.46, bf16[32,256]{1,0:T(8,128)(2,1)S(1)} %convert_element_type.50), kind=kCustom, calls=%fused_computation.58 | custom fusion | bytes 155648 | tf_op jit(solution)/shard_map/scatter | solution.py:199
  45.8 0.8 %scatter_custom_fusion.1 = bf16[576,128]{1,0:T(8,128)(2,1)S(1)} fusion(bf16[576,128]{1,0:T(8,128)(2,1)S(1)} %copy.68, s32[32]{0:T(128)S(1)} %fusion.46, bf16[32,256]{1,0:T(8,128)(2,1)S(1)} %convert_element_type.50), kind=kCustom, calls=%fused_computation.56 | custom fusion | bytes 155648 | tf_op jit(solution)/shard_map/scatter | solution.py:200
  46.6 4.6 %all-to-all-done.2 = bf16[8,32,512]{2,1,0:T(8,128)(2,1)S(1)} async-done(((bf16[8,32,512]{2,1,0:T(8,128)(2,1)}), bf16[8,32,512]{2,1,0:T(8,128)(2,1)S(1)}, u32[]{:S(2)}, u32[]{:S(2)}) %all-to-all-start.2) | async-done | bytes 262176 | tf_op jit(solution)/shard_map/all_to_all | solution.py:189
  51.3 0.6 %fusion.18 = bf16[1,32,512]{2,1,0:T(8,128)(2,1)} fusion(f32[32,512]{1,0:T(8,128)S(1)} %convert_reduce_fusion, bf16[1,32,512]{2,1,0:T(8,128)(2,1)S(1)} %copy-done.4), kind=kLoop, calls=%fused_computation.37 | loop fusion | flops 49152 | bytes 131072 | tf_op jit(solution)/shard_map/convert_element_type | solution.py:191
  (48 shorter events, 1.1 us)
Async XLA Ops:
  0.6 15.2 %copy-start.2 = (bf16[1,32,128]{2,1,0:T(8,128)(2,1)S(1)}, bf16[1,32,128]{2,1,0:T(8,128)(2,1)}, u32[]{:S(2)}) copy-start(bf16[1,32,128]{2,1,0:T(8,128)(2,1)} %param.12) | copy-start | bytes 24580
  0.6 15.4 %copy-start.3 = (bf16[1,32,128]{2,1,0:T(8,128)(2,1)S(1)}, bf16[1,32,128]{2,1,0:T(8,128)(2,1)}, u32[]{:S(2)}) copy-start(bf16[1,32,128]{2,1,0:T(8,128)(2,1)} %param.13) | copy-start | bytes 24580
  0.7 14.9 %copy-start.5 = (s32[64]{0:T(128)S(1)}, s32[64]{0:T(128)}, u32[]{:S(2)}) copy-start(s32[64]{0:T(128)} %param.18) | copy-start | bytes 772
  0.7 14.1 %copy-start.7 = (s32[1,32]{1,0:T(1,128)S(1)}, s32[1,32]{1,0:T(1,128)}, u32[]{:S(2)}) copy-start(s32[1,32]{1,0:T(1,128)} %param.19) | copy-start | bytes 388
  0.7 13.2 %copy-start.6 = (s32[1,8]{1,0:T(1,128)S(1)}, s32[1,8]{1,0:T(1,128)}, u32[]{:S(2)}) copy-start(s32[1,8]{1,0:T(1,128)} %param.20) | copy-start | bytes 100
  4.0 12.3 %all-to-all-start = ((bf16[4,32,512]{2,1,0:T(8,128)(2,1)}), bf16[4,32,512]{2,1,0:T(8,128)(2,1)S(1)}, u32[]{:S(2)}, u32[]{:S(2)}) async-start(bf16[4,32,512]{2,1,0:T(8,128)(2,1)} %broadcast_in_dim.83), calls=%async_computation | async-start | bytes 262144 | tf_op jit(solution)/shard_map/all_to_all | solution.py:114
  17.7 5.5 %copy-start.8 = (s32[64]{0:T(128)S(1)}, s32[64]{0:T(128)}, u32[]{:S(2)}) copy-start(s32[64]{0:T(128)} %param.21) | copy-start | bytes 772
  18.9 10.1 %all-to-all-start.1 = ((f32[4,40,512]{2,1,0:T(8,128)}), f32[4,40,512]{2,1,0:T(8,128)S(1)}, u32[]{:S(2)}, u32[]{:S(2)}) async-start(f32[4,40,512]{2,1,0:T(8,128)} %maximum_maximum_fusion), calls=%async_computation.1 | async-start | bytes 655360 | tf_op jit(solution)/shard_map/all_to_all | solution.py:149
  30.6 20.7 %copy-start.4 = (bf16[1,32,512]{2,1,0:T(8,128)(2,1)S(1)}, bf16[1,32,512]{2,1,0:T(8,128)(2,1)}, u32[]{:S(2)}) copy-start(bf16[1,32,512]{2,1,0:T(8,128)(2,1)} %param.16) | copy-start | bytes 98308
  34.6 16.7 %all-to-all-start.2 = ((bf16[8,32,512]{2,1,0:T(8,128)(2,1)}), bf16[8,32,512]{2,1,0:T(8,128)(2,1)S(1)}, u32[]{:S(2)}, u32[]{:S(2)}) async-start(bf16[8,32,512]{2,1,0:T(8,128)(2,1)} %shard_map.130), calls=%async_computation.2 | async-start | bytes 524288 | tf_op jit(solution)/shard_map/all_to_all | solution.py:189
  45.8 6.1 %copy-start = (bf16[576,128]{1,0:T(8,128)(2,1)}, bf16[576,128]{1,0:T(8,128)(2,1)S(1)}, u32[]{:S(2)}) copy-start(bf16[576,128]{1,0:T(8,128)(2,1)S(1)} %scatter_custom_fusion) | copy-start | bytes 442372
  46.6 5.3 %copy-start.1 = (bf16[576,128]{1,0:T(8,128)(2,1)}, bf16[576,128]{1,0:T(8,128)(2,1)S(1)}, u32[]{:S(2)}) copy-start(bf16[576,128]{1,0:T(8,128)(2,1)S(1)} %scatter_custom_fusion.1) | copy-start | bytes 442372

commit v6 on v3

--- a/solution.py
+++ b/solution.py
@@ -5,6 +5,7 @@
 import numpy as np
 from jax import lax
 from jax.experimental import pallas as pl
+from jax.experimental.pallas import tpu as pltpu
 from jax.sharding import Mesh
 from jax.sharding import PartitionSpec as P
 
@@ -31,27 +32,25 @@
     return reach > 0
 
 
-def project_kernel(attention_ref, weight_ref, out_ref):
-    result = jnp.dot(attention_ref[...], weight_ref[...], preferred_element_type=jnp.float32)
-    width = out_ref.shape[2]
-    for piece in range(out_ref.shape[0]):
-        out_ref[piece] = result[:, piece * width : (piece + 1) * width].astype(out_ref.dtype)
-
-
-def project(attention, weight, pieces):
-    rows, cols = weight.shape
-    width = cols // pieces
-    per_step = 2 if pieces % 2 == 0 else 1
+def copies_kernel(source_hbm, target_hbm, landed):
+    copies = [
+        pltpu.make_async_copy(source_hbm, target_hbm.at[pl.ds(slot, 1)], landed.at[slot])
+        for slot in range(target_hbm.shape[0])
+    ]
+    for copy in copies:
+        copy.start()
+    for copy in copies:
+        copy.wait()
+
+
+def replicate(block, count):
     return pl.pallas_call(
-        project_kernel,
-        grid=(pieces // per_step,),
-        in_specs=[
-            pl.BlockSpec((attention.shape[0], rows), lambda j: (0, 0)),
-            pl.BlockSpec((rows, width * per_step), lambda j: (0, j)),
-        ],
-        out_specs=pl.BlockSpec((per_step, attention.shape[0], width), lambda j: (j, 0, 0)),
-        out_shape=jax.ShapeDtypeStruct((pieces, attention.shape[0], width), jnp.bfloat16),
-    )(attention, weight)
+        copies_kernel,
+        in_specs=[pl.BlockSpec(memory_space=pl.ANY)],
+        out_specs=pl.BlockSpec(memory_space=pl.ANY),
+        out_shape=jax.ShapeDtypeStruct((count,) + block.shape[1:], block.dtype),
+        scratch_shapes=[pltpu.SemaphoreType.DMA((count,))],
+    )(block)
 
 
 def scale_heads(values, factors):
@@ -87,7 +86,7 @@
     keys_local = cache_keys.reshape(positions, kv_local, HD)
     values_local = cache_values.reshape(positions, kv_local, HD)
 
-    sent = jnp.broadcast_to(queries, (GROUP,) + queries.shape[1:])
+    sent = replicate(queries, GROUP)
     gathered_q = lax.all_to_all(sent, "mem", 0, 0, tiled=True)
 
     group_base = seq_rank - member
@@ -162,10 +161,13 @@
     attention = scale_heads(joint_out, 1.0 / joint_total).astype(jnp.bfloat16)
 
     tp_size = lax.axis_size("tp")
-    pieces = project(attention, out_weight, tp_size)
+    projected = lax.dot_general(
+        out_weight, attention, (((0,), (1,)), ((), ())), preferred_element_type=jnp.float32
+    ).astype(jnp.bfloat16)
+    pieces = projected.reshape(tp_size, -1, TREE)
     pieces = lax.all_to_all(pieces, "tp", 0, 0, tiled=True)
     summed_heads = jnp.sum(pieces.astype(jnp.float32), axis=0)
-    mixed = (residual[0].astype(jnp.float32) + summed_heads).astype(jnp.bfloat16)[None]
+    mixed = (residual[0].astype(jnp.float32) + summed_heads.T).astype(jnp.bfloat16)[None]
 
     row_accepted = lax.dynamic_slice_in_dim(accept_len, group_base, GROUP)
     column = jnp.arange(A_MAX, dtype=jnp.int32)

time: 53.1 us -> 55.4 us (1.043)
  matrix products: 1.94 us -> 4.95 us
  Pallas kernels: 4.36 us -> 5.1 us
  local copies, waits for them, and re-layouts: 8.89 us -> 8.19 us
  other arithmetic: 6.57 us -> 5.94 us
    dot_general x0 -> x1, matrix products: none -> 3 us  [on_device(): lax.dot_general(out_weight, attention, (((0,), (1,)), ((), ())), preferre...]
    broadcast_in_dim x1 -> x0, local copies, waits for them, and re-layouts: 1.42 us -> none  [on_device(): sent = jnp.broadcast_to(queries, (GROUP,) + queries.shape[1:])]
    convert_element_type x2 -> x0, other arithmetic: 1.26 us -> none  [the longest x1 0.64 us: on_device(): attention = scale_heads(joint_out, 1.0 / joint_total).astype(jnp.bfloat16)]
    pallas_call x1, Pallas kernels: 4.36 us -> 5.1 us  [replicate(): pl.pallas_call(copies_kernel, in_specs=[pl.BlockSpec(memory_space=pl.ANY)...]
    reshape x0 -> x1, local copies, waits for them, and re-layouts: none -> 0.72 us  [on_device(): pieces = projected.reshape(tp_size, -1, TREE)]
    broadcast_in_dim x0 -> x1, other arithmetic: none -> 0.63 us  [on_device(): (residual[0].astype(jnp.float32) + summed_heads.T).astype(jnp.bfloat16)]
  transfers between devices with their start and end apart: 3 -> 3, of which waited for: 2 -> 2; matrix products, arithmetic and copies ran while one was open for 18% -> 17% of each run, Pallas kernels for 0% -> 0%
where the time goes in v6:
time: 55.4 us; the launch traced here: 54.8 us
  starting transfers between devices  19.4 us (35%)
  waiting for transfers between devices  10.3 us (19%)
  local copies, waits for them, and re-layouts  8.19 us (15%)
  other arithmetic  5.94 us (11%)
  Pallas kernels  5.1 us (9%)
  matrix products  4.95 us (9%)
  between operations  0.91 us (2%)
    all_to_all x1, starting transfers between devices, on_device(): pieces = lax.all_to_all(pieces, 'tp', 0, 0, tiled=True)  10.2 us
    all_to_all x1, waiting for transfers between devices, on_device(): partials = lax.all_to_all(message, 'mem', 0, 0, tiled=True)  5.63 us
    pallas_call x1, Pallas kernels, replicate(): pl.pallas_call(copies_kernel, in_specs=[pl.BlockSpec(memory_space=pl.ANY)...  5.1 us
    all_to_all x1, starting transfers between devices, on_device(): gathered_q = lax.all_to_all(sent, 'mem', 0, 0, tiled=True)  5.01 us
    all_to_all x1, waiting for transfers between devices, on_device(): pieces = lax.all_to_all(pieces, 'tp', 0, 0, tiled=True)  4.65 us
    all_to_all x1, starting transfers between devices, on_device(): partials = lax.all_to_all(message, 'mem', 0, 0, tiled=True)  4.23 us
    dot_general x1, matrix products, on_device(): lax.dot_general(out_weight, attention, (((0,), (1,)), ((), ())), preferre...  3 us
    unnamed x21, local copies, waits for them, and re-layouts  2.42 us
  transfers between devices with their start and end apart: 3, of which 2 were waited for; matrix products, arithmetic and copies ran while one was open for 17% of the time, Pallas kernels for 0%

profile of v6, /device:TPU:1, one launch (start us, length us, event | category | flops | bytes accessed | tf_op | source)
XLA Modules:
  0.0 54.8 jit_solution(7534504798210176938)
XLA Ops:
  0.7 0.9 %copy.86 = bf16[576,128]{1,0:T(8,128)(2,1)S(1)} copy(bf16[576,128]{1,0:T(8,128)(2,1)} %param.14) | data formatting | bytes 294912
  1.6 0.9 %copy.87 = bf16[576,128]{1,0:T(8,128)(2,1)S(1)} copy(bf16[576,128]{1,0:T(8,128)(2,1)} %param.15) | data formatting | bytes 294912
  2.5 5.1 %shard_map.130 = bf16[4,32,512]{2,1,0:T(8,128)(2,1)} custom-call(bf16[1,32,512]{2,1,0:T(8,128)(2,1)} %source_hbm.1), custom_call_target="tpu_custom_call" | custom-call | tf_op jit(solution)/shard_map/pallas_call | solution.py:47
  7.6 5.0 %all-to-all-start = ((bf16[4,32,512]{2,1,0:T(8,128)(2,1)}), bf16[4,32,512]{2,1,0:T(8,128)(2,1)S(1)}, u32[]{:S(2)}, u32[]{:S(2)}) async-start(bf16[4,32,512]{2,1,0:T(8,128)(2,1)} %shard_map.130), calls=%async_computation | async-start | bytes 262144 | tf_op jit(solution)/shard_map/all_to_all | solution.py:90
  12.7 0.8 %reshape.336 = bf16[32,4,128]{2,1,0:T(4,128)(2,1)S(1)} reshape(bf16[1,32,512]{2,1,0:T(8,128)(2,1)} %source_hbm.1) | data formatting | bytes 65536 | tf_op jit(solution)/shard_map/reshape.13
  13.4 0.7 %add_bitcast_fusion = s32[64,1]{0,1:T(1,128)S(1)} fusion(s32[64]{0:T(128)} %param.18), kind=kLoop, calls=%fused_computation.95 | loop fusion | flops 64 | bytes 512 | tf_op jit(solution)/shard_map/reshape.287
  14.1 0.1 copy.36
  14.2 0.1 reduce-window.9
  14.3 0.1 reduce.4
  14.4 0.7 %add_subtract_fusion.1 = s32[64]{0:T(128)S(1)} fusion(s32[64]{0:T(128)S(1)} %reduce.4, s32[64]{0:T(128)} %param.18), kind=kLoop, calls=%fused_computation.94 | loop fusion | flops 128 | bytes 768 | tf_op jit(solution)/shard_map/sub | solution.py:83
  15.1 0.7 %fusion.47 = s32[8]{0:T(128)S(1)} fusion(s32[1,8]{1,0:T(1,128)} %param.20), kind=kLoop, calls=%fused_computation.91 | loop fusion | flops 24 | bytes 64 | tf_op jit(solution)/shard_map/jit(_take)/jit(_where)/select_n | solution.py:116
  15.7 0.7 %pad_maximum_fusion = bf16[32,256]{1,0:T(8,128)(2,1)S(1)} fusion(bf16[32,128]{1,0:T(8,128)(2,1)} %bitcast.154, bf16[32,128]{1,0:T(8,128)(2,1)} %bitcast.153), kind=kLoop, calls=%fused_computation.53 | loop fusion | flops 32768 | bytes 32768 | tf_op jit(solution)/shard_map/concatenate | solution.py:115
  16.5 0.6 %gather_fusion = bf16[8,256]{1,0:T(8,128)(2,1)S(1)} fusion(bf16[32,256]{1,0:T(8,128)(2,1)S(1)} %pad_maximum_fusion, s32[1024]{0:T(1024)S(1)} %pad_clamp_fusion), kind=kCustom, calls=%fused_computation | custom fusion | bytes 8224 | tf_op jit(solution)/shard_map/jit(_take)/gather | solution.py:116
  17.0 0.5 broadcast.187
  17.6 0.7 %reduce.10 = s32[8]{0:T(128)S(1)} reduce(s32[1,8]{1,0:T(1,128)S(1)} %copy-done.6, s32[]{:T(128)} %broadcast.187), dimensions={0}, to_apply=%param.20.reduce_sub_computation.3 | reduce | bytes 68 | tf_op args[9]
  18.3 0.1 copy.39
  18.4 0.2 convolution_compare_fusion.4
  18.6 0.2 convolution_compare_fusion.2
  18.9 0.2 fusion.3
  19.1 0.1 copy.41
  19.5 0.2 select_reduce_fusion.1
  19.8 0.2 convolution_bitcast_fusion.1
  20.0 0.4 select_reduce_fusion
  20.4 0.1 reshape.334
  20.5 0.4 fusion.4
  20.9 0.1 reshape.335
  21.0 0.4 convolution_bitcast_fusion
  21.5 0.2 copy.38
  21.6 0.1 reshape.333
  21.8 0.8 %maximum_maximum_fusion = f32[4,40,512]{2,1,0:T(8,128)} fusion(f32[4,4,512]{2,1,0:T(4,128)S(1)} %broadcast_in_dim.82, f32[4,1,512]{2,1,0:T(1,128)S(1)} %fusion.31, f32[4,32,512]{2,1,0:T(8,128)S(1)} %reshape.333, f32[40]{0:T(128)S(1)} %pad.8.clone), kind=kLoop, calls=%fused_computation.26 | loop fusion | flops 245760 | bytes 630944 | tf_op jit(solution)/shard_map/concatenate | solution.py:122
  22.6 4.2 %all-to-all-start.1 = ((f32[4,40,512]{2,1,0:T(8,128)}), f32[4,40,512]{2,1,0:T(8,128)S(1)}, u32[]{:S(2)}, u32[]{:S(2)}) async-start(f32[4,40,512]{2,1,0:T(8,128)} %maximum_maximum_fusion), calls=%async_computation.1 | async-start | bytes 655360 | tf_op jit(solution)/shard_map/all_to_all | solution.py:125
  27.1 5.6 %all-to-all-done.1 = f32[4,40,512]{2,1,0:T(8,128)S(1)} async-done(((f32[4,40,512]{2,1,0:T(8,128)}), f32[4,40,512]{2,1,0:T(8,128)S(1)}, u32[]{:S(2)}, u32[]{:S(2)}) %all-to-all-start.1) | async-done | bytes 327712 | tf_op jit(solution)/shard_map/all_to_all | solution.py:125
  32.7 0.1 reshape_squeeze.2
  32.8 0.1 copy.43
  33.0 0.2 mul.85
  33.2 0.1 mul.86
  33.3 0.1 copy.46
  33.4 0.1 copy.47
  33.5 0.1 mul.88
  33.6 0.1 mul.93
  33.7 3.0 %convolution_convert_fusion = bf16[32,4096]{1,0:T(8,128)(2,1)S(1)} fusion(bf16[512,4096]{1,0:T(8,128)(2,1)} %param.17, f32[4,8,4,128]{3,2,1,0:T(4,128)S(1)} %bitcast.151, f32[32,512]{1,0:T(8,128)S(1)} %fusion.11, f32[4,8,4,128]{3,2,1,0:T(4,128)S(1)} %bitcast.150, f32[4,8,4,128]{3,2,1,0:T(4,128)S(1)} %bitcast.152), kind=kOutput, calls=%fused_computation.3 | convolution fusion | flops 134414336 | bytes 4718592 | tf_op jit(solution)/shard_map/dot_general | solution.py:164
  36.7 0.7 %copy.75 = bf16[4,8,8,512]{3,2,0,1:T(8,128)(2,1)} copy(bf16[4,8,8,512]{3,2,1,0:T(8,128)(2,1)S(1)} %bitcast.149) | data formatting | bytes 524288 | tf_op jit(solution)/shard_map/reshape | solution.py:167
  37.4 10.2 %all-to-all-start.2 = ((bf16[8,512,32]{1,2,0:T(8,128)(2,1)}), bf16[8,512,32]{1,2,0:T(8,128)(2,1)S(1)}, u32[]{:S(2)}, u32[]{:S(2)}) async-start(bf16[8,512,32]{1,2,0:T(8,128)(2,1)} %bitcast.148), calls=%async_computation.2 | async-start | bytes 524288 | tf_op jit(solution)/shard_map/all_to_all | solution.py:168
  47.8 0.1 lt.95
  47.9 0.8 %scatter_custom_fusion = bf16[576,128]{1,0:T(8,128)(2,1)S(1)} fusion(bf16[576,128]{1,0:T(8,128)(2,1)S(1)} %copy.86, s32[32]{0:T(128)S(1)} %fusion.48, bf16[32,256]{1,0:T(8,128)(2,1)S(1)} %convert_element_type.60), kind=kCustom, calls=%fused_computation.61 | custom fusion | bytes 155648 | tf_op jit(solution)/shard_map/scatter | solution.py:178
  48.7 0.8 %scatter_custom_fusion.1 = bf16[576,128]{1,0:T(8,128)(2,1)S(1)} fusion(bf16[576,128]{1,0:T(8,128)(2,1)S(1)} %copy.87, s32[32]{0:T(128)S(1)} %fusion.48, bf16[32,256]{1,0:T(8,128)(2,1)S(1)} %convert_element_type.60), kind=kCustom, calls=%fused_computation.59 | custom fusion | bytes 155648 | tf_op jit(solution)/shard_map/scatter | solution.py:179
  49.5 4.6 %all-to-all-done.2 = bf16[8,512,32]{1,2,0:T(8,128)(2,1)S(1)} async-done(((bf16[8,512,32]{1,2,0:T(8,128)(2,1)}), bf16[8,512,32]{1,2,0:T(8,128)(2,1)S(1)}, u32[]{:S(2)}, u32[]{:S(2)}) %all-to-all-start.2) | async-done | bytes 262176 | tf_op jit(solution)/shard_map/all_to_all | solution.py:168
  54.2 0.6 %fusion.23 = bf16[1,32,512]{2,1,0:T(8,128)(2,1)} fusion(f32[512,32]{0,1:T(8,128)S(1)} %convert_reduce_fusion, bf16[1,32,512]{2,1,0:T(8,128)(2,1)S(1)} %copy-done.4), kind=kLoop, calls=%fused_computation.45 | loop fusion | flops 49152 | bytes 131072 | tf_op jit(solution)/shard_map/broadcast_in_dim | solution.py:170
  (48 shorter events, 1.1 us)
Async XLA Ops:
  0.6 18.9 %copy-start.2 = (bf16[1,32,128]{2,1,0:T(8,128)(2,1)S(1)}, bf16[1,32,128]{2,1,0:T(8,128)(2,1)}, u32[]{:S(2)}) copy-start(bf16[1,32,128]{2,1,0:T(8,128)(2,1)} %param.12) | copy-start | bytes 24580
  0.6 19.1 %copy-start.3 = (bf16[1,32,128]{2,1,0:T(8,128)(2,1)S(1)}, bf16[1,32,128]{2,1,0:T(8,128)(2,1)}, u32[]{:S(2)}) copy-start(bf16[1,32,128]{2,1,0:T(8,128)(2,1)} %param.13) | copy-start | bytes 24580
  0.7 18.6 %copy-start.5 = (s32[64]{0:T(128)S(1)}, s32[64]{0:T(128)}, u32[]{:S(2)}) copy-start(s32[64]{0:T(128)} %param.18) | copy-start | bytes 772
  0.7 17.8 %copy-start.7 = (s32[1,32]{1,0:T(1,128)S(1)}, s32[1,32]{1,0:T(1,128)}, u32[]{:S(2)}) copy-start(s32[1,32]{1,0:T(1,128)} %param.19) | copy-start | bytes 388
  0.7 16.9 %copy-start.6 = (s32[1,8]{1,0:T(1,128)S(1)}, s32[1,8]{1,0:T(1,128)}, u32[]{:S(2)}) copy-start(s32[1,8]{1,0:T(1,128)} %param.20) | copy-start | bytes 100
  7.6 12.3 %all-to-all-start = ((bf16[4,32,512]{2,1,0:T(8,128)(2,1)}), bf16[4,32,512]{2,1,0:T(8,128)(2,1)S(1)}, u32[]{:S(2)}, u32[]{:S(2)}) async-start(bf16[4,32,512]{2,1,0:T(8,128)(2,1)} %shard_map.130), calls=%async_computation | async-start | bytes 262144 | tf_op jit(solution)/shard_map/all_to_all | solution.py:90
  21.4 5.5 %copy-start.8 = (s32[64]{0:T(128)S(1)}, s32[64]{0:T(128)}, u32[]{:S(2)}) copy-start(s32[64]{0:T(128)} %param.21) | copy-start | bytes 772
  22.6 10.1 %all-to-all-start.1 = ((f32[4,40,512]{2,1,0:T(8,128)}), f32[4,40,512]{2,1,0:T(8,128)S(1)}, u32[]{:S(2)}, u32[]{:S(2)}) async-start(f32[4,40,512]{2,1,0:T(8,128)} %maximum_maximum_fusion), calls=%async_computation.1 | async-start | bytes 655360 | tf_op jit(solution)/shard_map/all_to_all | solution.py:125
  36.7 17.4 %copy-start.4 = (bf16[1,32,512]{2,1,0:T(8,128)(2,1)S(1)}, bf16[1,32,512]{2,1,0:T(8,128)(2,1)}, u32[]{:S(2)}) copy-start(bf16[1,32,512]{2,1,0:T(8,128)(2,1)} %param.16) | copy-start | bytes 98308
  37.4 16.7 %all-to-all-start.2 = ((bf16[8,512,32]{1,2,0:T(8,128)(2,1)}), bf16[8,512,32]{1,2,0:T(8,128)(2,1)S(1)}, u32[]{:S(2)}, u32[]{:S(2)}) async-start(bf16[8,512,32]{1,2,0:T(8,128)(2,1)} %bitcast.148), calls=%async_computation.2 | async-start | bytes 524288 | tf_op jit(solution)/shard_map/all_to_all | solution.py:168
  48.7 6.1 %copy-start = (bf16[576,128]{1,0:T(8,128)(2,1)}, bf16[576,128]{1,0:T(8,128)(2,1)S(1)}, u32[]{:S(2)}) copy-start(bf16[576,128]{1,0:T(8,128)(2,1)S(1)} %scatter_custom_fusion) | copy-start | bytes 442372
  49.4 5.3 %copy-start.1 = (bf16[576,128]{1,0:T(8,128)(2,1)}, bf16[576,128]{1,0:T(8,128)(2,1)S(1)}, u32[]{:S(2)}) copy-start(bf16[576,128]{1,0:T(8,128)(2,1)S(1)} %scatter_custom_fusion.1) | copy-start | bytes 442372

commit v7 on v5

--- a/solution.py
+++ b/solution.py
@@ -124,6 +124,7 @@
     )
     valid = inside[:, None, None, None, :]
     top_score = jnp.max(jnp.where(valid, scores, NEG), axis=-1)
+    top_score = top_score.astype(jnp.bfloat16).astype(jnp.float32)
     raised = jnp.where(valid, jnp.exp(scores - top_score[..., None]), 0.0)
     total = jnp.sum(raised, axis=-1)
     summed = jnp.einsum(
@@ -134,21 +135,25 @@
     )
     stats = jnp.concatenate(
         [top_score.reshape(GROUP, 1, -1), total.reshape(GROUP, 1, -1)], axis=-1
-    )
+    ).astype(jnp.bfloat16)
     stats = jnp.pad(stats, ((0, 0), (0, 0), (0, q_width - stats.shape[-1])))
     tree_pair = jnp.concatenate([tree_keys[0], tree_values[0]], axis=-1)
-    mine_rows = jnp.take(tree_pair, accept_rows[0], axis=0).astype(jnp.float32)
+    mine_rows = jnp.take(tree_pair, accept_rows[0], axis=0)
     row_lines = mine_rows.reshape(1, -1, q_width)
     row_count = row_lines.shape[1]
     row_lines = jnp.broadcast_to(row_lines, (GROUP,) + row_lines.shape[1:])
     used = TREE + 1 + row_count
-    filler = jnp.zeros((GROUP, -used % 8, q_width), jnp.float32)
+    filler = jnp.zeros((GROUP, -used % 16, q_width), jnp.bfloat16)
     message = jnp.concatenate(
-        [summed.reshape(GROUP, TREE, q_width), stats, row_lines, filler], axis=1
+        [summed.reshape(GROUP, TREE, q_width).astype(jnp.bfloat16), stats, row_lines, filler],
+        axis=1,
+    )
+    message, queries, tree_keys, tree_values, parents = lax.optimization_barrier(
+        (message, queries, tree_keys, tree_values, parents)
     )
     partials = lax.all_to_all(message, "mem", 0, 0, tiled=True)
     row_block = partials[:, TREE + 1 : used].reshape(GROUP, A_MAX, 2 * channels)
-    row_block = row_block.astype(jnp.bfloat16)
+    partials = partials.astype(jnp.float32)
     part_out = partials[:, :TREE]
     stat_count = kv_local * sharing * TREE
     part_stats = partials[:, TREE, : 2 * stat_count].reshape(GROUP, 2, heads_local, TREE)

time: 52.7 us -> 52 us (0.987)
  other arithmetic: 6.57 us -> 7.88 us
  waiting for transfers between devices: 10.3 us -> 9.34 us
  local copies, waits for them, and re-layouts: 8.89 us -> 7.95 us
    all_to_all x1, waiting for transfers between devices: 5.63 us -> 4.69 us  [on_device(): partials = lax.all_to_all(message, 'mem', 0, 0, tiled=True)]
    another operation x2 -> x3, local copies, waits for them, and re-layouts: 0.87 us -> 0.12 us
    unnamed x1, other arithmetic: 0.66 us -> 1.32 us
    add x1, other arithmetic: 0.08 us -> 0.73 us  [on_device(): begin + length]
    unnamed x21 -> x19, local copies, waits for them, and re-layouts: 2.41 us -> 2.38 us
where the time goes in v7:
time: 52 us; the launch traced here: 51.4 us
  starting transfers between devices  19.4 us (37%)
  waiting for transfers between devices  9.34 us (18%)
  local copies, waits for them, and re-layouts  7.95 us (15%)
  other arithmetic  7.88 us (15%)
  Pallas kernels  3.94 us (8%)
  matrix products  1.96 us (4%)
  between operations  0.88 us (2%)
    all_to_all x1, starting transfers between devices, on_device(): pieces = lax.all_to_all(pieces, 'tp', 0, 0, tiled=True)  10.2 us
    all_to_all x1, starting transfers between devices, on_device(): gathered_q = lax.all_to_all(sent, 'mem', 0, 0, tiled=True)  5 us
    all_to_all x1, waiting for transfers between devices, on_device(): partials = lax.all_to_all(message, 'mem', 0, 0, tiled=True)  4.69 us
    all_to_all x1, waiting for transfers between devices, on_device(): pieces = lax.all_to_all(pieces, 'tp', 0, 0, tiled=True)  4.65 us
    all_to_all x1, starting transfers between devices, on_device(): partials = lax.all_to_all(message, 'mem', 0, 0, tiled=True)  4.25 us
    pallas_call x1, Pallas kernels, project(): pl.pallas_call(project_kernel, in_specs=[pl.BlockSpec(memory_space=pltpu....  3.94 us
    unnamed x19, local copies, waits for them, and re-layouts  2.38 us
    broadcast_in_dim x1, local copies, waits for them, and re-layouts, on_device(): sent = jnp.broadcast_to(queries, (GROUP,) + queries.shape[1:])  1.42 us
  transfers between devices with their start and end apart: 3, of which 2 were waited for; matrix products, arithmetic and copies ran while one was open for 18% of the time, Pallas kernels for 0%

profile of v7, /device:TPU:1, one launch (start us, length us, event | category | flops | bytes accessed | tf_op | source)
XLA Modules:
  0.0 51.4 jit_solution(14598652359939285806)
XLA Ops:
  0.6 0.9 %copy.82 = bf16[576,128]{1,0:T(8,128)(2,1)S(1)} copy(bf16[576,128]{1,0:T(8,128)(2,1)} %param.14) | data formatting | bytes 294912
  1.6 0.9 %copy.83 = bf16[576,128]{1,0:T(8,128)(2,1)S(1)} copy(bf16[576,128]{1,0:T(8,128)(2,1)} %param.15) | data formatting | bytes 294912
  2.5 1.4 %broadcast_in_dim.83 = bf16[4,32,512]{2,1,0:T(8,128)(2,1)} broadcast(bf16[32,512]{1,0:T(8,128)(2,1)} %bitcast.139), dimensions={1,2} | broadcast | bytes 163840 | tf_op jit(solution)/shard_map/broadcast_in_dim | solution.py:113
  3.9 5.0 %all-to-all-start = ((bf16[4,32,512]{2,1,0:T(8,128)(2,1)}), bf16[4,32,512]{2,1,0:T(8,128)(2,1)S(1)}, u32[]{:S(2)}, u32[]{:S(2)}) async-start(bf16[4,32,512]{2,1,0:T(8,128)(2,1)} %broadcast_in_dim.83), calls=%async_computation | async-start | bytes 262144 | tf_op jit(solution)/shard_map/all_to_all | solution.py:114
  8.9 0.7 %add_bitcast_fusion = s32[64,1]{0,1:T(1,128)S(1)} fusion(s32[64]{0:T(128)} %param.18), kind=kLoop, calls=%fused_computation.92 | loop fusion | flops 64 | bytes 512 | tf_op jit(solution)/shard_map/reshape.323
  9.5 0.1 copy.37
  9.6 0.1 reduce-window.9
  9.7 0.1 reduce.4
  9.9 0.7 %add_subtract_fusion.1 = s32[64]{0:T(128)S(1)} fusion(s32[64]{0:T(128)S(1)} %reduce.4, s32[64]{0:T(128)} %param.18), kind=kLoop, calls=%fused_computation.91 | loop fusion | flops 128 | bytes 768 | tf_op jit(solution)/shard_map/sub | solution.py:107
  10.5 0.7 %fusion.46 = s32[8]{0:T(128)S(1)} fusion(s32[1,8]{1,0:T(1,128)} %param.20), kind=kLoop, calls=%fused_computation.88 | loop fusion | flops 24 | bytes 64 | tf_op jit(solution)/shard_map/jit(_take)/jit(_where)/select_n | solution.py:141
  11.2 0.7 %pad_maximum_fusion = bf16[32,256]{1,0:T(8,128)(2,1)S(1)} fusion(bf16[32,128]{1,0:T(8,128)(2,1)} %bitcast.141, bf16[32,128]{1,0:T(8,128)(2,1)} %bitcast.140), kind=kLoop, calls=%fused_computation.50 | loop fusion | flops 32768 | bytes 32768 | tf_op jit(solution)/shard_map/concatenate | solution.py:140
  11.9 0.6 %gather_fusion = bf16[8,256]{1,0:T(8,128)(2,1)S(1)} fusion(bf16[32,256]{1,0:T(8,128)(2,1)S(1)} %pad_maximum_fusion, s32[1024]{0:T(1024)S(1)} %pad_clamp_fusion), kind=kCustom, calls=%fused_computation | custom fusion | bytes 8224 | tf_op jit(solution)/shard_map/jit(_take)/gather | solution.py:141
  12.5 0.5 broadcast.186
  13.0 1.3 %reduce.10 = s32[8]{0:T(128)S(1)} reduce(s32[1,8]{1,0:T(1,128)} %param.20, s32[]{:T(128)} %broadcast.186), dimensions={0}, to_apply=%param.20.reduce_sub_computation.3 | reduce | bytes 68 | tf_op args[9]
  14.3 0.1 squeeze.18
  14.4 0.1 copy.42
  14.5 0.7 %dynamic-slice_add_fusion = (s32[4]{0:T(128)S(1)}, s32[4]{0:T(128)S(1)}) fusion(s32[64]{0:T(128)} %param.18, s32[]{:T(128)S(6)} %select_n.67, s32[64]{0:T(128)S(1)} %add_subtract_fusion.1), kind=kLoop, calls=%fused_computation.90 | loop fusion | flops 4 | bytes 68 | tf_op jit(solution)/shard_map/add | solution.py:119
  15.7 0.4 select_reduce_fusion
  16.1 0.1 concatenate.27
  16.2 0.4 fusion.5
  16.6 0.1 concatenate.28
  16.7 0.4 fusion.1
  17.4 0.8 %maximum_maximum_fusion = bf16[4,48,512]{2,1,0:T(8,128)(2,1)} fusion(bf16[4,4,512]{2,1,0:T(4,128)(2,1)S(1)} %broadcast_in_dim.89, bf16[4,1,512]{2,1,0:T(2,128)(2,1)S(1)} %fusion.30, bf16[4,32,512]{2,1,0:T(8,128)(2,1)S(1)} %convert_element_type.101, bf16[48]{0:T(256)(128)(2,1)S(1)} %pad.8.clone), kind=kLoop, calls=%fused_computation.28 | loop fusion | flops 786432 | bytes 348256 | tf_op jit(solution)/shard_map/concatenate | solution.py:147
  18.2 0.2 convolution_compare_fusion.4
  18.3 0.2 convolution_compare_fusion.2
  18.6 0.2 fusion.4
  18.8 0.1 copy.44
  18.9 4.3 %all-to-all-start.1 = ((bf16[4,48,512]{2,1,0:T(8,128)(2,1)}), bf16[4,48,512]{2,1,0:T(8,128)(2,1)S(1)}, u32[]{:S(2)}, u32[]{:S(2)}) async-start(bf16[4,48,512]{2,1,0:T(8,128)(2,1)} %maximum_maximum_fusion), calls=%async_computation.1 | async-start | bytes 393216 | tf_op jit(solution)/shard_map/all_to_all | solution.py:154
  23.2 0.2 select_reduce_fusion.1
  23.4 0.2 convolution_bitcast_fusion
  23.7 4.7 %all-to-all-done.1 = bf16[4,48,512]{2,1,0:T(8,128)(2,1)S(1)} async-done(((bf16[4,48,512]{2,1,0:T(8,128)(2,1)}), bf16[4,48,512]{2,1,0:T(8,128)(2,1)S(1)}, u32[]{:S(2)}, u32[]{:S(2)}) %all-to-all-start.1) | async-done | bytes 196640 | tf_op jit(solution)/shard_map/all_to_all | solution.py:154
  28.4 0.1 reshape_squeeze.2
  28.6 0.1 copy.46
  28.7 0.2 mul.85
  28.9 0.1 mul.86
  29.1 0.1 copy.49
  29.1 0.1 copy.50
  29.2 0.1 mul.88
  29.3 0.1 mul.93
  29.4 0.6 %fusion.17.attention_ref = bf16[32,512]{1,0:T(8,128)(2,1)} fusion(f32[4,8,4,128]{3,2,1,0:T(4,128)S(1)} %bitcast.137, f32[32,512]{1,0:T(8,128)S(1)} %fusion.12, f32[4,8,4,128]{3,2,1,0:T(4,128)S(1)} %bitcast.136, f32[4,8,4,128]{3,2,1,0:T(4,128)S(1)} %bitcast.138), kind=kLoop, calls=%fused_computation.34 | loop fusion | flops 65536 | bytes 294912 | tf_op jit(solution)/shard_map/convert_element_type | solution.py:190
  30.1 3.9 %shard_map.130 = bf16[8,32,512]{2,1,0:T(8,128)(2,1)} custom-call(bf16[32,512]{1,0:T(8,128)(2,1)} %fusion.17.attention_ref, bf16[512,4096]{1,0:T(8,128)(2,1)} %weight_hbm.1), custom_call_target="tpu_custom_call" | custom-call | tf_op jit(solution)/shard_map/pallas_call | solution.py:65
  34.0 10.2 %all-to-all-start.2 = ((bf16[8,32,512]{2,1,0:T(8,128)(2,1)}), bf16[8,32,512]{2,1,0:T(8,128)(2,1)S(1)}, u32[]{:S(2)}, u32[]{:S(2)}) async-start(bf16[8,32,512]{2,1,0:T(8,128)(2,1)} %shard_map.130), calls=%async_computation.2 | async-start | bytes 524288 | tf_op jit(solution)/shard_map/all_to_all | solution.py:194
  44.3 0.1 sub.65
  44.4 0.1 lt.95
  44.5 0.8 %scatter_custom_fusion = bf16[576,128]{1,0:T(8,128)(2,1)S(1)} fusion(bf16[576,128]{1,0:T(8,128)(2,1)S(1)} %copy.82, s32[32]{0:T(128)S(1)} %fusion.47, bf16[32,256]{1,0:T(8,128)(2,1)S(1)} %reshape_reshape.7), kind=kCustom, calls=%fused_computation.58 | custom fusion | bytes 155648 | tf_op jit(solution)/shard_map/scatter | solution.py:204
  45.3 0.8 %scatter_custom_fusion.1 = bf16[576,128]{1,0:T(8,128)(2,1)S(1)} fusion(bf16[576,128]{1,0:T(8,128)(2,1)S(1)} %copy.83, s32[32]{0:T(128)S(1)} %fusion.47, bf16[32,256]{1,0:T(8,128)(2,1)S(1)} %reshape_reshape.7), kind=kCustom, calls=%fused_computation.56 | custom fusion | bytes 155648 | tf_op jit(solution)/shard_map/scatter | solution.py:205
  46.0 4.6 %all-to-all-done.2 = bf16[8,32,512]{2,1,0:T(8,128)(2,1)S(1)} async-done(((bf16[8,32,512]{2,1,0:T(8,128)(2,1)}), bf16[8,32,512]{2,1,0:T(8,128)(2,1)S(1)}, u32[]{:S(2)}, u32[]{:S(2)}) %all-to-all-start.2) | async-done | bytes 262176 | tf_op jit(solution)/shard_map/all_to_all | solution.py:194
  50.7 0.6 %fusion.19 = bf16[1,32,512]{2,1,0:T(8,128)(2,1)} fusion(f32[32,512]{1,0:T(8,128)S(1)} %convert_reduce_fusion, bf16[1,32,512]{2,1,0:T(8,128)(2,1)S(1)} %copy-done.5), kind=kLoop, calls=%fused_computation.38 | loop fusion | flops 49152 | bytes 131072 | tf_op jit(solution)/shard_map/convert_element_type | solution.py:196
  (48 shorter events, 1.0 us)
Async XLA Ops:
  0.6 14.9 %copy-start.6 = (s32[64]{0:T(128)S(1)}, s32[64]{0:T(128)}, u32[]{:S(2)}) copy-start(s32[64]{0:T(128)} %param.21) | copy-start | bytes 772
  3.9 11.8 %all-to-all-start = ((bf16[4,32,512]{2,1,0:T(8,128)(2,1)}), bf16[4,32,512]{2,1,0:T(8,128)(2,1)S(1)}, u32[]{:S(2)}, u32[]{:S(2)}) async-start(bf16[4,32,512]{2,1,0:T(8,128)(2,1)} %broadcast_in_dim.83), calls=%async_computation | async-start | bytes 262144 | tf_op jit(solution)/shard_map/all_to_all | solution.py:114
  16.7 1.4 %copy-start.2 = (bf16[1,32,512]{2,1,0:T(8,128)(2,1)S(1)}, bf16[1,32,512]{2,1,0:T(8,128)(2,1)}, u32[]{:S(2)}) copy-start(bf16[1,32,512]{2,1,0:T(8,128)(2,1)} %param.11) | copy-start | bytes 98308
  16.7 1.4 %copy-start.7 = (s32[1,32]{1,0:T(1,128)S(1)}, s32[1,32]{1,0:T(1,128)}, u32[]{:S(2)}) copy-start(s32[1,32]{1,0:T(1,128)} %param.19) | copy-start | bytes 388
  16.7 6.5 %copy-start.3 = (bf16[1,32,128]{2,1,0:T(8,128)(2,1)S(1)}, bf16[1,32,128]{2,1,0:T(8,128)(2,1)}, u32[]{:S(2)}) copy-start(bf16[1,32,128]{2,1,0:T(8,128)(2,1)} %param.12) | copy-start | bytes 24580
  16.7 6.7 %copy-start.4 = (bf16[1,32,128]{2,1,0:T(8,128)(2,1)S(1)}, bf16[1,32,128]{2,1,0:T(8,128)(2,1)}, u32[]{:S(2)}) copy-start(bf16[1,32,128]{2,1,0:T(8,128)(2,1)} %param.13) | copy-start | bytes 24580
  18.9 9.4 %all-to-all-start.1 = ((bf16[4,48,512]{2,1,0:T(8,128)(2,1)}), bf16[4,48,512]{2,1,0:T(8,128)(2,1)S(1)}, u32[]{:S(2)}, u32[]{:S(2)}) async-start(bf16[4,48,512]{2,1,0:T(8,128)(2,1)} %maximum_maximum_fusion), calls=%async_computation.1 | async-start | bytes 393216 | tf_op jit(solution)/shard_map/all_to_all | solution.py:154
  30.1 20.7 %copy-start.5 = (bf16[1,32,512]{2,1,0:T(8,128)(2,1)S(1)}, bf16[1,32,512]{2,1,0:T(8,128)(2,1)}, u32[]{:S(2)}) copy-start(bf16[1,32,512]{2,1,0:T(8,128)(2,1)} %param.16) | copy-start | bytes 98308
  34.0 16.7 %all-to-all-start.2 = ((bf16[8,32,512]{2,1,0:T(8,128)(2,1)}), bf16[8,32,512]{2,1,0:T(8,128)(2,1)S(1)}, u32[]{:S(2)}, u32[]{:S(2)}) async-start(bf16[8,32,512]{2,1,0:T(8,128)(2,1)} %shard_map.130), calls=%async_computation.2 | async-start | bytes 524288 | tf_op jit(solution)/shard_map/all_to_all | solution.py:194
  45.3 6.1 %copy-start = (bf16[576,128]{1,0:T(8,128)(2,1)}, bf16[576,128]{1,0:T(8,128)(2,1)S(1)}, u32[]{:S(2)}) copy-start(bf16[576,128]{1,0:T(8,128)(2,1)S(1)} %scatter_custom_fusion) | copy-start | bytes 442372
  46.0 5.3 %copy-start.1 = (bf16[576,128]{1,0:T(8,128)(2,1)}, bf16[576,128]{1,0:T(8,128)(2,1)S(1)}, u32[]{:S(2)}) copy-start(bf16[576,128]{1,0:T(8,128)(2,1)S(1)} %scatter_custom_fusion.1) | copy-start | bytes 442372

commit v8 on v7

--- a/solution.py
+++ b/solution.py
@@ -107,10 +107,11 @@
     starts = jnp.cumsum(regions) - regions
     low_edge = seq_rank * positions
     places = low_edge + jnp.arange(positions, dtype=jnp.int32)
+
+    sent = jnp.broadcast_to(queries, (GROUP,) + queries.shape[1:])
+    sent, cache_keys, cache_values = lax.optimization_barrier((sent, cache_keys, cache_values))
     keys_local = cache_keys.reshape(positions, kv_local, HD)
     values_local = cache_values.reshape(positions, kv_local, HD)
-
-    sent = jnp.broadcast_to(queries, (GROUP,) + queries.shape[1:])
     gathered_q = lax.all_to_all(sent, "mem", 0, 0, tiled=True)
 
     group_base = seq_rank - member
@@ -190,10 +191,13 @@
     attention = scale_heads(joint_out, 1.0 / joint_total).astype(jnp.bfloat16)
 
     tp_size = lax.axis_size("tp")
-    pieces = project(attention, out_weight, tp_size)
+    projected = lax.dot_general(
+        out_weight, attention, (((0,), (1,)), ((), ())), preferred_element_type=jnp.float32
+    ).astype(jnp.bfloat16)
+    pieces = projected.reshape(tp_size, -1, TREE)
     pieces = lax.all_to_all(pieces, "tp", 0, 0, tiled=True)
     summed_heads = jnp.sum(pieces.astype(jnp.float32), axis=0)
-    mixed = (residual[0].astype(jnp.float32) + summed_heads).astype(jnp.bfloat16)[None]
+    mixed = (residual[0].astype(jnp.float32) + summed_heads.T).astype(jnp.bfloat16)[None]
 
     row_accepted = lax.dynamic_slice_in_dim(accept_len, group_base, GROUP)
     column = jnp.arange(A_MAX, dtype=jnp.int32)

time: 52 us -> 51.1 us (0.983)
  Pallas kernels: 3.94 us -> 0 us
  matrix products: 1.96 us -> 4.95 us
  local copies, waits for them, and re-layouts: 7.95 us -> 8.67 us
  other arithmetic: 7.88 us -> 7.24 us
    pallas_call x1 -> x0, Pallas kernels: 3.94 us -> none  [project(): pl.pallas_call(project_kernel, in_specs=[pl.BlockSpec(memory_space=pltpu....]
    dot_general x0 -> x1, matrix products: none -> 3 us  [on_device(): lax.dot_general(out_weight, attention, (((0,), (1,)), ((), ())), preferre...]
    optimization_barrier x0 -> x2, local copies, waits for them, and re-layouts: none -> 1.83 us  [on_device(): lax.optimization_barrier((sent, cache_keys, cache_values))]
    unnamed x19 -> x17, local copies, waits for them, and re-layouts: 2.38 us -> 0.56 us
    convert_element_type x2 -> x0, other arithmetic: 1.26 us -> none  [the longest x1 0.64 us: on_device(): attention = scale_heads(joint_out, 1.0 / joint_total).astype(jnp.bfloat16)]
    reshape x0 -> x1, local copies, waits for them, and re-layouts: none -> 0.72 us  [on_device(): pieces = projected.reshape(tp_size, -1, TREE)]
    broadcast_in_dim x0 -> x1, other arithmetic: none -> 0.62 us  [on_device(): (residual[0].astype(jnp.float32) + summed_heads.T).astype(jnp.bfloat16)]
where the time goes in v8:
time: 51.1 us; the launch traced here: 50.5 us
  starting transfers between devices  19.4 us (38%)
  waiting for transfers between devices  9.34 us (18%)
  local copies, waits for them, and re-layouts  8.67 us (17%)
  other arithmetic  7.24 us (14%)
  matrix products  4.95 us (10%)
  between operations  0.88 us (2%)
    all_to_all x1, starting transfers between devices, on_device(): pieces = lax.all_to_all(pieces, 'tp', 0, 0, tiled=True)  10.2 us
    all_to_all x1, starting transfers between devices, on_device(): gathered_q = lax.all_to_all(sent, 'mem', 0, 0, tiled=True)  5 us
    all_to_all x1, waiting for transfers between devices, on_device(): partials = lax.all_to_all(message, 'mem', 0, 0, tiled=True)  4.69 us
    all_to_all x1, waiting for transfers between devices, on_device(): pieces = lax.all_to_all(pieces, 'tp', 0, 0, tiled=True)  4.65 us
    all_to_all x1, starting transfers between devices, on_device(): partials = lax.all_to_all(message, 'mem', 0, 0, tiled=True)  4.25 us
    dot_general x1, matrix products, on_device(): lax.dot_general(out_weight, attention, (((0,), (1,)), ((), ())), preferre...  3 us
    optimization_barrier x2, local copies, waits for them, and re-layouts, on_device(): lax.optimization_barrier((sent, cache_keys, cache_values))  1.83 us
    broadcast_in_dim x1, local copies, waits for them, and re-layouts, on_device(): sent = jnp.broadcast_to(queries, (GROUP,) + queries.shape[1:])  1.42 us
  transfers between devices with their start and end apart: 3, of which 2 were waited for; matrix products, arithmetic and copies ran while one was open for 18% of the time, Pallas kernels for 0%

profile of v8, /device:TPU:1, one launch (start us, length us, event | category | flops | bytes accessed | tf_op | source)
XLA Modules:
  0.0 50.5 jit_solution(1446722743770838679)
XLA Ops:
  0.6 0.9 %copy.102 = bf16[576,128]{1,0:T(8,128)(2,1)S(1)} copy(bf16[576,128]{1,0:T(8,128)(2,1)} %param.14) | data formatting | bytes 294912 | tf_op jit(solution)/shard_map/optimization_barrier | solution.py:112
  1.6 0.9 %copy.103 = bf16[576,128]{1,0:T(8,128)(2,1)S(1)} copy(bf16[576,128]{1,0:T(8,128)(2,1)} %param.15) | data formatting | bytes 294912 | tf_op jit(solution)/shard_map/optimization_barrier | solution.py:112
  2.5 1.4 %broadcast_in_dim.84 = bf16[4,32,512]{2,1,0:T(8,128)(2,1)} broadcast(bf16[32,512]{1,0:T(8,128)(2,1)} %bitcast.152), dimensions={1,2} | broadcast | bytes 163840 | tf_op jit(solution)/shard_map/broadcast_in_dim | solution.py:111
  3.9 5.0 %all-to-all-start = ((bf16[4,32,512]{2,1,0:T(8,128)(2,1)}), bf16[4,32,512]{2,1,0:T(8,128)(2,1)S(1)}, u32[]{:S(2)}, u32[]{:S(2)}) async-start(bf16[4,32,512]{2,1,0:T(8,128)(2,1)} %broadcast_in_dim.84), calls=%async_computation | async-start | bytes 262144 | tf_op jit(solution)/shard_map/all_to_all | solution.py:115
  8.9 0.7 %add_bitcast_fusion = s32[64,1]{0,1:T(1,128)S(1)} fusion(s32[64]{0:T(128)} %param.18), kind=kLoop, calls=%fused_computation.95 | loop fusion | flops 64 | bytes 512 | tf_op jit(solution)/shard_map/reshape.323
  9.5 0.1 copy.50
  9.6 0.1 reduce-window.9
  9.7 0.1 reduce.4
  9.9 0.7 %add_subtract_fusion.1 = s32[64]{0:T(128)S(1)} fusion(s32[64]{0:T(128)S(1)} %reduce.4, s32[64]{0:T(128)} %param.18), kind=kLoop, calls=%fused_computation.94 | loop fusion | flops 128 | bytes 768 | tf_op jit(solution)/shard_map/sub | solution.py:107
  10.5 0.7 %fusion.48 = s32[8]{0:T(128)S(1)} fusion(s32[1,8]{1,0:T(1,128)} %param.20), kind=kLoop, calls=%fused_computation.91 | loop fusion | flops 24 | bytes 64 | tf_op jit(solution)/shard_map/jit(_take)/jit(_where)/select_n | solution.py:142
  11.2 0.7 %pad_maximum_fusion = bf16[32,256]{1,0:T(8,128)(2,1)S(1)} fusion(bf16[32,128]{1,0:T(8,128)(2,1)} %bitcast.154, bf16[32,128]{1,0:T(8,128)(2,1)} %bitcast.153), kind=kLoop, calls=%fused_computation.53 | loop fusion | flops 32768 | bytes 32768 | tf_op jit(solution)/shard_map/concatenate | solution.py:141
  11.9 0.6 %gather_fusion = bf16[8,256]{1,0:T(8,128)(2,1)S(1)} fusion(bf16[32,256]{1,0:T(8,128)(2,1)S(1)} %pad_maximum_fusion, s32[1024]{0:T(1024)S(1)} %pad_clamp_fusion), kind=kCustom, calls=%fused_computation | custom fusion | bytes 8224 | tf_op jit(solution)/shard_map/jit(_take)/gather | solution.py:142
  12.5 0.5 %broadcast.186 = s32[]{:T(128)} broadcast(s32[]{:T(128)} %constant.13.clone.1), dimensions={} | broadcast | bytes 8 | tf_op args[9]
  13.0 1.3 %reduce.10 = s32[8]{0:T(128)S(1)} reduce(s32[1,8]{1,0:T(1,128)} %param.20, s32[]{:T(128)} %broadcast.186), dimensions={0}, to_apply=%param.20.reduce_sub_computation.3 | reduce | bytes 68 | tf_op args[9]
  14.3 0.1 squeeze.18
  14.4 0.1 copy.55
  14.5 0.7 %dynamic-slice_add_fusion = (s32[4]{0:T(128)S(1)}, s32[4]{0:T(128)S(1)}) fusion(s32[64]{0:T(128)} %param.18, s32[]{:T(128)S(6)} %select_n.67, s32[64]{0:T(128)S(1)} %add_subtract_fusion.1), kind=kLoop, calls=%fused_computation.93 | loop fusion | flops 4 | bytes 68 | tf_op jit(solution)/shard_map/add | solution.py:120
  15.7 0.4 select_reduce_fusion
  16.1 0.1 concatenate.27
  16.2 0.4 fusion.5
  16.6 0.1 concatenate.28
  16.7 0.4 fusion.1
  17.3 0.8 %maximum_maximum_fusion = bf16[4,48,512]{2,1,0:T(8,128)(2,1)} fusion(bf16[4,4,512]{2,1,0:T(4,128)(2,1)S(1)} %broadcast_in_dim.91, bf16[4,1,512]{2,1,0:T(2,128)(2,1)S(1)} %fusion.32, bf16[4,32,512]{2,1,0:T(8,128)(2,1)S(1)} %convert_element_type.105, bf16[48]{0:T(256)(128)(2,1)S(1)} %pad.8.clone), kind=kLoop, calls=%fused_computation.30 | loop fusion | flops 786432 | bytes 348256 | tf_op jit(solution)/shard_map/concatenate | solution.py:148
  18.1 0.2 convolution_compare_fusion.4
  18.3 0.2 convolution_compare_fusion.2
  18.6 0.2 fusion.4
  18.8 0.1 copy.57
  18.9 4.2 %all-to-all-start.1 = ((bf16[4,48,512]{2,1,0:T(8,128)(2,1)}), bf16[4,48,512]{2,1,0:T(8,128)(2,1)S(1)}, u32[]{:S(2)}, u32[]{:S(2)}) async-start(bf16[4,48,512]{2,1,0:T(8,128)(2,1)} %maximum_maximum_fusion), calls=%async_computation.1 | async-start | bytes 393216 | tf_op jit(solution)/shard_map/all_to_all | solution.py:155
  23.2 0.2 select_reduce_fusion.1
  23.4 0.2 convolution_bitcast_fusion
  23.7 4.7 %all-to-all-done.1 = bf16[4,48,512]{2,1,0:T(8,128)(2,1)S(1)} async-done(((bf16[4,48,512]{2,1,0:T(8,128)(2,1)}), bf16[4,48,512]{2,1,0:T(8,128)(2,1)S(1)}, u32[]{:S(2)}, u32[]{:S(2)}) %all-to-all-start.1) | async-done | bytes 196640 | tf_op jit(solution)/shard_map/all_to_all | solution.py:155
  28.4 0.1 reshape_squeeze.2
  28.5 0.1 copy.59
  28.7 0.2 mul.85
  28.9 0.1 mul.86
  29.0 0.1 copy.62
  29.1 0.1 copy.63
  29.2 0.1 mul.88
  29.3 0.1 mul.93
  29.4 3.0 %convolution_convert_fusion = bf16[32,4096]{1,0:T(8,128)(2,1)S(1)} fusion(bf16[512,4096]{1,0:T(8,128)(2,1)} %param.17, f32[4,8,4,128]{3,2,1,0:T(4,128)S(1)} %bitcast.150, f32[32,512]{1,0:T(8,128)S(1)} %fusion.12, f32[4,8,4,128]{3,2,1,0:T(4,128)S(1)} %bitcast.149, f32[4,8,4,128]{3,2,1,0:T(4,128)S(1)} %bitcast.151), kind=kOutput, calls=%fused_computation.3 | convolution fusion | flops 134414336 | bytes 4718592 | tf_op jit(solution)/shard_map/dot_general | solution.py:194
  32.4 0.7 %copy.91 = bf16[4,8,8,512]{3,2,0,1:T(8,128)(2,1)} copy(bf16[4,8,8,512]{3,2,1,0:T(8,128)(2,1)S(1)} %bitcast.148) | data formatting | bytes 524288 | tf_op jit(solution)/shard_map/reshape | solution.py:197
  33.1 10.2 %all-to-all-start.2 = ((bf16[8,512,32]{1,2,0:T(8,128)(2,1)}), bf16[8,512,32]{1,2,0:T(8,128)(2,1)S(1)}, u32[]{:S(2)}, u32[]{:S(2)}) async-start(bf16[8,512,32]{1,2,0:T(8,128)(2,1)} %bitcast.147), calls=%async_computation.2 | async-start | bytes 524288 | tf_op jit(solution)/shard_map/all_to_all | solution.py:198
  43.4 0.1 sub.65
  43.5 0.1 lt.95
  43.6 0.8 %scatter_custom_fusion = bf16[576,128]{1,0:T(8,128)(2,1)S(1)} fusion(bf16[576,128]{1,0:T(8,128)(2,1)S(1)} %copy.102, s32[32]{0:T(128)S(1)} %fusion.49, bf16[32,256]{1,0:T(8,128)(2,1)S(1)} %reshape_reshape.7), kind=kCustom, calls=%fused_computation.61 | custom fusion | bytes 155648 | tf_op jit(solution)/shard_map/scatter | solution.py:208
  44.4 0.8 %scatter_custom_fusion.1 = bf16[576,128]{1,0:T(8,128)(2,1)S(1)} fusion(bf16[576,128]{1,0:T(8,128)(2,1)S(1)} %copy.103, s32[32]{0:T(128)S(1)} %fusion.49, bf16[32,256]{1,0:T(8,128)(2,1)S(1)} %reshape_reshape.7), kind=kCustom, calls=%fused_computation.59 | custom fusion | bytes 155648 | tf_op jit(solution)/shard_map/scatter | solution.py:209
  45.2 4.6 %all-to-all-done.2 = bf16[8,512,32]{1,2,0:T(8,128)(2,1)S(1)} async-done(((bf16[8,512,32]{1,2,0:T(8,128)(2,1)}), bf16[8,512,32]{1,2,0:T(8,128)(2,1)S(1)}, u32[]{:S(2)}, u32[]{:S(2)}) %all-to-all-start.2) | async-done | bytes 262176 | tf_op jit(solution)/shard_map/all_to_all | solution.py:198
  49.9 0.6 %fusion.24 = bf16[1,32,512]{2,1,0:T(8,128)(2,1)} fusion(f32[512,32]{0,1:T(8,128)S(1)} %convert_reduce_fusion, bf16[1,32,512]{2,1,0:T(8,128)(2,1)S(1)} %copy-done.5), kind=kLoop, calls=%fused_computation.46 | loop fusion | flops 49152 | bytes 131072 | tf_op jit(solution)/shard_map/broadcast_in_dim | solution.py:200
  (48 shorter events, 1.0 us)
Async XLA Ops:
  0.6 14.9 %copy-start.6 = (s32[64]{0:T(128)S(1)}, s32[64]{0:T(128)}, u32[]{:S(2)}) copy-start(s32[64]{0:T(128)} %param.21) | copy-start | bytes 772
  3.9 11.8 %all-to-all-start = ((bf16[4,32,512]{2,1,0:T(8,128)(2,1)}), bf16[4,32,512]{2,1,0:T(8,128)(2,1)S(1)}, u32[]{:S(2)}, u32[]{:S(2)}) async-start(bf16[4,32,512]{2,1,0:T(8,128)(2,1)} %broadcast_in_dim.84), calls=%async_computation | async-start | bytes 262144 | tf_op jit(solution)/shard_map/all_to_all | solution.py:115
  16.6 1.5 %copy-start.2 = (bf16[1,32,512]{2,1,0:T(8,128)(2,1)S(1)}, bf16[1,32,512]{2,1,0:T(8,128)(2,1)}, u32[]{:S(2)}) copy-start(bf16[1,32,512]{2,1,0:T(8,128)(2,1)} %param.11) | copy-start | bytes 98308
  16.7 1.4 %copy-start.7 = (s32[1,32]{1,0:T(1,128)S(1)}, s32[1,32]{1,0:T(1,128)}, u32[]{:S(2)}) copy-start(s32[1,32]{1,0:T(1,128)} %param.19) | copy-start | bytes 388
  16.7 6.5 %copy-start.3 = (bf16[1,32,128]{2,1,0:T(8,128)(2,1)S(1)}, bf16[1,32,128]{2,1,0:T(8,128)(2,1)}, u32[]{:S(2)}) copy-start(bf16[1,32,128]{2,1,0:T(8,128)(2,1)} %param.12) | copy-start | bytes 24580
  16.7 6.6 %copy-start.4 = (bf16[1,32,128]{2,1,0:T(8,128)(2,1)S(1)}, bf16[1,32,128]{2,1,0:T(8,128)(2,1)}, u32[]{:S(2)}) copy-start(bf16[1,32,128]{2,1,0:T(8,128)(2,1)} %param.13) | copy-start | bytes 24580
  18.9 9.4 %all-to-all-start.1 = ((bf16[4,48,512]{2,1,0:T(8,128)(2,1)}), bf16[4,48,512]{2,1,0:T(8,128)(2,1)S(1)}, u32[]{:S(2)}, u32[]{:S(2)}) async-start(bf16[4,48,512]{2,1,0:T(8,128)(2,1)} %maximum_maximum_fusion), calls=%async_computation.1 | async-start | bytes 393216 | tf_op jit(solution)/shard_map/all_to_all | solution.py:155
  32.4 17.4 %copy-start.5 = (bf16[1,32,512]{2,1,0:T(8,128)(2,1)S(1)}, bf16[1,32,512]{2,1,0:T(8,128)(2,1)}, u32[]{:S(2)}) copy-start(bf16[1,32,512]{2,1,0:T(8,128)(2,1)} %param.16) | copy-start | bytes 98308
  33.1 16.7 %all-to-all-start.2 = ((bf16[8,512,32]{1,2,0:T(8,128)(2,1)}), bf16[8,512,32]{1,2,0:T(8,128)(2,1)S(1)}, u32[]{:S(2)}, u32[]{:S(2)}) async-start(bf16[8,512,32]{1,2,0:T(8,128)(2,1)} %bitcast.147), calls=%async_computation.2 | async-start | bytes 524288 | tf_op jit(solution)/shard_map/all_to_all | solution.py:198
  44.4 6.1 %copy-start = (bf16[576,128]{1,0:T(8,128)(2,1)}, bf16[576,128]{1,0:T(8,128)(2,1)S(1)}, u32[]{:S(2)}) copy-start(bf16[576,128]{1,0:T(8,128)(2,1)S(1)} %scatter_custom_fusion) | copy-start | bytes 442372
  45.1 5.3 %copy-start.1 = (bf16[576,128]{1,0:T(8,128)(2,1)}, bf16[576,128]{1,0:T(8,128)(2,1)S(1)}, u32[]{:S(2)}) copy-start(bf16[576,128]{1,0:T(8,128)(2,1)S(1)} %scatter_custom_fusion.1) | copy-start | bytes 442372

commit v9 on v8

--- a/solution.py
+++ b/solution.py
@@ -75,6 +75,80 @@
             pltpu.SemaphoreType.DMA((CHUNKS,)),
         ],
     )(attention, weight)
+
+
+def attend_kernel(
+    bounds_ref, queries_ref, keys_hbm, values_hbm, extra_ref, out_ref, keys_vmem, values_vmem, landed
+):
+    keys_copy = pltpu.make_async_copy(keys_hbm, keys_vmem, landed.at[0])
+    values_copy = pltpu.make_async_copy(values_hbm, values_vmem, landed.at[1])
+    keys_copy.start()
+    values_copy.start()
+    count = out_ref.shape[0]
+    tree = queries_ref.shape[1]
+    heads = queries_ref.shape[2] // HD
+    positions = keys_vmem.shape[0]
+    factor = 1.0 / math.sqrt(HD)
+    place = lax.broadcasted_iota(jnp.int32, (tree, positions), 1)
+    lane = lax.broadcasted_iota(jnp.int32, (tree, HD), 1)
+    pick = (
+        lax.broadcasted_iota(jnp.int32, (16, HD), 0) == lax.broadcasted_iota(jnp.int32, (16, HD), 1)
+    ) & (lax.broadcasted_iota(jnp.int32, (16, HD), 0) < 2 * heads)
+    pick = pick.astype(jnp.bfloat16)
+    spare = jnp.zeros((out_ref.shape[2] - tree, HD), jnp.bfloat16)
+    keys_copy.wait()
+    values_copy.wait()
+    keys = keys_vmem[...]
+    values = values_vmem[...]
+    for request in range(count):
+        valid = (place >= bounds_ref[request]) & (place < bounds_ref[count + request])
+        stat = jnp.zeros((tree, HD), jnp.float32)
+        for head in range(heads):
+            rows = queries_ref[request, :, head * HD : (head + 1) * HD]
+            scores = (
+                lax.dot_general(
+                    rows, keys, (((1,), (1,)), ((), ())), preferred_element_type=jnp.float32
+                )
+                * factor
+            )
+            top = jnp.max(jnp.where(valid, scores, NEG), axis=1, keepdims=True)
+            top = top.astype(jnp.bfloat16).astype(jnp.float32)
+            raised = jnp.where(valid, jnp.exp(scores - top), 0.0)
+            total = jnp.sum(raised, axis=1, keepdims=True)
+            summed = jnp.dot(
+                raised.astype(jnp.bfloat16), values, preferred_element_type=jnp.float32
+            )
+            out_ref[request, 0:tree, head * HD : (head + 1) * HD] = summed.astype(out_ref.dtype)
+            stat = jnp.where(lane == head, top, stat)
+            total = total.astype(jnp.bfloat16).astype(jnp.float32)
+            stat = jnp.where(lane == heads + head, total, stat)
+        padded = jnp.concatenate([stat.astype(jnp.bfloat16), spare], axis=0)
+        placed = lax.dot_general(
+            pick, padded, (((1,), (1,)), ((), ())), preferred_element_type=jnp.float32
+        )
+        block = extra_ref[...].astype(jnp.float32) + placed
+        out_ref[request, tree : tree + 16, :] = block.astype(out_ref.dtype)
+
+
+def attend(bounds, queries, keys, values, extra):
+    count, tree, width = queries.shape
+    return pl.pallas_call(
+        attend_kernel,
+        in_specs=[
+            pl.BlockSpec(memory_space=pltpu.SMEM),
+            pl.BlockSpec(memory_space=pltpu.VMEM),
+            pl.BlockSpec(memory_space=pl.ANY),
+            pl.BlockSpec(memory_space=pl.ANY),
+            pl.BlockSpec(memory_space=pltpu.VMEM),
+        ],
+        out_specs=pl.BlockSpec(memory_space=pltpu.VMEM),
+        out_shape=jax.ShapeDtypeStruct((count, tree + 16, width), jnp.bfloat16),
+        scratch_shapes=[
+            pltpu.VMEM(keys.shape, keys.dtype),
+            pltpu.VMEM(values.shape, values.dtype),
+            pltpu.SemaphoreType.DMA((2,)),
+        ],
+    )(bounds, queries, keys, values, extra)
 
 
 def scale_heads(values, factors):
@@ -109,7 +183,6 @@
     places = low_edge + jnp.arange(positions, dtype=jnp.int32)
 
     sent = jnp.broadcast_to(queries, (GROUP,) + queries.shape[1:])
-    sent, cache_keys, cache_values = lax.optimization_barrier((sent, cache_keys, cache_values))
     keys_local = cache_keys.reshape(positions, kv_local, HD)
     values_local = cache_values.reshape(positions, kv_local, HD)
     gathered_q = lax.all_to_all(sent, "mem", 0, 0, tiled=True)
@@ -117,49 +190,24 @@
     group_base = seq_rank - member
     begin = lax.dynamic_slice_in_dim(starts, group_base, GROUP)
     length = lax.dynamic_slice_in_dim(cache_len, group_base, GROUP)
-    inside = (places[None, :] >= begin[:, None]) & (places[None, :] < (begin + length)[:, None])
-    shaped = gathered_q.reshape(GROUP, TREE, kv_local, sharing, HD)
-    scores = (
-        jnp.einsum("rtkgd,pkd->rkgtp", shaped, keys_local, preferred_element_type=jnp.float32)
-        * factor
-    )
-    valid = inside[:, None, None, None, :]
-    top_score = jnp.max(jnp.where(valid, scores, NEG), axis=-1)
-    top_score = top_score.astype(jnp.bfloat16).astype(jnp.float32)
-    raised = jnp.where(valid, jnp.exp(scores - top_score[..., None]), 0.0)
-    total = jnp.sum(raised, axis=-1)
-    summed = jnp.einsum(
-        "rkgtp,pkd->rtkgd",
-        raised.astype(jnp.bfloat16),
-        values_local,
-        preferred_element_type=jnp.float32,
-    )
-    stats = jnp.concatenate(
-        [top_score.reshape(GROUP, 1, -1), total.reshape(GROUP, 1, -1)], axis=-1
-    ).astype(jnp.bfloat16)
-    stats = jnp.pad(stats, ((0, 0), (0, 0), (0, q_width - stats.shape[-1])))
+    bounds = jnp.concatenate([begin - low_edge, begin + length - low_edge]).astype(jnp.int32)
     tree_pair = jnp.concatenate([tree_keys[0], tree_values[0]], axis=-1)
     mine_rows = jnp.take(tree_pair, accept_rows[0], axis=0)
-    row_lines = mine_rows.reshape(1, -1, q_width)
-    row_count = row_lines.shape[1]
-    row_lines = jnp.broadcast_to(row_lines, (GROUP,) + row_lines.shape[1:])
-    used = TREE + 1 + row_count
-    filler = jnp.zeros((GROUP, -used % 16, q_width), jnp.bfloat16)
-    message = jnp.concatenate(
-        [summed.reshape(GROUP, TREE, q_width).astype(jnp.bfloat16), stats, row_lines, filler],
-        axis=1,
-    )
+    row_lines = mine_rows.reshape(-1, q_width)
+    row_count = row_lines.shape[0]
+    extra = jnp.zeros((16, q_width), jnp.bfloat16)
+    extra = lax.dynamic_update_slice(extra, row_lines, (8, 0))
+    message = attend(bounds, gathered_q, cache_keys, cache_values, extra)
     message, queries, tree_keys, tree_values, parents = lax.optimization_barrier(
         (message, queries, tree_keys, tree_values, parents)
     )
     partials = lax.all_to_all(message, "mem", 0, 0, tiled=True)
-    row_block = partials[:, TREE + 1 : used].reshape(GROUP, A_MAX, 2 * channels)
+    row_block = partials[:, TREE + 8 : TREE + 8 + row_count].reshape(GROUP, A_MAX, 2 * channels)
     partials = partials.astype(jnp.float32)
     part_out = partials[:, :TREE]
-    stat_count = kv_local * sharing * TREE
-    part_stats = partials[:, TREE, : 2 * stat_count].reshape(GROUP, 2, heads_local, TREE)
-    part_top = jnp.transpose(part_stats[:, 0], (0, 2, 1))
-    part_total = jnp.transpose(part_stats[:, 1], (0, 2, 1))
+    part_stats = partials[:, TREE : TREE + 2 * heads_local, :TREE]
+    part_top = jnp.transpose(part_stats[:, :heads_local], (0, 2, 1))
+    part_total = jnp.transpose(part_stats[:, heads_local:], (0, 2, 1))
 
     linked = ancestry(parents[0])
     shaped_q = queries[0].reshape(TREE, kv_local, sharing, HD)

time: 51.1 us -> 60.6 us (1.19)
  Pallas kernels: 0 us -> 7.46 us
  local copies, waits for them, and re-layouts: 8.67 us -> 12.1 us
  waiting for transfers between devices: 9.34 us -> 7.15 us
  matrix products: 4.95 us -> 6.2 us
  other arithmetic: 7.24 us -> 6.62 us
    pallas_call x0 -> x1, Pallas kernels: none -> 7.46 us  [attend(): pl.pallas_call(attend_kernel, in_specs=[pl.BlockSpec(memory_space=pltpu.S...]
    unnamed x17 -> x15, local copies, waits for them, and re-layouts: 0.56 us -> 4.34 us
    all_to_all x1, waiting for transfers between devices: 4.69 us -> 2.52 us  [on_device(): partials = lax.all_to_all(message, 'mem', 0, 0, tiled=True)]
    optimization_barrier x2 -> x0, local copies, waits for them, and re-layouts: 1.83 us -> none  [on_device(): lax.optimization_barrier((sent, cache_keys, cache_values))]
    dot_general x2 -> x0, matrix products: 0.87 us -> none  [the longest x1 0.44 us: on_device(): jnp.einsum('rtkgd,pkd->rkgtp', shaped, keys_local, preferred_element_type...]
    add x2 -> x0, other arithmetic: 0.73 us -> none  [the longest x1 0.73 us: on_device(): begin + length]
    sub x0 -> x1, other arithmetic: none -> 0.73 us  [on_device(): begin + length - low_edge]
    dot_general x3, matrix products: 0.69 us -> 1.42 us  [ancestry(): jnp.dot(reach, reach, preferred_element_type=jnp.float32) > 0]
  transfers between devices with their start and end apart: 3 -> 3, of which waited for: 2 -> 2; matrix products, arithmetic and copies ran while one was open for 18% -> 22% of each run, Pallas kernels for 0% -> 0%
where the time goes in v9:
time: 60.6 us; the launch traced here: 59.8 us
  starting transfers between devices  19.4 us (32%)
  local copies, waits for them, and re-layouts  12.1 us (20%)
  Pallas kernels  7.46 us (12%)
  waiting for transfers between devices  7.15 us (12%)
  other arithmetic  6.62 us (11%)
  matrix products  6.2 us (10%)
  between operations  0.83 us (1%)
    all_to_all x1, starting transfers between devices, on_device(): pieces = lax.all_to_all(pieces, 'tp', 0, 0, tiled=True)  10.1 us
    pallas_call x1, Pallas kernels, attend(): pl.pallas_call(attend_kernel, in_specs=[pl.BlockSpec(memory_space=pltpu.S...  7.46 us
    all_to_all x1, starting transfers between devices, on_device(): gathered_q = lax.all_to_all(sent, 'mem', 0, 0, tiled=True)  5 us
    all_to_all x1, waiting for transfers between devices, on_device(): pieces = lax.all_to_all(pieces, 'tp', 0, 0, tiled=True)  4.63 us
    unnamed x15, local copies, waits for them, and re-layouts  4.34 us
    all_to_all x1, starting transfers between devices, on_device(): partials = lax.all_to_all(message, 'mem', 0, 0, tiled=True)  4.25 us
    dot_general x1, matrix products, on_device(): lax.dot_general(out_weight, attention, (((0,), (1,)), ((), ())), preferre...  3 us
    all_to_all x1, waiting for transfers between devices, on_device(): partials = lax.all_to_all(message, 'mem', 0, 0, tiled=True)  2.52 us
  transfers between devices with their start and end apart: 3, of which 2 were waited for; matrix products, arithmetic and copies ran while one was open for 22% of the time, Pallas kernels for 0%

profile of v9, /device:TPU:1, one launch (start us, length us, event | category | flops | bytes accessed | tf_op | source)
XLA Modules:
  0.0 59.8 jit_solution(9607481817075942182)
XLA Ops:
  0.6 1.6 %copy.67.keys_hbm = bf16[576,128]{1,0:T(8,128)(2,1)} copy(bf16[576,128]{1,0:T(8,128)(2,1)} %param.14) | data formatting | bytes 294912
  2.2 1.6 %copy.68.values_hbm = bf16[576,128]{1,0:T(8,128)(2,1)} copy(bf16[576,128]{1,0:T(8,128)(2,1)} %param.15) | data formatting | bytes 294912
  3.8 1.4 %broadcast_in_dim.53 = bf16[4,32,512]{2,1,0:T(8,128)(2,1)} broadcast(bf16[32,512]{1,0:T(8,128)(2,1)} %bitcast.114), dimensions={1,2} | broadcast | bytes 163840 | tf_op jit(solution)/shard_map/broadcast_in_dim | solution.py:185
  5.2 5.0 %all-to-all-start = ((bf16[4,32,512]{2,1,0:T(8,128)(2,1)}), bf16[4,32,512]{2,1,0:T(8,128)(2,1)S(1)}, u32[]{:S(2)}, u32[]{:S(2)}) async-start(bf16[4,32,512]{2,1,0:T(8,128)(2,1)} %broadcast_in_dim.53), calls=%async_computation | async-start | bytes 262144 | tf_op jit(solution)/shard_map/all_to_all | solution.py:188
  10.2 0.7 %fusion.34 = s32[8]{0:T(128)S(1)} fusion(s32[1,8]{1,0:T(1,128)} %param.20), kind=kLoop, calls=%fused_computation.68 | loop fusion | flops 24 | bytes 64 | tf_op jit(solution)/shard_map/jit(_take)/jit(_where)/select_n | solution.py:195
  10.9 0.5 broadcast.132
  11.4 1.3 %reduce.6 = s32[8]{0:T(128)S(1)} reduce(s32[1,8]{1,0:T(1,128)} %param.20, s32[]{:T(128)} %broadcast.132), dimensions={0}, to_apply=%param.20.reduce_sub_computation.3 | reduce | bytes 68 | tf_op args[9]
  12.7 0.7 %add_bitcast_fusion = s32[64,1]{0,1:T(1,128)S(1)} fusion(s32[64]{0:T(128)} %param.18), kind=kLoop, calls=%fused_computation.73 | loop fusion | flops 64 | bytes 512 | tf_op jit(solution)/shard_map/reshape.197
  13.3 0.1 squeeze.12
  13.4 0.1 copy.31
  13.6 0.7 %pad_maximum_fusion = bf16[32,256]{1,0:T(8,128)(2,1)S(1)} fusion(bf16[32,128]{1,0:T(8,128)(2,1)} %bitcast.116, bf16[32,128]{1,0:T(8,128)(2,1)} %bitcast.115), kind=kLoop, calls=%fused_computation.34 | loop fusion | flops 32768 | bytes 32768 | tf_op jit(solution)/shard_map/concatenate | solution.py:194
  14.3 0.6 gather_fusion
  14.9 0.1 copy.30
  15.0 0.1 reduce-window.9
  15.0 0.1 reduce.2
  15.2 0.7 %add_subtract_fusion.1 = s32[64]{0:T(128)S(1)} fusion(s32[64]{0:T(128)S(1)} %reduce.2, s32[64]{0:T(128)} %param.18), kind=kLoop, calls=%fused_computation.72 | loop fusion | flops 128 | bytes 768 | tf_op jit(solution)/shard_map/sub | solution.py:181
  15.8 0.7 %dynamic_slice.11 = s32[4]{0:T(128)S(1)} dynamic-slice(s32[64]{0:T(128)} %param.21, s32[]{:T(128)S(6)} %select_n.57), dynamic_slice_sizes={4} | dynamic-slice | bytes 36 | tf_op jit(solution)/shard_map/dynamic_slice | solution.py:250
  16.6 0.7 %broadcast_subtract_fusion = (s32[4]{0:T(128)S(1)}, s32[4]{0:T(128)S(1)}, s32[4]{0:T(128)S(1)}) fusion(s32[]{:T(128)S(6)} %mul.64, s32[64]{0:T(128)} %param.18, s32[]{:T(128)S(6)} %select_n.57, s32[64]{0:T(128)S(1)} %add_subtract_fusion.1), kind=kLoop, calls=%fused_computation.74 | loop fusion | flops 12 | bytes 88 | tf_op jit(solution)/shard_map/sub | solution.py:193
  17.4 0.1 broadcast_in_dim.54
  17.4 0.6 %dynamic_update_slice.3.extra_ref = bf16[16,512]{1,0:T(8,128)(2,1)} pad(bf16[4,512]{1,0:T(4,128)(2,1)S(1)} %broadcast_select_fusion, bf16[]{:T(256)} %constant.28.clone.1), padding=8_4x0_0 | pad | bytes 20482 | tf_op jit(solution)/shard_map/dynamic_update_slice | solution.py:199
  18.1 0.7 %pad_add_fusion.bounds_ref = s32[8]{0:T(128)} fusion(s32[4]{0:T(128)S(1)} %get-tuple-element.17, s32[4]{0:T(128)S(1)} %get-tuple-element.19), kind=kLoop, calls=%fused_computation.70 | loop fusion | flops 8 | bytes 64 | tf_op jit(solution)/shard_map/concatenate | solution.py:193
  18.7 0.6 %copy-done.4 = bf16[4,32,512]{2,1,0:T(8,128)(2,1)} copy-done((bf16[4,32,512]{2,1,0:T(8,128)(2,1)}, bf16[4,32,512]{2,1,0:T(8,128)(2,1)S(1)}, u32[]{:S(2)}) %copy-start.4) | copy-done | bytes 131096
  19.4 7.5 %shard_map.130 = bf16[4,48,512]{2,1,0:T(8,128)(2,1)} custom-call(s32[8]{0:T(128)} %pad_add_fusion.bounds_ref, bf16[4,32,512]{2,1,0:T(8,128)(2,1)} %copy-done.4, bf16[576,128]{1,0:T(8,128)(2,1)} %copy.67.keys_hbm, bf16[576,128]{1,0:T(8,128)(2,1)} %copy.68.values_hbm, bf16[16,512]{1,0:T(8,128)(2,1)} %dynamic_update_slice.3.extra_ref), custom_call_target="tpu_custom_call" | custom-call | tf_op jit(solution)/shard_map/pallas_call | solution.py:135
  26.8 0.9 %convolution_compare_fusion.4 = pred[32,32]{1,0:T(32,128)(4,1)S(1)} fusion(s32[32]{0:T(128)} %bitcast.118), kind=kOutput, calls=%fused_computation.11 | convolution fusion | flops 69632 | bytes 1152 | tf_op jit(solution)/shard_map/dot_general | solution.py:29
  27.8 0.2 convolution_compare_fusion.2
  28.0 0.2 fusion.2
  28.3 0.1 copy.32
  28.3 4.2 %all-to-all-start.1 = ((bf16[4,48,512]{2,1,0:T(8,128)(2,1)}), bf16[4,48,512]{2,1,0:T(8,128)(2,1)S(1)}, u32[]{:S(2)}, u32[]{:S(2)}) async-start(bf16[4,48,512]{2,1,0:T(8,128)(2,1)} %shard_map.130), calls=%async_computation.1 | async-start | bytes 393216 | tf_op jit(solution)/shard_map/all_to_all | solution.py:204
  32.6 0.8 %reshape.233 = bf16[32,4,128]{2,1,0:T(4,128)(2,1)S(1)} reshape(bf16[1,32,512]{2,1,0:T(8,128)(2,1)} %param.11) | data formatting | bytes 65536 | tf_op jit(solution)/shard_map/reshape.4
  33.4 0.9 %select_reduce_fusion = (f32[4,32]{1,0:T(4,128)S(1)}, f32[1,4,32,32]{2,3,1,0:T(8,128)S(1)}) fusion(pred[32,32]{0,1:T(8,128)(4,1)S(1)} %copy.32, bf16[32,4,128]{2,1,0:T(4,128)(2,1)S(1)} %reshape.233, bf16[1,32,128]{2,1,0:T(8,128)(2,1)} %param.12), kind=kOutput, calls=%fused_computation.25 | convolution fusion | flops 1060736 | bytes 58880 | tf_op jit(solution)/shard_map/tkgd,jkd->kgtj/dot_general | solution.py:217
  34.2 0.9 %convolution_bitcast_fusion = f32[32,1,4,128]{3,0,2,1:T(8,128)S(1)} fusion(f32[1,4,32,32]{2,3,1,0:T(8,128)S(1)} %get-tuple-element.21, f32[4,32]{1,0:T(4,128)S(1)} %get-tuple-element.20, pred[32,32]{0,1:T(8,128)(4,1)S(1)} %copy.32, bf16[1,32,128]{2,1,0:T(8,128)(2,1)} %param.13), kind=kOutput, calls=%fused_computation.4 | convolution fusion | flops 1060864 | bytes 91648 | tf_op jit(solution)/shard_map/kgtj,jkd->tkgd/dot_general | solution.py:223
  35.3 2.5 %all-to-all-done.1 = bf16[4,48,512]{2,1,0:T(8,128)(2,1)S(1)} async-done(((bf16[4,48,512]{2,1,0:T(8,128)(2,1)}), bf16[4,48,512]{2,1,0:T(8,128)(2,1)S(1)}, u32[]{:S(2)}, u32[]{:S(2)}) %all-to-all-start.1) | async-done | bytes 196640 | tf_op jit(solution)/shard_map/all_to_all | solution.py:204
  37.9 0.1 copy.38
  38.0 0.1 copy.37
  38.1 0.1 copy.34
  38.2 0.2 mul.69
  38.4 0.1 mul.70
  38.5 0.1 mul.72
  38.6 0.1 mul.77
  38.7 3.0 %convolution_convert_fusion = bf16[32,4096]{1,0:T(8,128)(2,1)S(1)} fusion(bf16[512,4096]{1,0:T(8,128)(2,1)} %param.17, f32[4,8,4,128]{3,2,1,0:T(4,128)S(1)} %bitcast.112, f32[32,512]{1,0:T(8,128)S(1)} %fusion.3, f32[4,8,4,128]{3,2,1,0:T(4,128)S(1)} %bitcast.111, f32[4,8,4,128]{3,2,1,0:T(4,128)S(1)} %bitcast.113), kind=kOutput, calls=%fused_computation.3 | convolution fusion | flops 134414336 | bytes 4718592 | tf_op jit(solution)/shard_map/dot_general | solution.py:242
  41.7 0.7 %copy.56 = bf16[4,8,8,512]{3,2,0,1:T(8,128)(2,1)} copy(bf16[4,8,8,512]{3,2,1,0:T(8,128)(2,1)S(1)} %bitcast.110) | data formatting | bytes 524288 | tf_op jit(solution)/shard_map/reshape | solution.py:245
  42.5 10.1 %all-to-all-start.2 = ((bf16[8,512,32]{1,2,0:T(8,128)(2,1)}), bf16[8,512,32]{1,2,0:T(8,128)(2,1)S(1)}, u32[]{:S(2)}, u32[]{:S(2)}) async-start(bf16[8,512,32]{1,2,0:T(8,128)(2,1)} %bitcast.107), calls=%async_computation.2 | async-start | bytes 524288 | tf_op jit(solution)/shard_map/all_to_all | solution.py:246
  52.7 0.1 lt.78
  52.8 0.1 sub.68
  52.9 0.8 %scatter_custom_fusion.1 = bf16[576,128]{1,0:T(8,128)(2,1)S(1)} fusion(bf16[576,128]{1,0:T(8,128)(2,1)S(1)} %copy-done.2, s32[32]{0:T(128)S(1)} %fusion.35, bf16[32,256]{1,0:T(8,128)(2,1)S(1)} %reshape_reshape.7), kind=kCustom, calls=%fused_computation.38 | custom fusion | bytes 155648 | tf_op jit(solution)/shard_map/scatter | solution.py:257
  53.7 0.8 %scatter_custom_fusion = bf16[576,128]{1,0:T(8,128)(2,1)S(1)} fusion(bf16[576,128]{1,0:T(8,128)(2,1)S(1)} %copy-done, s32[32]{0:T(128)S(1)} %fusion.35, bf16[32,256]{1,0:T(8,128)(2,1)S(1)} %reshape_reshape.7), kind=kCustom, calls=%fused_computation.40 | custom fusion | bytes 155648 | tf_op jit(solution)/shard_map/scatter | solution.py:256
  54.5 4.6 %all-to-all-done.2 = bf16[8,512,32]{1,2,0:T(8,128)(2,1)S(1)} async-done(((bf16[8,512,32]{1,2,0:T(8,128)(2,1)}), bf16[8,512,32]{1,2,0:T(8,128)(2,1)S(1)}, u32[]{:S(2)}, u32[]{:S(2)}) %all-to-all-start.2) | async-done | bytes 262176 | tf_op jit(solution)/shard_map/all_to_all | solution.py:246
  59.2 0.6 %fusion.11 = bf16[1,32,512]{2,1,0:T(8,128)(2,1)} fusion(f32[512,32]{0,1:T(8,128)S(1)} %convert_reduce_fusion, bf16[1,32,512]{2,1,0:T(8,128)(2,1)S(1)} %copy-done.5), kind=kLoop, calls=%fused_computation.29 | loop fusion | flops 49152 | bytes 131072 | tf_op jit(solution)/shard_map/broadcast_in_dim | solution.py:248
  (30 shorter events, 0.5 us)
Async XLA Ops:
  5.2 13.5 %all-to-all-start = ((bf16[4,32,512]{2,1,0:T(8,128)(2,1)}), bf16[4,32,512]{2,1,0:T(8,128)(2,1)S(1)}, u32[]{:S(2)}, u32[]{:S(2)}) async-start(bf16[4,32,512]{2,1,0:T(8,128)(2,1)} %broadcast_in_dim.53), calls=%async_computation | async-start | bytes 262144 | tf_op jit(solution)/shard_map/all_to_all | solution.py:188
  18.7 0.6 %copy-start.4 = (bf16[4,32,512]{2,1,0:T(8,128)(2,1)}, bf16[4,32,512]{2,1,0:T(8,128)(2,1)S(1)}, u32[]{:S(2)}) copy-start(bf16[4,32,512]{2,1,0:T(8,128)(2,1)S(1)} %all-to-all-done.queries_ref) | copy-start | bytes 393220
  28.3 9.4 %all-to-all-start.1 = ((bf16[4,48,512]{2,1,0:T(8,128)(2,1)}), bf16[4,48,512]{2,1,0:T(8,128)(2,1)S(1)}, u32[]{:S(2)}, u32[]{:S(2)}) async-start(bf16[4,48,512]{2,1,0:T(8,128)(2,1)} %shard_map.130), calls=%async_computation.1 | async-start | bytes 393216 | tf_op jit(solution)/shard_map/all_to_all | solution.py:204
  35.1 17.8 %copy-start.2 = (bf16[576,128]{1,0:T(8,128)(2,1)S(1)}, bf16[576,128]{1,0:T(8,128)(2,1)}, u32[]{:S(2)}) copy-start(bf16[576,128]{1,0:T(8,128)(2,1)} %copy.68.values_hbm) | copy-start | bytes 442372
  35.2 18.4 %copy-start = (bf16[576,128]{1,0:T(8,128)(2,1)S(1)}, bf16[576,128]{1,0:T(8,128)(2,1)}, u32[]{:S(2)}) copy-start(bf16[576,128]{1,0:T(8,128)(2,1)} %copy.67.keys_hbm) | copy-start | bytes 442372
  37.8 21.3 %copy-start.5 = (bf16[1,32,512]{2,1,0:T(8,128)(2,1)S(1)}, bf16[1,32,512]{2,1,0:T(8,128)(2,1)}, u32[]{:S(2)}) copy-start(bf16[1,32,512]{2,1,0:T(8,128)(2,1)} %param.16) | copy-start | bytes 98308
  42.5 16.6 %all-to-all-start.2 = ((bf16[8,512,32]{1,2,0:T(8,128)(2,1)}), bf16[8,512,32]{1,2,0:T(8,128)(2,1)S(1)}, u32[]{:S(2)}, u32[]{:S(2)}) async-start(bf16[8,512,32]{1,2,0:T(8,128)(2,1)} %bitcast.107), calls=%async_computation.2 | async-start | bytes 524288 | tf_op jit(solution)/shard_map/all_to_all | solution.py:246
  53.7 6.1 %copy-start.3 = (bf16[576,128]{1,0:T(8,128)(2,1)}, bf16[576,128]{1,0:T(8,128)(2,1)S(1)}, u32[]{:S(2)}) copy-start(bf16[576,128]{1,0:T(8,128)(2,1)S(1)} %scatter_custom_fusion.1) | copy-start | bytes 442372
  54.5 5.3 %copy-start.1 = (bf16[576,128]{1,0:T(8,128)(2,1)}, bf16[576,128]{1,0:T(8,128)(2,1)S(1)}, u32[]{:S(2)}) copy-start(bf16[576,128]{1,0:T(8,128)(2,1)S(1)} %scatter_custom_fusion) | copy-start | bytes 442372

commit v10 on v8

--- a/solution.py
+++ b/solution.py
@@ -109,7 +109,6 @@
     places = low_edge + jnp.arange(positions, dtype=jnp.int32)
 
     sent = jnp.broadcast_to(queries, (GROUP,) + queries.shape[1:])
-    sent, cache_keys, cache_values = lax.optimization_barrier((sent, cache_keys, cache_values))
     keys_local = cache_keys.reshape(positions, kv_local, HD)
     values_local = cache_values.reshape(positions, kv_local, HD)
     gathered_q = lax.all_to_all(sent, "mem", 0, 0, tiled=True)
@@ -149,8 +148,8 @@
         [summed.reshape(GROUP, TREE, q_width).astype(jnp.bfloat16), stats, row_lines, filler],
         axis=1,
     )
-    message, queries, tree_keys, tree_values, parents = lax.optimization_barrier(
-        (message, queries, tree_keys, tree_values, parents)
+    message, queries, tree_keys, tree_values = lax.optimization_barrier(
+        (message, queries, tree_keys, tree_values)
     )
     partials = lax.all_to_all(message, "mem", 0, 0, tiled=True)
     row_block = partials[:, TREE + 1 : used].reshape(GROUP, A_MAX, 2 * channels)

time: 51.1 us -> 51.2 us (level)
  matrix products: 4.95 us -> 5.69 us
  other arithmetic: 7.24 us -> 6.59 us
    unnamed x17 -> x19, local copies, waits for them, and re-layouts: 0.56 us -> 2.39 us
    optimization_barrier x2 -> x0, local copies, waits for them, and re-layouts: 1.83 us -> none  [on_device(): lax.optimization_barrier((sent, cache_keys, cache_values))]
    dot_general x3, matrix products: 0.69 us -> 1.42 us  [ancestry(): jnp.dot(reach, reach, preferred_element_type=jnp.float32) > 0]
    add x1, other arithmetic: 0.73 us -> 0.08 us  [on_device(): begin + length]
  transfers between devices with their start and end apart: 3 -> 3, of which waited for: 2 -> 2; matrix products, arithmetic and copies ran while one was open for 18% -> 20% of each run, Pallas kernels for 0% -> 0%
where the time goes in v10:
time: 51.2 us; the launch traced here: 50.6 us
  starting transfers between devices  19.4 us (38%)
  waiting for transfers between devices  9.34 us (18%)
  local copies, waits for them, and re-layouts  8.69 us (17%)
  other arithmetic  6.59 us (13%)
  matrix products  5.69 us (11%)
  between operations  0.88 us (2%)
    all_to_all x1, starting transfers between devices, on_device(): pieces = lax.all_to_all(pieces, 'tp', 0, 0, tiled=True)  10.2 us
    all_to_all x1, starting transfers between devices, on_device(): gathered_q = lax.all_to_all(sent, 'mem', 0, 0, tiled=True)  5 us
    all_to_all x1, waiting for transfers between devices, on_device(): partials = lax.all_to_all(message, 'mem', 0, 0, tiled=True)  4.69 us
    all_to_all x1, waiting for transfers between devices, on_device(): pieces = lax.all_to_all(pieces, 'tp', 0, 0, tiled=True)  4.65 us
    all_to_all x1, starting transfers between devices, on_device(): partials = lax.all_to_all(message, 'mem', 0, 0, tiled=True)  4.25 us
    dot_general x1, matrix products, on_device(): lax.dot_general(out_weight, attention, (((0,), (1,)), ((), ())), preferre...  3 us
    unnamed x19, local copies, waits for them, and re-layouts  2.39 us
    broadcast_in_dim x1, local copies, waits for them, and re-layouts, on_device(): sent = jnp.broadcast_to(queries, (GROUP,) + queries.shape[1:])  1.42 us
  transfers between devices with their start and end apart: 3, of which 2 were waited for; matrix products, arithmetic and copies ran while one was open for 20% of the time, Pallas kernels for 0%

profile of v10, /device:TPU:1, one launch (start us, length us, event | category | flops | bytes accessed | tf_op | source)
XLA Modules:
  0.0 50.6 jit_solution(6903961243527547212)
XLA Ops:
  0.7 0.9 %copy.102 = bf16[576,128]{1,0:T(8,128)(2,1)S(1)} copy(bf16[576,128]{1,0:T(8,128)(2,1)} %param.14) | data formatting | bytes 294912
  1.6 0.9 %copy.103 = bf16[576,128]{1,0:T(8,128)(2,1)S(1)} copy(bf16[576,128]{1,0:T(8,128)(2,1)} %param.15) | data formatting | bytes 294912
  2.5 1.4 %broadcast_in_dim.85 = bf16[4,32,512]{2,1,0:T(8,128)(2,1)} broadcast(bf16[32,512]{1,0:T(8,128)(2,1)} %bitcast.154), dimensions={1,2} | broadcast | bytes 163840 | tf_op jit(solution)/shard_map/broadcast_in_dim | solution.py:111
  3.9 5.0 %all-to-all-start = ((bf16[4,32,512]{2,1,0:T(8,128)(2,1)}), bf16[4,32,512]{2,1,0:T(8,128)(2,1)S(1)}, u32[]{:S(2)}, u32[]{:S(2)}) async-start(bf16[4,32,512]{2,1,0:T(8,128)(2,1)} %broadcast_in_dim.85), calls=%async_computation | async-start | bytes 262144 | tf_op jit(solution)/shard_map/all_to_all | solution.py:114
  8.9 0.7 %add_bitcast_fusion = s32[64,1]{0,1:T(1,128)S(1)} fusion(s32[64]{0:T(128)} %param.18), kind=kLoop, calls=%fused_computation.95 | loop fusion | flops 64 | bytes 512 | tf_op jit(solution)/shard_map/reshape.323
  9.6 0.1 copy.50
  9.7 0.1 reduce-window.9
  9.8 0.1 reduce.4
  9.9 0.7 %add_subtract_fusion.1 = s32[64]{0:T(128)S(1)} fusion(s32[64]{0:T(128)S(1)} %reduce.4, s32[64]{0:T(128)} %param.18), kind=kLoop, calls=%fused_computation.94 | loop fusion | flops 128 | bytes 768 | tf_op jit(solution)/shard_map/sub | solution.py:107
  10.5 0.7 %fusion.48 = s32[8]{0:T(128)S(1)} fusion(s32[1,8]{1,0:T(1,128)} %param.20), kind=kLoop, calls=%fused_computation.91 | loop fusion | flops 24 | bytes 64 | tf_op jit(solution)/shard_map/jit(_take)/jit(_where)/select_n | solution.py:141
  11.2 0.7 %pad_maximum_fusion = bf16[32,256]{1,0:T(8,128)(2,1)S(1)} fusion(bf16[32,128]{1,0:T(8,128)(2,1)} %bitcast.156, bf16[32,128]{1,0:T(8,128)(2,1)} %bitcast.155), kind=kLoop, calls=%fused_computation.53 | loop fusion | flops 32768 | bytes 32768 | tf_op jit(solution)/shard_map/concatenate | solution.py:140
  11.9 0.6 %gather_fusion = bf16[8,256]{1,0:T(8,128)(2,1)S(1)} fusion(bf16[32,256]{1,0:T(8,128)(2,1)S(1)} %pad_maximum_fusion, s32[1024]{0:T(1024)S(1)} %pad_clamp_fusion), kind=kCustom, calls=%fused_computation | custom fusion | bytes 8224 | tf_op jit(solution)/shard_map/jit(_take)/gather | solution.py:141
  12.5 0.5 %broadcast.186 = s32[]{:T(128)} broadcast(s32[]{:T(128)} %constant.13.clone.1), dimensions={} | broadcast | bytes 8 | tf_op args[9]
  13.0 1.3 %reduce.10 = s32[8]{0:T(128)S(1)} reduce(s32[1,8]{1,0:T(1,128)} %param.20, s32[]{:T(128)} %broadcast.186), dimensions={0}, to_apply=%param.20.reduce_sub_computation.3 | reduce | bytes 68 | tf_op args[9]
  14.3 0.1 squeeze.18
  14.4 0.1 copy.55
  14.6 0.9 %convolution_compare_fusion.4 = pred[32,32]{1,0:T(32,128)(4,1)S(1)} fusion(s32[32]{0:T(128)} %bitcast.158), kind=kOutput, calls=%fused_computation.17 | convolution fusion | flops 69632 | bytes 1152 | tf_op jit(solution)/shard_map/dot_general | solution.py:29
  15.5 0.2 convolution_compare_fusion.2
  16.0 0.2 fusion.4
  16.3 0.1 copy.57
  16.4 0.1 dynamic_slice.11
  16.6 0.4 select_reduce_fusion
  17.0 0.1 concatenate.27
  17.1 0.4 fusion.5
  17.5 0.1 concatenate.28
  17.6 0.4 fusion.1
  18.2 0.8 %maximum_maximum_fusion = bf16[4,48,512]{2,1,0:T(8,128)(2,1)} fusion(bf16[4,4,512]{2,1,0:T(4,128)(2,1)S(1)} %broadcast_in_dim.91, bf16[4,1,512]{2,1,0:T(2,128)(2,1)S(1)} %fusion.32, bf16[4,32,512]{2,1,0:T(8,128)(2,1)S(1)} %convert_element_type.109, bf16[48]{0:T(256)(128)(2,1)S(1)} %pad.8.clone), kind=kLoop, calls=%fused_computation.30 | loop fusion | flops 786432 | bytes 348256 | tf_op jit(solution)/shard_map/concatenate | solution.py:147
  19.0 4.2 %all-to-all-start.1 = ((bf16[4,48,512]{2,1,0:T(8,128)(2,1)}), bf16[4,48,512]{2,1,0:T(8,128)(2,1)S(1)}, u32[]{:S(2)}, u32[]{:S(2)}) async-start(bf16[4,48,512]{2,1,0:T(8,128)(2,1)} %maximum_maximum_fusion), calls=%async_computation.1 | async-start | bytes 393216 | tf_op jit(solution)/shard_map/all_to_all | solution.py:154
  23.3 0.2 select_reduce_fusion.1
  23.5 0.2 convolution_bitcast_fusion
  23.8 4.7 %all-to-all-done.1 = bf16[4,48,512]{2,1,0:T(8,128)(2,1)S(1)} async-done(((bf16[4,48,512]{2,1,0:T(8,128)(2,1)}), bf16[4,48,512]{2,1,0:T(8,128)(2,1)S(1)}, u32[]{:S(2)}, u32[]{:S(2)}) %all-to-all-start.1) | async-done | bytes 196640 | tf_op jit(solution)/shard_map/all_to_all | solution.py:154
  28.5 0.1 reshape_squeeze.2
  28.7 0.1 copy.59
  28.8 0.2 mul.85
  29.0 0.1 mul.86
  29.1 0.1 copy.62
  29.2 0.1 copy.63
  29.3 0.1 mul.88
  29.4 0.1 mul.93
  29.5 3.0 %convolution_convert_fusion = bf16[32,4096]{1,0:T(8,128)(2,1)S(1)} fusion(bf16[512,4096]{1,0:T(8,128)(2,1)} %param.17, f32[4,8,4,128]{3,2,1,0:T(4,128)S(1)} %bitcast.152, f32[32,512]{1,0:T(8,128)S(1)} %fusion.12, f32[4,8,4,128]{3,2,1,0:T(4,128)S(1)} %bitcast.151, f32[4,8,4,128]{3,2,1,0:T(4,128)S(1)} %bitcast.153), kind=kOutput, calls=%fused_computation.3 | convolution fusion | flops 134414336 | bytes 4718592 | tf_op jit(solution)/shard_map/dot_general | solution.py:193
  32.5 0.7 %copy.91 = bf16[4,8,8,512]{3,2,0,1:T(8,128)(2,1)} copy(bf16[4,8,8,512]{3,2,1,0:T(8,128)(2,1)S(1)} %bitcast.150) | data formatting | bytes 524288 | tf_op jit(solution)/shard_map/reshape | solution.py:196
  33.3 10.2 %all-to-all-start.2 = ((bf16[8,512,32]{1,2,0:T(8,128)(2,1)}), bf16[8,512,32]{1,2,0:T(8,128)(2,1)S(1)}, u32[]{:S(2)}, u32[]{:S(2)}) async-start(bf16[8,512,32]{1,2,0:T(8,128)(2,1)} %bitcast.149), calls=%async_computation.2 | async-start | bytes 524288 | tf_op jit(solution)/shard_map/all_to_all | solution.py:197
  43.5 0.1 sub.65
  43.6 0.1 lt.95
  43.7 0.8 %scatter_custom_fusion = bf16[576,128]{1,0:T(8,128)(2,1)S(1)} fusion(bf16[576,128]{1,0:T(8,128)(2,1)S(1)} %copy.102, s32[32]{0:T(128)S(1)} %fusion.49, bf16[32,256]{1,0:T(8,128)(2,1)S(1)} %reshape_reshape.7), kind=kCustom, calls=%fused_computation.61 | custom fusion | bytes 155648 | tf_op jit(solution)/shard_map/scatter | solution.py:207
  44.5 0.8 %scatter_custom_fusion.1 = bf16[576,128]{1,0:T(8,128)(2,1)S(1)} fusion(bf16[576,128]{1,0:T(8,128)(2,1)S(1)} %copy.103, s32[32]{0:T(128)S(1)} %fusion.49, bf16[32,256]{1,0:T(8,128)(2,1)S(1)} %reshape_reshape.7), kind=kCustom, calls=%fused_computation.59 | custom fusion | bytes 155648 | tf_op jit(solution)/shard_map/scatter | solution.py:208
  45.3 4.6 %all-to-all-done.2 = bf16[8,512,32]{1,2,0:T(8,128)(2,1)S(1)} async-done(((bf16[8,512,32]{1,2,0:T(8,128)(2,1)}), bf16[8,512,32]{1,2,0:T(8,128)(2,1)S(1)}, u32[]{:S(2)}, u32[]{:S(2)}) %all-to-all-start.2) | async-done | bytes 262176 | tf_op jit(solution)/shard_map/all_to_all | solution.py:197
  50.0 0.6 %fusion.24 = bf16[1,32,512]{2,1,0:T(8,128)(2,1)} fusion(f32[512,32]{0,1:T(8,128)S(1)} %convert_reduce_fusion, bf16[1,32,512]{2,1,0:T(8,128)(2,1)S(1)} %copy-done.5), kind=kLoop, calls=%fused_computation.46 | loop fusion | flops 49152 | bytes 131072 | tf_op jit(solution)/shard_map/broadcast_in_dim | solution.py:199
  (48 shorter events, 1.0 us)
Async XLA Ops:
  0.6 15.1 %copy-start.6 = (s32[64]{0:T(128)S(1)}, s32[64]{0:T(128)}, u32[]{:S(2)}) copy-start(s32[64]{0:T(128)} %param.18) | copy-start | bytes 772
  0.6 15.7 %copy-start.7 = (s32[64]{0:T(128)S(1)}, s32[64]{0:T(128)}, u32[]{:S(2)}) copy-start(s32[64]{0:T(128)} %param.21) | copy-start | bytes 772
  3.9 12.6 %all-to-all-start = ((bf16[4,32,512]{2,1,0:T(8,128)(2,1)}), bf16[4,32,512]{2,1,0:T(8,128)(2,1)S(1)}, u32[]{:S(2)}, u32[]{:S(2)}) async-start(bf16[4,32,512]{2,1,0:T(8,128)(2,1)} %broadcast_in_dim.85), calls=%async_computation | async-start | bytes 262144 | tf_op jit(solution)/shard_map/all_to_all | solution.py:114
  17.6 1.4 %copy-start.2 = (bf16[1,32,512]{2,1,0:T(8,128)(2,1)S(1)}, bf16[1,32,512]{2,1,0:T(8,128)(2,1)}, u32[]{:S(2)}) copy-start(bf16[1,32,512]{2,1,0:T(8,128)(2,1)} %param.11) | copy-start | bytes 98308
  17.6 5.7 %copy-start.3 = (bf16[1,32,128]{2,1,0:T(8,128)(2,1)S(1)}, bf16[1,32,128]{2,1,0:T(8,128)(2,1)}, u32[]{:S(2)}) copy-start(bf16[1,32,128]{2,1,0:T(8,128)(2,1)} %param.12) | copy-start | bytes 24580
  17.6 5.9 %copy-start.4 = (bf16[1,32,128]{2,1,0:T(8,128)(2,1)S(1)}, bf16[1,32,128]{2,1,0:T(8,128)(2,1)}, u32[]{:S(2)}) copy-start(bf16[1,32,128]{2,1,0:T(8,128)(2,1)} %param.13) | copy-start | bytes 24580
  19.0 9.4 %all-to-all-start.1 = ((bf16[4,48,512]{2,1,0:T(8,128)(2,1)}), bf16[4,48,512]{2,1,0:T(8,128)(2,1)S(1)}, u32[]{:S(2)}, u32[]{:S(2)}) async-start(bf16[4,48,512]{2,1,0:T(8,128)(2,1)} %maximum_maximum_fusion), calls=%async_computation.1 | async-start | bytes 393216 | tf_op jit(solution)/shard_map/all_to_all | solution.py:154
  32.5 17.4 %copy-start.5 = (bf16[1,32,512]{2,1,0:T(8,128)(2,1)S(1)}, bf16[1,32,512]{2,1,0:T(8,128)(2,1)}, u32[]{:S(2)}) copy-start(bf16[1,32,512]{2,1,0:T(8,128)(2,1)} %param.16) | copy-start | bytes 98308
  33.3 16.7 %all-to-all-start.2 = ((bf16[8,512,32]{1,2,0:T(8,128)(2,1)}), bf16[8,512,32]{1,2,0:T(8,128)(2,1)S(1)}, u32[]{:S(2)}, u32[]{:S(2)}) async-start(bf16[8,512,32]{1,2,0:T(8,128)(2,1)} %bitcast.149), calls=%async_computation.2 | async-start | bytes 524288 | tf_op jit(solution)/shard_map/all_to_all | solution.py:197
  44.5 6.1 %copy-start = (bf16[576,128]{1,0:T(8,128)(2,1)}, bf16[576,128]{1,0:T(8,128)(2,1)S(1)}, u32[]{:S(2)}) copy-start(bf16[576,128]{1,0:T(8,128)(2,1)S(1)} %scatter_custom_fusion) | copy-start | bytes 442372
  45.3 5.3 %copy-start.1 = (bf16[576,128]{1,0:T(8,128)(2,1)}, bf16[576,128]{1,0:T(8,128)(2,1)S(1)}, u32[]{:S(2)}) copy-start(bf16[576,128]{1,0:T(8,128)(2,1)S(1)} %scatter_custom_fusion.1) | copy-start | bytes 442372

commit v11 on v10

--- a/solution.py
+++ b/solution.py
@@ -104,7 +104,6 @@
     sharing = heads_local // kv_local
     factor = 1.0 / math.sqrt(HD)
     regions = cache_len + A_MAX
-    starts = jnp.cumsum(regions) - regions
     low_edge = seq_rank * positions
     places = low_edge + jnp.arange(positions, dtype=jnp.int32)
 
@@ -114,8 +113,10 @@
     gathered_q = lax.all_to_all(sent, "mem", 0, 0, tiled=True)
 
     group_base = seq_rank - member
-    begin = lax.dynamic_slice_in_dim(starts, group_base, GROUP)
-    length = lax.dynamic_slice_in_dim(cache_len, group_base, GROUP)
+    owners = jnp.arange(cache_len.shape[0], dtype=jnp.int32)[None, :]
+    wanted = group_base + jnp.arange(GROUP, dtype=jnp.int32)[:, None]
+    begin = jnp.sum(jnp.where(owners < wanted, regions[None, :], 0), axis=1)
+    length = jnp.sum(jnp.where(owners == wanted, cache_len[None, :], 0), axis=1)
     inside = (places[None, :] >= begin[:, None]) & (places[None, :] < (begin + length)[:, None])
     shaped = gathered_q.reshape(GROUP, TREE, kv_local, sharing, HD)
     scores = (
@@ -137,8 +138,16 @@
         [top_score.reshape(GROUP, 1, -1), total.reshape(GROUP, 1, -1)], axis=-1
     ).astype(jnp.bfloat16)
     stats = jnp.pad(stats, ((0, 0), (0, 0), (0, q_width - stats.shape[-1])))
-    tree_pair = jnp.concatenate([tree_keys[0], tree_values[0]], axis=-1)
-    mine_rows = jnp.take(tree_pair, accept_rows[0], axis=0)
+    chosen = (accept_rows.reshape(-1, 1) == jnp.arange(TREE, dtype=jnp.int32)[None, :]).astype(
+        jnp.bfloat16
+    )
+    mine_rows = jnp.concatenate(
+        [
+            jnp.dot(chosen, tree_keys[0], preferred_element_type=jnp.float32),
+            jnp.dot(chosen, tree_values[0], preferred_element_type=jnp.float32),
+        ],
+        axis=-1,
+    ).astype(jnp.bfloat16)
     row_lines = mine_rows.reshape(1, -1, q_width)
     row_count = row_lines.shape[1]
     row_lines = jnp.broadcast_to(row_lines, (GROUP,) + row_lines.shape[1:])

time: 51.2 us -> 48.7 us (0.951)
  other arithmetic: 6.59 us -> 3.81 us
  matrix products: 5.69 us -> 7.45 us
  local copies, waits for them, and re-layouts: 8.69 us -> 7.24 us
    dot_general x0 -> x2, matrix products: none -> 1.74 us  [the longest x1 0.9 us: on_device(): jnp.dot(chosen, tree_keys[0], preferred_element_type=jnp.float32)]
    unnamed x1 -> x0, other arithmetic: 1.32 us -> none
    reduce_sum x0 -> x1, other arithmetic: none -> 0.86 us  [on_device(): length = jnp.sum(jnp.where(owners == wanted, cache_len[None, :], 0), axis=1)]
    another operation x3 -> x0, other arithmetic: 0.86 us -> none
    concatenate x1, other arithmetic: 0.72 us -> 0.01 us  [on_device(): jnp.concatenate([jnp.dot(chosen, tree_keys[0], preferred_element_type=jnp...]
    select_n x2 -> x0, other arithmetic: 0.67 us -> none  [on_device(): mine_rows = jnp.take(tree_pair, accept_rows[0], axis=0)]
    sub x1 -> x0, other arithmetic: 0.67 us -> none  [on_device(): starts = jnp.cumsum(regions) - regions]
    add x0 -> x2, other arithmetic: none -> 0.66 us  [the longest x1 0.66 us: on_device(): regions = cache_len + A_MAX]
  transfers between devices with their start and end apart: 3 -> 3, of which waited for: 2 -> 2; matrix products, arithmetic and copies ran while one was open for 20% -> 15% of each run, Pallas kernels for 0% -> 0%
where the time goes in v11:
time: 48.7 us; the launch traced here: 48.1 us
  starting transfers between devices  19.4 us (40%)
  waiting for transfers between devices  9.34 us (19%)
  matrix products  7.45 us (15%)
  local copies, waits for them, and re-layouts  7.24 us (15%)
  other arithmetic  3.81 us (8%)
  between operations  0.87 us (2%)
    all_to_all x1, starting transfers between devices, on_device(): pieces = lax.all_to_all(pieces, 'tp', 0, 0, tiled=True)  10.2 us
    all_to_all x1, starting transfers between devices, on_device(): gathered_q = lax.all_to_all(sent, 'mem', 0, 0, tiled=True)  5 us
    all_to_all x1, waiting for transfers between devices, on_device(): partials = lax.all_to_all(message, 'mem', 0, 0, tiled=True)  4.7 us
    all_to_all x1, waiting for transfers between devices, on_device(): pieces = lax.all_to_all(pieces, 'tp', 0, 0, tiled=True)  4.65 us
    all_to_all x1, starting transfers between devices, on_device(): partials = lax.all_to_all(message, 'mem', 0, 0, tiled=True)  4.24 us
    dot_general x1, matrix products, on_device(): lax.dot_general(out_weight, attention, (((0,), (1,)), ((), ())), preferre...  3.01 us
    unnamed x16, local copies, waits for them, and re-layouts  1.88 us
    broadcast_in_dim x1, local copies, waits for them, and re-layouts, on_device(): sent = jnp.broadcast_to(queries, (GROUP,) + queries.shape[1:])  1.42 us
  transfers between devices with their start and end apart: 3, of which 2 were waited for; matrix products, arithmetic and copies ran while one was open for 15% of the time, Pallas kernels for 0%

profile of v11, /device:TPU:1, one launch (start us, length us, event | category | flops | bytes accessed | tf_op | source)
XLA Modules:
  0.0 48.1 jit_solution(2748402945811414462)
XLA Ops:
  0.6 0.0 copy-start
  0.7 0.9 %copy.108 = bf16[576,128]{1,0:T(8,128)(2,1)S(1)} copy(bf16[576,128]{1,0:T(8,128)(2,1)} %param.14) | data formatting | bytes 294912
  1.6 0.9 %copy.109 = bf16[576,128]{1,0:T(8,128)(2,1)S(1)} copy(bf16[576,128]{1,0:T(8,128)(2,1)} %param.15) | data formatting | bytes 294912
  2.5 1.4 %broadcast_in_dim.99 = bf16[4,32,512]{2,1,0:T(8,128)(2,1)} broadcast(bf16[32,512]{1,0:T(8,128)(2,1)} %bitcast.152), dimensions={1,2} | broadcast | bytes 163840 | tf_op jit(solution)/shard_map/broadcast_in_dim | solution.py:110
  3.9 5.0 %all-to-all-start = ((bf16[4,32,512]{2,1,0:T(8,128)(2,1)}), bf16[4,32,512]{2,1,0:T(8,128)(2,1)S(1)}, u32[]{:S(2)}, u32[]{:S(2)}) async-start(bf16[4,32,512]{2,1,0:T(8,128)(2,1)} %broadcast_in_dim.99), calls=%async_computation | async-start | bytes 262144 | tf_op jit(solution)/shard_map/all_to_all | solution.py:113
  8.9 0.7 %broadcast_add_fusion = s32[64]{0:T(128)S(1)} fusion(s32[64]{0:T(128)} %param.18), kind=kLoop, calls=%fused_computation.98 | loop fusion | flops 64 | bytes 512 | tf_op jit(solution)/shard_map/add | solution.py:106
  9.6 0.9 %select_reduce_fusion.2 = (s32[4]{0:T(128)S(1)}, s32[4]{0:T(128)S(1)}) fusion(s32[64]{0:T(128)} %param.18, s32[4]{0:T(128)S(1)} %iota_add_fusion.1, s32[64]{0:T(128)S(1)} %broadcast_add_fusion), kind=kLoop, calls=%fused_computation.91 | loop fusion | flops 1528 | bytes 560 | tf_op jit(solution)/shard_map/reduce_sum | solution.py:119
  10.5 0.1 add_subtract_fusion
  10.5 0.1 compare_and_fusion
  10.6 0.8 %convolution_convert_fusion.2 = bf16[8,128]{1,0:T(8,128)(2,1)S(1)} fusion(bf16[1,32,128]{2,1,0:T(8,128)(2,1)S(1)} %copy-done, s32[8]{0:T(128)} %bitcast.153), kind=kOutput, calls=%fused_computation.19 | convolution fusion | flops 66816 | bytes 10272 | tf_op jit(solution)/shard_map/dot_general | solution.py:147
  11.5 0.9 %convolution_convert_fusion.3 = bf16[8,128]{1,0:T(8,128)(2,1)S(1)} fusion(bf16[1,32,128]{2,1,0:T(8,128)(2,1)} %param.12, s32[8]{0:T(128)} %bitcast.154), kind=kOutput, calls=%fused_computation.20 | convolution fusion | flops 66816 | bytes 10272 | tf_op jit(solution)/shard_map/dot_general | solution.py:146
  12.4 0.9 %convolution_compare_fusion.4 = pred[32,32]{1,0:T(32,128)(4,1)S(1)} fusion(s32[32]{0:T(128)} %bitcast.155), kind=kOutput, calls=%fused_computation.16 | convolution fusion | flops 69632 | bytes 1152 | tf_op jit(solution)/shard_map/dot_general | solution.py:29
  13.3 0.2 convolution_compare_fusion.2
  13.6 0.2 fusion.4
  13.8 0.1 copy.63
  13.9 0.1 pad.8.clone
  14.0 0.1 dynamic_slice.3
  14.1 0.4 select_reduce_fusion
  14.5 0.1 concatenate.28
  14.6 0.4 fusion.5
  15.0 0.1 concatenate.29
  15.1 0.5 fusion.1
  15.6 0.1 copy.59
  15.7 0.1 convert_element_type.118
  15.8 0.8 %maximum_maximum_fusion = bf16[4,48,512]{2,1,0:T(8,128)(2,1)} fusion(bf16[4,4,512]{2,1,0:T(4,128)(2,1)S(1)} %broadcast_in_dim.102, bf16[4,1,512]{2,1,0:T(2,128)(2,1)S(1)} %fusion.32, bf16[4,32,512]{2,1,0:T(8,128)(2,1)S(1)} %convert_element_type.118, bf16[48]{0:T(256)(128)(2,1)S(1)} %pad.8.clone), kind=kLoop, calls=%fused_computation.31 | loop fusion | flops 786432 | bytes 348256 | tf_op jit(solution)/shard_map/concatenate | solution.py:156
  16.5 4.2 %all-to-all-start.1 = ((bf16[4,48,512]{2,1,0:T(8,128)(2,1)}), bf16[4,48,512]{2,1,0:T(8,128)(2,1)S(1)}, u32[]{:S(2)}, u32[]{:S(2)}) async-start(bf16[4,48,512]{2,1,0:T(8,128)(2,1)} %maximum_maximum_fusion), calls=%async_computation.1 | async-start | bytes 393216 | tf_op jit(solution)/shard_map/all_to_all | solution.py:163
  20.8 0.2 select_reduce_fusion.1
  21.0 0.2 convolution_bitcast_fusion
  21.3 4.7 %all-to-all-done.1 = bf16[4,48,512]{2,1,0:T(8,128)(2,1)S(1)} async-done(((bf16[4,48,512]{2,1,0:T(8,128)(2,1)}), bf16[4,48,512]{2,1,0:T(8,128)(2,1)S(1)}, u32[]{:S(2)}, u32[]{:S(2)}) %all-to-all-start.1) | async-done | bytes 196640 | tf_op jit(solution)/shard_map/all_to_all | solution.py:163
  26.0 0.1 reshape_squeeze.2
  26.2 0.1 copy.65
  26.3 0.2 mul.85
  26.5 0.1 mul.86
  26.7 0.1 copy.68
  26.8 0.1 copy.69
  26.8 0.1 mul.88
  26.9 0.1 mul.93
  27.0 3.0 %convolution_convert_fusion = bf16[32,4096]{1,0:T(8,128)(2,1)S(1)} fusion(bf16[512,4096]{1,0:T(8,128)(2,1)} %param.17, f32[4,8,4,128]{3,2,1,0:T(4,128)S(1)} %bitcast.150, f32[32,512]{1,0:T(8,128)S(1)} %fusion.12, f32[4,8,4,128]{3,2,1,0:T(4,128)S(1)} %bitcast.149, f32[4,8,4,128]{3,2,1,0:T(4,128)S(1)} %bitcast.151), kind=kOutput, calls=%fused_computation.2 | convolution fusion | flops 134414336 | bytes 4718592 | tf_op jit(solution)/shard_map/dot_general | solution.py:202
  30.0 0.0 copy-start.4
  30.1 0.7 %copy.97 = bf16[4,8,8,512]{3,2,0,1:T(8,128)(2,1)} copy(bf16[4,8,8,512]{3,2,1,0:T(8,128)(2,1)S(1)} %bitcast.148) | data formatting | bytes 524288 | tf_op jit(solution)/shard_map/reshape | solution.py:205
  30.8 10.2 %all-to-all-start.2 = ((bf16[8,512,32]{1,2,0:T(8,128)(2,1)}), bf16[8,512,32]{1,2,0:T(8,128)(2,1)S(1)}, u32[]{:S(2)}, u32[]{:S(2)}) async-start(bf16[8,512,32]{1,2,0:T(8,128)(2,1)} %bitcast.147), calls=%async_computation.2 | async-start | bytes 524288 | tf_op jit(solution)/shard_map/all_to_all | solution.py:206
  40.9 0.1 iota_compare_fusion.6
  41.0 0.1 sub.61
  41.1 0.1 lt.94
  41.2 0.8 %scatter_custom_fusion = bf16[576,128]{1,0:T(8,128)(2,1)S(1)} fusion(bf16[576,128]{1,0:T(8,128)(2,1)S(1)} %copy.108, s32[32]{0:T(128)S(1)} %fusion.52, bf16[32,256]{1,0:T(8,128)(2,1)S(1)} %reshape_reshape.7), kind=kCustom, calls=%fused_computation.61 | custom fusion | bytes 155648 | tf_op jit(solution)/shard_map/scatter | solution.py:216
  42.0 0.8 %scatter_custom_fusion.1 = bf16[576,128]{1,0:T(8,128)(2,1)S(1)} fusion(bf16[576,128]{1,0:T(8,128)(2,1)S(1)} %copy.109, s32[32]{0:T(128)S(1)} %fusion.52, bf16[32,256]{1,0:T(8,128)(2,1)S(1)} %reshape_reshape.7), kind=kCustom, calls=%fused_computation.59 | custom fusion | bytes 155648 | tf_op jit(solution)/shard_map/scatter | solution.py:217
  42.8 4.6 %all-to-all-done.2 = bf16[8,512,32]{1,2,0:T(8,128)(2,1)S(1)} async-done(((bf16[8,512,32]{1,2,0:T(8,128)(2,1)}), bf16[8,512,32]{1,2,0:T(8,128)(2,1)S(1)}, u32[]{:S(2)}, u32[]{:S(2)}) %all-to-all-start.2) | async-done | bytes 262176 | tf_op jit(solution)/shard_map/all_to_all | solution.py:206
  47.5 0.6 %fusion.24 = bf16[1,32,512]{2,1,0:T(8,128)(2,1)} fusion(f32[512,32]{0,1:T(8,128)S(1)} %convert_reduce_fusion, bf16[1,32,512]{2,1,0:T(8,128)(2,1)S(1)} %copy-done.4), kind=kLoop, calls=%fused_computation.47 | loop fusion | flops 49152 | bytes 131072 | tf_op jit(solution)/shard_map/broadcast_in_dim | solution.py:208
  (36 shorter events, 0.4 us)
Async XLA Ops:
  0.6 10.0 %copy-start = (bf16[1,32,128]{2,1,0:T(8,128)(2,1)S(1)}, bf16[1,32,128]{2,1,0:T(8,128)(2,1)}, u32[]{:S(2)}) copy-start(bf16[1,32,128]{2,1,0:T(8,128)(2,1)} %param.13) | copy-start | bytes 24580
  0.6 13.3 %copy-start.6 = (s32[64]{0:T(128)S(1)}, s32[64]{0:T(128)}, u32[]{:S(2)}) copy-start(s32[64]{0:T(128)} %param.21) | copy-start | bytes 772
  3.9 10.1 %all-to-all-start = ((bf16[4,32,512]{2,1,0:T(8,128)(2,1)}), bf16[4,32,512]{2,1,0:T(8,128)(2,1)S(1)}, u32[]{:S(2)}, u32[]{:S(2)}) async-start(bf16[4,32,512]{2,1,0:T(8,128)(2,1)} %broadcast_in_dim.99), calls=%async_computation | async-start | bytes 262144 | tf_op jit(solution)/shard_map/all_to_all | solution.py:113
  15.1 1.4 %copy-start.3 = (bf16[1,32,512]{2,1,0:T(8,128)(2,1)S(1)}, bf16[1,32,512]{2,1,0:T(8,128)(2,1)}, u32[]{:S(2)}) copy-start(bf16[1,32,512]{2,1,0:T(8,128)(2,1)} %param.11) | copy-start | bytes 98308
  15.1 5.7 %copy-start.5 = (bf16[1,32,128]{2,1,0:T(8,128)(2,1)S(1)}, bf16[1,32,128]{2,1,0:T(8,128)(2,1)}, u32[]{:S(2)}) copy-start(bf16[1,32,128]{2,1,0:T(8,128)(2,1)} %param.12) | copy-start | bytes 24580
  16.5 9.4 %all-to-all-start.1 = ((bf16[4,48,512]{2,1,0:T(8,128)(2,1)}), bf16[4,48,512]{2,1,0:T(8,128)(2,1)S(1)}, u32[]{:S(2)}, u32[]{:S(2)}) async-start(bf16[4,48,512]{2,1,0:T(8,128)(2,1)} %maximum_maximum_fusion), calls=%async_computation.1 | async-start | bytes 393216 | tf_op jit(solution)/shard_map/all_to_all | solution.py:163
  30.0 17.4 %copy-start.4 = (bf16[1,32,512]{2,1,0:T(8,128)(2,1)S(1)}, bf16[1,32,512]{2,1,0:T(8,128)(2,1)}, u32[]{:S(2)}) copy-start(bf16[1,32,512]{2,1,0:T(8,128)(2,1)} %param.16) | copy-start | bytes 98308
  30.8 16.7 %all-to-all-start.2 = ((bf16[8,512,32]{1,2,0:T(8,128)(2,1)}), bf16[8,512,32]{1,2,0:T(8,128)(2,1)S(1)}, u32[]{:S(2)}, u32[]{:S(2)}) async-start(bf16[8,512,32]{1,2,0:T(8,128)(2,1)} %bitcast.147), calls=%async_computation.2 | async-start | bytes 524288 | tf_op jit(solution)/shard_map/all_to_all | solution.py:206
  42.0 6.1 %copy-start.1 = (bf16[576,128]{1,0:T(8,128)(2,1)}, bf16[576,128]{1,0:T(8,128)(2,1)S(1)}, u32[]{:S(2)}) copy-start(bf16[576,128]{1,0:T(8,128)(2,1)S(1)} %scatter_custom_fusion) | copy-start | bytes 442372
  42.8 5.3 %copy-start.2 = (bf16[576,128]{1,0:T(8,128)(2,1)}, bf16[576,128]{1,0:T(8,128)(2,1)S(1)}, u32[]{:S(2)}) copy-start(bf16[576,128]{1,0:T(8,128)(2,1)S(1)} %scatter_custom_fusion.1) | copy-start | bytes 442372

commit v12 on v11

--- a/solution.py
+++ b/solution.py
@@ -199,10 +199,12 @@
     attention = scale_heads(joint_out, 1.0 / joint_total).astype(jnp.bfloat16)
 
     tp_size = lax.axis_size("tp")
-    projected = lax.dot_general(
-        out_weight, attention, (((0,), (1,)), ((), ())), preferred_element_type=jnp.float32
+    pieces = lax.dot_general(
+        out_weight.reshape(out_weight.shape[0], tp_size, -1),
+        attention,
+        (((0,), (1,)), ((), ())),
+        preferred_element_type=jnp.float32,
     ).astype(jnp.bfloat16)
-    pieces = projected.reshape(tp_size, -1, TREE)
     pieces = lax.all_to_all(pieces, "tp", 0, 0, tiled=True)
     summed_heads = jnp.sum(pieces.astype(jnp.float32), axis=0)
     mixed = (residual[0].astype(jnp.float32) + summed_heads.T).astype(jnp.bfloat16)[None]

time: 48.7 us -> 48.6 us (level)
  local copies, waits for them, and re-layouts: 7.24 us -> 6.15 us
  matrix products: 7.45 us -> 8.17 us
    reshape x1 -> x0, local copies, waits for them, and re-layouts: 0.72 us -> none  [on_device(): pieces = projected.reshape(tp_size, -1, TREE)]
    dot_general x1, matrix products: 3.01 us -> 3.72 us  [on_device(): lax.dot_general(out_weight.reshape(out_weight.shape[0], tp_size, -1), att...]
where the time goes in v12:
time: 48.6 us; the launch traced here: 48 us
  starting transfers between devices  19.4 us (40%)
  waiting for transfers between devices  9.58 us (20%)
  matrix products  8.17 us (17%)
  local copies, waits for them, and re-layouts  6.15 us (13%)
  other arithmetic  3.81 us (8%)
  between operations  0.88 us (2%)
    all_to_all x1, starting transfers between devices, on_device(): pieces = lax.all_to_all(pieces, 'tp', 0, 0, tiled=True)  10.2 us
    all_to_all x1, starting transfers between devices, on_device(): gathered_q = lax.all_to_all(sent, 'mem', 0, 0, tiled=True)  5 us
    all_to_all x1, waiting for transfers between devices, on_device(): partials = lax.all_to_all(message, 'mem', 0, 0, tiled=True)  4.93 us
    all_to_all x1, waiting for transfers between devices, on_device(): pieces = lax.all_to_all(pieces, 'tp', 0, 0, tiled=True)  4.65 us
    all_to_all x1, starting transfers between devices, on_device(): partials = lax.all_to_all(message, 'mem', 0, 0, tiled=True)  4.23 us
    dot_general x1, matrix products, on_device(): lax.dot_general(out_weight.reshape(out_weight.shape[0], tp_size, -1), att...  3.72 us
    unnamed x16, local copies, waits for them, and re-layouts  1.88 us
    broadcast_in_dim x1, local copies, waits for them, and re-layouts, on_device(): sent = jnp.broadcast_to(queries, (GROUP,) + queries.shape[1:])  1.42 us
  transfers between devices with their start and end apart: 3, of which 2 were waited for; matrix products, arithmetic and copies ran while one was open for 15% of the time, Pallas kernels for 0%

profile of v12, /device:TPU:1, one launch (start us, length us, event | category | flops | bytes accessed | tf_op | source)
XLA Modules:
  0.0 48.0 jit_solution(12708867423284582408)
XLA Ops:
  0.6 0.0 copy-start
  0.6 0.0 copy-start.6
  0.7 0.9 %copy.92 = bf16[576,128]{1,0:T(8,128)(2,1)S(1)} copy(bf16[576,128]{1,0:T(8,128)(2,1)} %param.14) | data formatting | bytes 294912
  1.6 0.9 %copy.93 = bf16[576,128]{1,0:T(8,128)(2,1)S(1)} copy(bf16[576,128]{1,0:T(8,128)(2,1)} %param.15) | data formatting | bytes 294912
  2.5 1.4 %broadcast_in_dim.99 = bf16[4,32,512]{2,1,0:T(8,128)(2,1)} broadcast(bf16[32,512]{1,0:T(8,128)(2,1)} %bitcast.149), dimensions={1,2} | broadcast | bytes 163840 | tf_op jit(solution)/shard_map/broadcast_in_dim | solution.py:110
  3.9 5.0 %all-to-all-start = ((bf16[4,32,512]{2,1,0:T(8,128)(2,1)}), bf16[4,32,512]{2,1,0:T(8,128)(2,1)S(1)}, u32[]{:S(2)}, u32[]{:S(2)}) async-start(bf16[4,32,512]{2,1,0:T(8,128)(2,1)} %broadcast_in_dim.99), calls=%async_computation | async-start | bytes 262144 | tf_op jit(solution)/shard_map/all_to_all | solution.py:113
  8.9 0.7 %broadcast_add_fusion = s32[64]{0:T(128)S(1)} fusion(s32[64]{0:T(128)} %param.18), kind=kLoop, calls=%fused_computation.101 | loop fusion | flops 64 | bytes 512 | tf_op jit(solution)/shard_map/add | solution.py:106
  9.6 0.9 %select_reduce_fusion.2 = (s32[4]{0:T(128)S(1)}, s32[4]{0:T(128)S(1)}) fusion(s32[64]{0:T(128)} %param.18, s32[4]{0:T(128)S(1)} %iota_add_fusion.1, s32[64]{0:T(128)S(1)} %broadcast_add_fusion), kind=kLoop, calls=%fused_computation.94 | loop fusion | flops 1528 | bytes 560 | tf_op jit(solution)/shard_map/reduce_sum | solution.py:119
  10.5 0.1 add_subtract_fusion
  10.5 0.1 compare_and_fusion
  10.6 0.0 copy-done
  10.6 0.8 %convolution_convert_fusion.1 = bf16[8,128]{1,0:T(8,128)(2,1)S(1)} fusion(bf16[1,32,128]{2,1,0:T(8,128)(2,1)S(1)} %copy-done, s32[8]{0:T(128)} %bitcast.150), kind=kOutput, calls=%fused_computation.27 | convolution fusion | flops 66816 | bytes 10272 | tf_op jit(solution)/shard_map/dot_general | solution.py:147
  11.5 0.9 %convolution_convert_fusion.2 = bf16[8,128]{1,0:T(8,128)(2,1)S(1)} fusion(bf16[1,32,128]{2,1,0:T(8,128)(2,1)} %param.12, s32[8]{0:T(128)} %bitcast.151), kind=kOutput, calls=%fused_computation.28 | convolution fusion | flops 66816 | bytes 10272 | tf_op jit(solution)/shard_map/dot_general | solution.py:146
  12.4 0.9 %convolution_compare_fusion.4 = pred[32,32]{1,0:T(32,128)(4,1)S(1)} fusion(s32[32]{0:T(128)} %bitcast.152), kind=kOutput, calls=%fused_computation.24 | convolution fusion | flops 69632 | bytes 1152 | tf_op jit(solution)/shard_map/dot_general | solution.py:29
  13.3 0.2 convolution_compare_fusion.2
  13.6 0.2 fusion.17
  13.8 0.1 copy.49
  13.9 0.1 pad.8.clone
  14.0 0.1 dynamic_slice.3
  14.1 0.0 all-to-all-done
  14.1 0.4 select_reduce_fusion
  14.5 0.1 concatenate.28
  14.6 0.4 fusion.18
  15.0 0.1 concatenate.29
  15.1 0.5 fusion.10
  15.6 0.1 copy.45
  15.7 0.1 convert_element_type.127
  15.8 0.8 %maximum_maximum_fusion = bf16[4,48,512]{2,1,0:T(8,128)(2,1)} fusion(bf16[4,4,512]{2,1,0:T(4,128)(2,1)S(1)} %broadcast_in_dim.102, bf16[4,1,512]{2,1,0:T(2,128)(2,1)S(1)} %fusion.42, bf16[4,32,512]{2,1,0:T(8,128)(2,1)S(1)} %convert_element_type.127, bf16[48]{0:T(256)(128)(2,1)S(1)} %pad.8.clone), kind=kLoop, calls=%fused_computation.38 | loop fusion | flops 786432 | bytes 348256 | tf_op jit(solution)/shard_map/concatenate | solution.py:156
  16.5 4.2 %all-to-all-start.1 = ((bf16[4,48,512]{2,1,0:T(8,128)(2,1)}), bf16[4,48,512]{2,1,0:T(8,128)(2,1)S(1)}, u32[]{:S(2)}, u32[]{:S(2)}) async-start(bf16[4,48,512]{2,1,0:T(8,128)(2,1)} %maximum_maximum_fusion), calls=%async_computation.1 | async-start | bytes 393216 | tf_op jit(solution)/shard_map/all_to_all | solution.py:163
  20.8 0.2 select_reduce_fusion.1
  21.0 4.9 %all-to-all-done.1 = bf16[4,48,512]{2,1,0:T(8,128)(2,1)S(1)} async-done(((bf16[4,48,512]{2,1,0:T(8,128)(2,1)}), bf16[4,48,512]{2,1,0:T(8,128)(2,1)S(1)}, u32[]{:S(2)}, u32[]{:S(2)}) %all-to-all-start.1) | async-done | bytes 196640 | tf_op jit(solution)/shard_map/all_to_all | solution.py:163
  26.0 0.1 reshape_squeeze.2
  26.1 0.1 copy.51
  26.2 0.2 mul.95
  26.5 0.1 mul.96
  26.6 0.2 fusion.15
  26.9 0.0 copy-start.4
  26.9 3.7 %fusion.7 = bf16[8,512,32]{1,2,0:T(8,128)(2,1)} fusion(bf16[32,512,1]{1,0,2:T(8,128)(2,1)S(1)} %reshape.369, bf16[64,8,8,512]{3,2,1,0:T(8,128)(2,1)} %bitcast.148), kind=kOutput, calls=%fused_computation.10 | convolution fusion | flops 134348800 | bytes 4489216 | tf_op jit(solution)/shard_map/dot_general | solution.py:202
  30.6 10.2 %all-to-all-start.2 = ((bf16[8,512,32]{1,2,0:T(8,128)(2,1)}), bf16[8,512,32]{1,2,0:T(8,128)(2,1)S(1)}, u32[]{:S(2)}, u32[]{:S(2)}) async-start(bf16[8,512,32]{1,2,0:T(8,128)(2,1)} %fusion.7), calls=%async_computation.2 | async-start | bytes 524288 | tf_op jit(solution)/shard_map/all_to_all | solution.py:208
  40.8 0.1 iota_compare_fusion.6
  40.9 0.1 sub.61
  40.9 0.1 lt.94
  41.1 0.8 %scatter_custom_fusion = bf16[576,128]{1,0:T(8,128)(2,1)S(1)} fusion(bf16[576,128]{1,0:T(8,128)(2,1)S(1)} %copy.92, s32[32]{0:T(128)S(1)} %fusion.62, bf16[32,256]{1,0:T(8,128)(2,1)S(1)} %reshape_reshape.7), kind=kCustom, calls=%fused_computation.64 | custom fusion | bytes 155648 | tf_op jit(solution)/shard_map/scatter | solution.py:218
  41.8 0.0 copy-start.1
  41.9 0.8 %scatter_custom_fusion.1 = bf16[576,128]{1,0:T(8,128)(2,1)S(1)} fusion(bf16[576,128]{1,0:T(8,128)(2,1)S(1)} %copy.93, s32[32]{0:T(128)S(1)} %fusion.62, bf16[32,256]{1,0:T(8,128)(2,1)S(1)} %reshape_reshape.7), kind=kCustom, calls=%fused_computation.62 | custom fusion | bytes 155648 | tf_op jit(solution)/shard_map/scatter | solution.py:219
  42.6 0.0 copy-start.2
  42.6 4.6 %all-to-all-done.2 = bf16[8,512,32]{1,2,0:T(8,128)(2,1)S(1)} async-done(((bf16[8,512,32]{1,2,0:T(8,128)(2,1)}), bf16[8,512,32]{1,2,0:T(8,128)(2,1)S(1)}, u32[]{:S(2)}, u32[]{:S(2)}) %all-to-all-start.2) | async-done | bytes 262176 | tf_op jit(solution)/shard_map/all_to_all | solution.py:208
  47.3 0.6 %fusion.35 = bf16[1,32,512]{2,1,0:T(8,128)(2,1)} fusion(f32[512,32]{0,1:T(8,128)S(1)} %convert_reduce_fusion, bf16[1,32,512]{2,1,0:T(8,128)(2,1)S(1)} %copy-done.4), kind=kLoop, calls=%fused_computation.50 | loop fusion | flops 49152 | bytes 131072 | tf_op jit(solution)/shard_map/broadcast_in_dim | solution.py:210
  (32 shorter events, 0.4 us)
Async XLA Ops:
  0.6 10.0 %copy-start = (bf16[1,32,128]{2,1,0:T(8,128)(2,1)S(1)}, bf16[1,32,128]{2,1,0:T(8,128)(2,1)}, u32[]{:S(2)}) copy-start(bf16[1,32,128]{2,1,0:T(8,128)(2,1)} %param.13) | copy-start | bytes 24580
  0.6 13.3 %copy-start.6 = (s32[64]{0:T(128)S(1)}, s32[64]{0:T(128)}, u32[]{:S(2)}) copy-start(s32[64]{0:T(128)} %param.21) | copy-start | bytes 772
  3.9 10.1 %all-to-all-start = ((bf16[4,32,512]{2,1,0:T(8,128)(2,1)}), bf16[4,32,512]{2,1,0:T(8,128)(2,1)S(1)}, u32[]{:S(2)}, u32[]{:S(2)}) async-start(bf16[4,32,512]{2,1,0:T(8,128)(2,1)} %broadcast_in_dim.99), calls=%async_computation | async-start | bytes 262144 | tf_op jit(solution)/shard_map/all_to_all | solution.py:113
  15.1 5.6 %copy-start.3 = (bf16[1,32,512]{2,1,0:T(8,128)(2,1)S(1)}, bf16[1,32,512]{2,1,0:T(8,128)(2,1)}, u32[]{:S(2)}) copy-start(bf16[1,32,512]{2,1,0:T(8,128)(2,1)} %param.11) | copy-start | bytes 98308
  15.1 5.7 %copy-start.5 = (bf16[1,32,128]{2,1,0:T(8,128)(2,1)S(1)}, bf16[1,32,128]{2,1,0:T(8,128)(2,1)}, u32[]{:S(2)}) copy-start(bf16[1,32,128]{2,1,0:T(8,128)(2,1)} %param.12) | copy-start | bytes 24580
  16.5 9.4 %all-to-all-start.1 = ((bf16[4,48,512]{2,1,0:T(8,128)(2,1)}), bf16[4,48,512]{2,1,0:T(8,128)(2,1)S(1)}, u32[]{:S(2)}, u32[]{:S(2)}) async-start(bf16[4,48,512]{2,1,0:T(8,128)(2,1)} %maximum_maximum_fusion), calls=%async_computation.1 | async-start | bytes 393216 | tf_op jit(solution)/shard_map/all_to_all | solution.py:163
  26.9 20.4 %copy-start.4 = (bf16[1,32,512]{2,1,0:T(8,128)(2,1)S(1)}, bf16[1,32,512]{2,1,0:T(8,128)(2,1)}, u32[]{:S(2)}) copy-start(bf16[1,32,512]{2,1,0:T(8,128)(2,1)} %param.16) | copy-start | bytes 98308
  30.6 16.7 %all-to-all-start.2 = ((bf16[8,512,32]{1,2,0:T(8,128)(2,1)}), bf16[8,512,32]{1,2,0:T(8,128)(2,1)S(1)}, u32[]{:S(2)}, u32[]{:S(2)}) async-start(bf16[8,512,32]{1,2,0:T(8,128)(2,1)} %fusion.7), calls=%async_computation.2 | async-start | bytes 524288 | tf_op jit(solution)/shard_map/all_to_all | solution.py:208
  41.8 6.1 %copy-start.1 = (bf16[576,128]{1,0:T(8,128)(2,1)}, bf16[576,128]{1,0:T(8,128)(2,1)S(1)}, u32[]{:S(2)}) copy-start(bf16[576,128]{1,0:T(8,128)(2,1)S(1)} %scatter_custom_fusion) | copy-start | bytes 442372
  42.6 5.3 %copy-start.2 = (bf16[576,128]{1,0:T(8,128)(2,1)}, bf16[576,128]{1,0:T(8,128)(2,1)S(1)}, u32[]{:S(2)}) copy-start(bf16[576,128]{1,0:T(8,128)(2,1)S(1)} %scatter_custom_fusion.1) | copy-start | bytes 442372

commit v13 on v12

--- a/solution.py
+++ b/solution.py
@@ -209,14 +209,26 @@
     summed_heads = jnp.sum(pieces.astype(jnp.float32), axis=0)
     mixed = (residual[0].astype(jnp.float32) + summed_heads.T).astype(jnp.bfloat16)[None]
 
-    row_accepted = lax.dynamic_slice_in_dim(accept_len, group_base, GROUP)
-    column = jnp.arange(A_MAX, dtype=jnp.int32)
-    targets = begin[:, None] + length[:, None] + column[None, :] - low_edge
-    keep_row = (column[None, :] < row_accepted[:, None]) & (targets >= 0) & (targets < positions)
-    targets = jnp.where(keep_row, targets, positions).reshape(-1)
-    rows = row_block.reshape(-1, 2 * channels)
-    new_keys = cache_keys.at[targets].set(rows[:, :channels], mode="drop")
-    new_values = cache_values.at[targets].set(rows[:, channels:], mode="drop")
+    row_accepted = jnp.sum(jnp.where(owners == wanted, accept_len[None, :], 0), axis=1)
+    offset = places[:, None] - (begin + length)[None, :]
+    accepted = (offset >= 0) & (offset < row_accepted[None, :])
+    slot = jnp.arange(GROUP * A_MAX, dtype=jnp.int32)[None, :]
+    request_of = slot // A_MAX
+    picked = jnp.zeros((positions, GROUP * A_MAX), dtype=jnp.bool_)
+    for request in range(GROUP):
+        picked = picked | (
+            (request_of == request)
+            & accepted[:, request : request + 1]
+            & (offset[:, request : request + 1] == slot % A_MAX)
+        )
+    gathered = jnp.dot(
+        picked.astype(jnp.bfloat16),
+        row_block.reshape(GROUP * A_MAX, 2 * channels),
+        preferred_element_type=jnp.float32,
+    ).astype(jnp.bfloat16)
+    matched = jnp.any(accepted, axis=1)[:, None]
+    new_keys = jnp.where(matched, gathered[:, :channels], cache_keys)
+    new_values = jnp.where(matched, gathered[:, channels:], cache_values)
     return (mixed, new_keys, new_values)
 
 

time: 48.6 us -> 48 us (0.988)
  local copies, waits for them, and re-layouts: 6.15 us -> 2.63 us
  matrix products: 8.17 us -> 9.51 us
  other arithmetic: 3.81 us -> 4.72 us
  waiting for transfers between devices: 9.58 us -> 10.1 us
    unnamed x16 -> x12, local copies, waits for them, and re-layouts: 1.88 us -> 0.03 us
    scatter x2 -> x0, local copies, waits for them, and re-layouts: 1.52 us -> none  [the longest x1 0.76 us: on_device(): new_keys = cache_keys.at[targets].set(rows[:, :channels], mode='drop')]
    dot_general x1, matrix products: 0.45 us -> 1.38 us  [on_device(): jnp.einsum('rtkgd,pkd->rkgtp', shaped, keys_local, preferred_element_type...]
    select_n x1 -> x2, other arithmetic: 0.01 us -> 0.87 us  [the longest x1 0.87 us: on_device(): new_values = jnp.where(matched, gathered[:, channels:], cache_values)]
    all_to_all x1, waiting for transfers between devices: 4.65 us -> 5.2 us  [on_device(): pieces = lax.all_to_all(pieces, 'tp', 0, 0, tiled=True)]
  transfers between devices with their start and end apart: 3 -> 3, of which waited for: 2 -> 2; matrix products, arithmetic and copies ran while one was open for 15% -> 14% of each run, Pallas kernels for 0% -> 0%
where the time goes in v13:
time: 48 us; the launch traced here: 47.4 us
  starting transfers between devices  19.5 us (41%)
  waiting for transfers between devices  10.1 us (21%)
  matrix products  9.51 us (20%)
  other arithmetic  4.72 us (10%)
  local copies, waits for them, and re-layouts  2.63 us (5%)
  between operations  0.87 us (2%)
    all_to_all x1, starting transfers between devices, on_device(): pieces = lax.all_to_all(pieces, 'tp', 0, 0, tiled=True)  10.3 us
    all_to_all x1, waiting for transfers between devices, on_device(): pieces = lax.all_to_all(pieces, 'tp', 0, 0, tiled=True)  5.2 us
    all_to_all x1, starting transfers between devices, on_device(): gathered_q = lax.all_to_all(sent, 'mem', 0, 0, tiled=True)  5 us
    all_to_all x1, waiting for transfers between devices, on_device(): partials = lax.all_to_all(message, 'mem', 0, 0, tiled=True)  4.93 us
    all_to_all x1, starting transfers between devices, on_device(): partials = lax.all_to_all(message, 'mem', 0, 0, tiled=True)  4.24 us
    dot_general x1, matrix products, on_device(): lax.dot_general(out_weight.reshape(out_weight.shape[0], tp_size, -1), att...  3.75 us
    broadcast_in_dim x1, local copies, waits for them, and re-layouts, on_device(): sent = jnp.broadcast_to(queries, (GROUP,) + queries.shape[1:])  1.43 us
    dot_general x3, matrix products, ancestry(): jnp.dot(reach, reach, preferred_element_type=jnp.float32) > 0  1.42 us
  transfers between devices with their start and end apart: 3, of which 2 were waited for; matrix products, arithmetic and copies ran while one was open for 14% of the time, Pallas kernels for 0%

profile of v13, /device:TPU:1, one launch (start us, length us, event | category | flops | bytes accessed | tf_op | source)
XLA Modules:
  0.0 47.4 jit_solution(15769324816130500955)
XLA Ops:
  0.6 0.0 copy-start
  0.6 1.4 %broadcast_in_dim.113 = bf16[4,32,512]{2,1,0:T(8,128)(2,1)} broadcast(bf16[32,512]{1,0:T(8,128)(2,1)} %bitcast.148), dimensions={1,2} | broadcast | bytes 163840 | tf_op jit(solution)/shard_map/broadcast_in_dim | solution.py:110
  2.1 5.0 %all-to-all-start = ((bf16[4,32,512]{2,1,0:T(8,128)(2,1)}), bf16[4,32,512]{2,1,0:T(8,128)(2,1)S(1)}, u32[]{:S(2)}, u32[]{:S(2)}) async-start(bf16[4,32,512]{2,1,0:T(8,128)(2,1)} %broadcast_in_dim.113), calls=%async_computation | async-start | bytes 262144 | tf_op jit(solution)/shard_map/all_to_all | solution.py:113
  7.1 0.7 %broadcast_add_fusion = s32[64]{0:T(128)S(1)} fusion(s32[64]{0:T(128)} %param.18), kind=kLoop, calls=%fused_computation.141 | loop fusion | flops 64 | bytes 512 | tf_op jit(solution)/shard_map/add | solution.py:106
  7.7 0.9 %select_reduce_fusion.2 = (s32[4]{0:T(128)S(1)}, s32[4]{0:T(128)S(1)}, s32[4]{0:T(128)S(1)}) fusion(s32[64]{0:T(128)} %param.21, s32[4]{0:T(128)S(1)} %iota_add_fusion.1, s32[64]{0:T(128)} %param.18, s32[64]{0:T(128)S(1)} %broadcast_add_fusion), kind=kLoop, calls=%fused_computation.124 | loop fusion | flops 2036 | bytes 832 | tf_op jit(solution)/shard_map/reduce_sum | solution.py:212
  8.6 0.1 compare_and_fusion.1
  8.7 0.1 broadcast_subtract_fusion
  8.8 0.0 copy-done
  8.8 0.8 %convolution_convert_fusion.2 = bf16[8,128]{1,0:T(8,128)(2,1)S(1)} fusion(bf16[1,32,128]{2,1,0:T(8,128)(2,1)S(1)} %copy-done, s32[8]{0:T(128)} %bitcast.149), kind=kOutput, calls=%fused_computation.26 | convolution fusion | flops 66816 | bytes 10272 | tf_op jit(solution)/shard_map/dot_general | solution.py:147
  9.7 0.9 %convolution_convert_fusion.3 = bf16[8,128]{1,0:T(8,128)(2,1)S(1)} fusion(bf16[1,32,128]{2,1,0:T(8,128)(2,1)} %param.12, s32[8]{0:T(128)} %bitcast.150), kind=kOutput, calls=%fused_computation.27 | convolution fusion | flops 66816 | bytes 10272 | tf_op jit(solution)/shard_map/dot_general | solution.py:146
  10.6 0.9 %convolution_compare_fusion.4 = pred[32,32]{1,0:T(32,128)(4,1)S(1)} fusion(s32[32]{0:T(128)} %bitcast.151), kind=kOutput, calls=%fused_computation.23 | convolution fusion | flops 69632 | bytes 1152 | tf_op jit(solution)/shard_map/dot_general | solution.py:29
  11.5 0.2 convolution_compare_fusion.2
  11.7 0.2 fusion.17
  12.0 0.1 copy.60
  12.1 0.1 fusion.90
  12.2 0.1 slice_reduce_fusion.3
  12.3 0.1 pad.8.clone
  12.4 0.0 copy-start.2
  12.4 0.0 all-to-all-done
  12.4 1.4 %select_reduce_fusion = (bf16[4,4,32]{2,1,0:T(4,128)(2,1)S(1)}, f32[4,1,4,32,576]{4,3,2,0,1:T(8,128)S(1)}) fusion(pred[4,576]{1,0:T(4,128)(4,1)S(1)} %compare_and_fusion.1, bf16[576,128]{1,0:T(8,128)(2,1)} %param.14, bf16[4,32,512]{2,1,0:T(8,128)(2,1)S(1)} %all-to-all-done), kind=kOutput, calls=%fused_computation.6 | convolution fusion | flops 76381696 | bytes 1461504 | tf_op jit(solution)/shard_map/rtkgd,pkd->rkgtp/dot_general | solution.py:123
  13.8 0.1 concatenate.28
  13.9 0.4 fusion.18
  14.3 0.1 concatenate.29
  14.4 0.0 copy-done.2
  14.4 0.0 copy-start.3
  14.4 0.5 fusion.10
  14.8 0.1 copy.56
  14.9 0.1 convert_element_type.131
  15.0 0.8 %maximum_maximum_fusion = bf16[4,48,512]{2,1,0:T(8,128)(2,1)} fusion(bf16[4,4,512]{2,1,0:T(4,128)(2,1)S(1)} %broadcast_in_dim.116, bf16[4,1,512]{2,1,0:T(2,128)(2,1)S(1)} %fusion.70, bf16[4,32,512]{2,1,0:T(8,128)(2,1)S(1)} %convert_element_type.131, bf16[48]{0:T(256)(128)(2,1)S(1)} %pad.8.clone), kind=kLoop, calls=%fused_computation.37 | loop fusion | flops 786432 | bytes 348256 | tf_op jit(solution)/shard_map/concatenate | solution.py:156
  15.8 4.2 %all-to-all-start.1 = ((bf16[4,48,512]{2,1,0:T(8,128)(2,1)}), bf16[4,48,512]{2,1,0:T(8,128)(2,1)S(1)}, u32[]{:S(2)}, u32[]{:S(2)}) async-start(bf16[4,48,512]{2,1,0:T(8,128)(2,1)} %maximum_maximum_fusion), calls=%async_computation.1 | async-start | bytes 393216 | tf_op jit(solution)/shard_map/all_to_all | solution.py:163
  20.0 0.0 copy-done.3
  20.0 0.0 copy-done.5
  20.1 0.2 select_reduce_fusion.1
  20.3 4.9 %all-to-all-done.1 = bf16[4,48,512]{2,1,0:T(8,128)(2,1)S(1)} async-done(((bf16[4,48,512]{2,1,0:T(8,128)(2,1)}), bf16[4,48,512]{2,1,0:T(8,128)(2,1)S(1)}, u32[]{:S(2)}, u32[]{:S(2)}) %all-to-all-start.1) | async-done | bytes 196640 | tf_op jit(solution)/shard_map/all_to_all | solution.py:163
  25.3 0.1 reshape_squeeze.2
  25.4 0.1 copy.62
  25.5 0.2 mul.95
  25.7 0.1 mul.96
  25.9 0.2 fusion.15
  26.2 0.0 copy-start.1
  26.2 3.7 %fusion.7 = bf16[8,512,32]{1,2,0:T(8,128)(2,1)} fusion(bf16[32,512,1]{1,0,2:T(8,128)(2,1)S(1)} %reshape.354, bf16[64,8,8,512]{3,2,1,0:T(8,128)(2,1)} %bitcast.147), kind=kOutput, calls=%fused_computation.9 | convolution fusion | flops 134348800 | bytes 4489216 | tf_op jit(solution)/shard_map/dot_general | solution.py:202
  29.9 10.3 %all-to-all-start.2 = ((bf16[8,512,32]{1,2,0:T(8,128)(2,1)}), bf16[8,512,32]{1,2,0:T(8,128)(2,1)S(1)}, u32[]{:S(2)}, u32[]{:S(2)}) async-start(bf16[8,512,32]{1,2,0:T(8,128)(2,1)} %fusion.7), calls=%async_computation.2 | async-start | bytes 524288 | tf_op jit(solution)/shard_map/all_to_all | solution.py:208
  40.2 0.4 convolution_convert_fusion
  40.6 0.0 copy-done.1
  40.6 0.9 %slice_select_fusion = (bf16[576,128]{1,0:T(8,128)(2,1)}, bf16[576,128]{1,0:T(8,128)(2,1)}) fusion(bf16[576,128]{1,0:T(8,128)(2,1)S(1)} %copy-done.2, bf16[576,256]{1,0:T(8,128)(2,1)S(1)} %convolution_convert_fusion, pred[576]{0:T(1024)(128)(4,1)S(1)} %get-tuple-element.22, bf16[576,128]{1,0:T(8,128)(2,1)S(1)} %copy-done.1), kind=kLoop, calls=%fused_computation.38 | loop fusion | flops 147456 | bytes 885312 | tf_op jit(solution)/shard_map/jit(_where)/select_n | solution.py:231
  41.5 5.2 %all-to-all-done.2 = bf16[8,512,32]{1,2,0:T(8,128)(2,1)S(1)} async-done(((bf16[8,512,32]{1,2,0:T(8,128)(2,1)}), bf16[8,512,32]{1,2,0:T(8,128)(2,1)S(1)}, u32[]{:S(2)}, u32[]{:S(2)}) %all-to-all-start.2) | async-done | bytes 262176 | tf_op jit(solution)/shard_map/all_to_all | solution.py:208
  46.8 0.0 copy-done.4
  46.8 0.6 %fusion.63 = bf16[1,32,512]{2,1,0:T(8,128)(2,1)} fusion(f32[512,32]{0,1:T(8,128)S(1)} %convert_reduce_fusion, bf16[1,32,512]{2,1,0:T(8,128)(2,1)S(1)} %copy-done.4), kind=kLoop, calls=%fused_computation.79 | loop fusion | flops 49152 | bytes 131072 | tf_op jit(solution)/shard_map/broadcast_in_dim | solution.py:210
  (29 shorter events, 0.4 us)
Async XLA Ops:
  0.6 8.2 %copy-start = (bf16[1,32,128]{2,1,0:T(8,128)(2,1)S(1)}, bf16[1,32,128]{2,1,0:T(8,128)(2,1)}, u32[]{:S(2)}) copy-start(bf16[1,32,128]{2,1,0:T(8,128)(2,1)} %param.13) | copy-start | bytes 24580
  2.1 10.3 %all-to-all-start = ((bf16[4,32,512]{2,1,0:T(8,128)(2,1)}), bf16[4,32,512]{2,1,0:T(8,128)(2,1)S(1)}, u32[]{:S(2)}, u32[]{:S(2)}) async-start(bf16[4,32,512]{2,1,0:T(8,128)(2,1)} %broadcast_in_dim.113), calls=%async_computation | async-start | bytes 262144 | tf_op jit(solution)/shard_map/all_to_all | solution.py:113
  12.4 2.0 %copy-start.2 = (bf16[576,128]{1,0:T(8,128)(2,1)S(1)}, bf16[576,128]{1,0:T(8,128)(2,1)}, u32[]{:S(2)}) copy-start(bf16[576,128]{1,0:T(8,128)(2,1)} %param.15) | copy-start | bytes 442372
  14.4 5.7 %copy-start.3 = (bf16[1,32,512]{2,1,0:T(8,128)(2,1)S(1)}, bf16[1,32,512]{2,1,0:T(8,128)(2,1)}, u32[]{:S(2)}) copy-start(bf16[1,32,512]{2,1,0:T(8,128)(2,1)} %param.11) | copy-start | bytes 98308
  14.4 5.7 %copy-start.5 = (bf16[1,32,128]{2,1,0:T(8,128)(2,1)S(1)}, bf16[1,32,128]{2,1,0:T(8,128)(2,1)}, u32[]{:S(2)}) copy-start(bf16[1,32,128]{2,1,0:T(8,128)(2,1)} %param.12) | copy-start | bytes 24580
  15.8 9.4 %all-to-all-start.1 = ((bf16[4,48,512]{2,1,0:T(8,128)(2,1)}), bf16[4,48,512]{2,1,0:T(8,128)(2,1)S(1)}, u32[]{:S(2)}, u32[]{:S(2)}) async-start(bf16[4,48,512]{2,1,0:T(8,128)(2,1)} %maximum_maximum_fusion), calls=%async_computation.1 | async-start | bytes 393216 | tf_op jit(solution)/shard_map/all_to_all | solution.py:163
  26.2 14.5 %copy-start.1 = (bf16[576,128]{1,0:T(8,128)(2,1)S(1)}, bf16[576,128]{1,0:T(8,128)(2,1)}, u32[]{:S(2)}) copy-start(bf16[576,128]{1,0:T(8,128)(2,1)} %param.14) | copy-start | bytes 442372
  29.9 16.8 %copy-start.4 = (bf16[1,32,512]{2,1,0:T(8,128)(2,1)S(1)}, bf16[1,32,512]{2,1,0:T(8,128)(2,1)}, u32[]{:S(2)}) copy-start(bf16[1,32,512]{2,1,0:T(8,128)(2,1)} %param.16) | copy-start | bytes 98308
  29.9 16.8 %all-to-all-start.2 = ((bf16[8,512,32]{1,2,0:T(8,128)(2,1)}), bf16[8,512,32]{1,2,0:T(8,128)(2,1)S(1)}, u32[]{:S(2)}, u32[]{:S(2)}) async-start(bf16[8,512,32]{1,2,0:T(8,128)(2,1)} %fusion.7), calls=%async_computation.2 | async-start | bytes 524288 | tf_op jit(solution)/shard_map/all_to_all | solution.py:208

commit v14 on v13

--- a/solution.py
+++ b/solution.py
@@ -166,8 +166,8 @@
     part_out = partials[:, :TREE]
     stat_count = kv_local * sharing * TREE
     part_stats = partials[:, TREE, : 2 * stat_count].reshape(GROUP, 2, heads_local, TREE)
-    part_top = jnp.transpose(part_stats[:, 0], (0, 2, 1))
-    part_total = jnp.transpose(part_stats[:, 1], (0, 2, 1))
+    part_top = part_stats[:, 0]
+    part_total = part_stats[:, 1]
 
     linked = ancestry(parents[0])
     shaped_q = queries[0].reshape(TREE, kv_local, sharing, HD)
@@ -186,17 +186,19 @@
         own_values,
         preferred_element_type=jnp.float32,
     ).reshape(TREE, q_width)
-    tree_top = jnp.transpose(tree_top, (2, 0, 1)).reshape(TREE, heads_local)
-    tree_total = jnp.transpose(tree_total, (2, 0, 1)).reshape(TREE, heads_local)
+    tree_top = tree_top.reshape(heads_local, TREE)
+    tree_total = tree_total.reshape(heads_local, TREE)
 
     joint_top = jnp.maximum(jnp.max(part_top, axis=0), tree_top)
     part_factor = jnp.exp(part_top - joint_top[None])
     tree_factor = jnp.exp(tree_top - joint_top)
+    joint_total = jnp.sum(part_total * part_factor, axis=0) + tree_total * tree_factor
+    part_factor = jnp.transpose(part_factor, (0, 2, 1))
+    tree_factor = tree_factor.T
     joint_out = jnp.sum(scale_heads(part_out, part_factor), axis=0) + scale_heads(
         tree_out, tree_factor
     )
-    joint_total = jnp.sum(part_total * part_factor, axis=0) + tree_total * tree_factor
-    attention = scale_heads(joint_out, 1.0 / joint_total).astype(jnp.bfloat16)
+    attention = scale_heads(joint_out, 1.0 / joint_total.T).astype(jnp.bfloat16)
 
     tp_size = lax.axis_size("tp")
     pieces = lax.dot_general(

time: 48 us -> 48 us (level)
  no operation moved by 1% of the time
where the time goes in v14:
time: 48 us; the launch traced here: 47.4 us
  starting transfers between devices  19.5 us (41%)
  waiting for transfers between devices  10.1 us (21%)
  matrix products  9.51 us (20%)
  other arithmetic  4.72 us (10%)
  local copies, waits for them, and re-layouts  2.63 us (5%)
  between operations  0.86 us (2%)
    all_to_all x1, starting transfers between devices, on_device(): pieces = lax.all_to_all(pieces, 'tp', 0, 0, tiled=True)  10.3 us
    all_to_all x1, waiting for transfers between devices, on_device(): pieces = lax.all_to_all(pieces, 'tp', 0, 0, tiled=True)  5.2 us
    all_to_all x1, starting transfers between devices, on_device(): gathered_q = lax.all_to_all(sent, 'mem', 0, 0, tiled=True)  5 us
    all_to_all x1, waiting for transfers between devices, on_device(): partials = lax.all_to_all(message, 'mem', 0, 0, tiled=True)  4.93 us
    all_to_all x1, starting transfers between devices, on_device(): partials = lax.all_to_all(message, 'mem', 0, 0, tiled=True)  4.24 us
    dot_general x1, matrix products, on_device(): lax.dot_general(out_weight.reshape(out_weight.shape[0], tp_size, -1), att...  3.75 us
    broadcast_in_dim x1, local copies, waits for them, and re-layouts, on_device(): sent = jnp.broadcast_to(queries, (GROUP,) + queries.shape[1:])  1.43 us
    dot_general x3, matrix products, ancestry(): jnp.dot(reach, reach, preferred_element_type=jnp.float32) > 0  1.42 us
  transfers between devices with their start and end apart: 3, of which 2 were waited for; matrix products, arithmetic and copies ran while one was open for 14% of the time, Pallas kernels for 0%

profile of v14, /device:TPU:1, one launch (start us, length us, event | category | flops | bytes accessed | tf_op | source)
XLA Modules:
  0.0 47.4 jit_solution(17079863707583016454)
XLA Ops:
  0.6 0.0 copy-start
  0.6 1.4 %broadcast_in_dim.113 = bf16[4,32,512]{2,1,0:T(8,128)(2,1)} broadcast(bf16[32,512]{1,0:T(8,128)(2,1)} %bitcast.140), dimensions={1,2} | broadcast | bytes 163840 | tf_op jit(solution)/shard_map/broadcast_in_dim | solution.py:110
  2.1 5.0 %all-to-all-start = ((bf16[4,32,512]{2,1,0:T(8,128)(2,1)}), bf16[4,32,512]{2,1,0:T(8,128)(2,1)S(1)}, u32[]{:S(2)}, u32[]{:S(2)}) async-start(bf16[4,32,512]{2,1,0:T(8,128)(2,1)} %broadcast_in_dim.113), calls=%async_computation | async-start | bytes 262144 | tf_op jit(solution)/shard_map/all_to_all | solution.py:113
  7.1 0.7 %broadcast_add_fusion = s32[64]{0:T(128)S(1)} fusion(s32[64]{0:T(128)} %param.18), kind=kLoop, calls=%fused_computation.141 | loop fusion | flops 64 | bytes 512 | tf_op jit(solution)/shard_map/add | solution.py:106
  7.7 0.9 %select_reduce_fusion.2 = (s32[4]{0:T(128)S(1)}, s32[4]{0:T(128)S(1)}, s32[4]{0:T(128)S(1)}) fusion(s32[64]{0:T(128)} %param.21, s32[4]{0:T(128)S(1)} %iota_add_fusion.1, s32[64]{0:T(128)} %param.18, s32[64]{0:T(128)S(1)} %broadcast_add_fusion), kind=kLoop, calls=%fused_computation.124 | loop fusion | flops 2036 | bytes 832 | tf_op jit(solution)/shard_map/reduce_sum | solution.py:214
  8.6 0.1 compare_and_fusion.1
  8.7 0.1 broadcast_subtract_fusion
  8.8 0.0 copy-done
  8.8 0.8 %convolution_convert_fusion.2 = bf16[8,128]{1,0:T(8,128)(2,1)S(1)} fusion(bf16[1,32,128]{2,1,0:T(8,128)(2,1)S(1)} %copy-done, s32[8]{0:T(128)} %bitcast.141), kind=kOutput, calls=%fused_computation.26 | convolution fusion | flops 66816 | bytes 10272 | tf_op jit(solution)/shard_map/dot_general | solution.py:147
  9.7 0.9 %convolution_convert_fusion.3 = bf16[8,128]{1,0:T(8,128)(2,1)S(1)} fusion(bf16[1,32,128]{2,1,0:T(8,128)(2,1)} %param.12, s32[8]{0:T(128)} %bitcast.142), kind=kOutput, calls=%fused_computation.27 | convolution fusion | flops 66816 | bytes 10272 | tf_op jit(solution)/shard_map/dot_general | solution.py:146
  10.6 0.9 %convolution_compare_fusion.4 = pred[32,32]{1,0:T(32,128)(4,1)S(1)} fusion(s32[32]{0:T(128)} %bitcast.143), kind=kOutput, calls=%fused_computation.23 | convolution fusion | flops 69632 | bytes 1152 | tf_op jit(solution)/shard_map/dot_general | solution.py:29
  11.5 0.2 convolution_compare_fusion.2
  11.7 0.2 fusion.17
  12.0 0.1 copy.60
  12.1 0.1 fusion.91
  12.2 0.1 slice_reduce_fusion.3
  12.3 0.1 pad.8.clone
  12.4 0.0 copy-start.2
  12.4 0.0 all-to-all-done
  12.4 1.4 %select_reduce_fusion = (bf16[4,4,32]{2,1,0:T(4,128)(2,1)S(1)}, f32[4,1,4,32,576]{4,3,2,0,1:T(8,128)S(1)}) fusion(pred[4,576]{1,0:T(4,128)(4,1)S(1)} %compare_and_fusion.1, bf16[576,128]{1,0:T(8,128)(2,1)} %param.14, bf16[4,32,512]{2,1,0:T(8,128)(2,1)S(1)} %all-to-all-done), kind=kOutput, calls=%fused_computation.6 | convolution fusion | flops 76381696 | bytes 1461504 | tf_op jit(solution)/shard_map/rtkgd,pkd->rkgtp/dot_general | solution.py:123
  13.8 0.1 concatenate.28
  13.9 0.4 fusion.18
  14.3 0.1 concatenate.29
  14.4 0.0 copy-done.2
  14.4 0.0 copy-start.3
  14.4 0.5 fusion.10
  14.8 0.1 copy.56
  14.9 0.1 convert_element_type.131
  15.0 0.8 %maximum_maximum_fusion = bf16[4,48,512]{2,1,0:T(8,128)(2,1)} fusion(bf16[4,4,512]{2,1,0:T(4,128)(2,1)S(1)} %broadcast_in_dim.116, bf16[4,1,512]{2,1,0:T(2,128)(2,1)S(1)} %fusion.70, bf16[4,32,512]{2,1,0:T(8,128)(2,1)S(1)} %convert_element_type.131, bf16[48]{0:T(256)(128)(2,1)S(1)} %pad.8.clone), kind=kLoop, calls=%fused_computation.37 | loop fusion | flops 786432 | bytes 348256 | tf_op jit(solution)/shard_map/concatenate | solution.py:156
  15.8 4.2 %all-to-all-start.1 = ((bf16[4,48,512]{2,1,0:T(8,128)(2,1)}), bf16[4,48,512]{2,1,0:T(8,128)(2,1)S(1)}, u32[]{:S(2)}, u32[]{:S(2)}) async-start(bf16[4,48,512]{2,1,0:T(8,128)(2,1)} %maximum_maximum_fusion), calls=%async_computation.1 | async-start | bytes 393216 | tf_op jit(solution)/shard_map/all_to_all | solution.py:163
  20.0 0.0 copy-done.3
  20.0 0.0 copy-done.5
  20.1 0.2 select_reduce_fusion.1
  20.3 4.9 %all-to-all-done.1 = bf16[4,48,512]{2,1,0:T(8,128)(2,1)S(1)} async-done(((bf16[4,48,512]{2,1,0:T(8,128)(2,1)}), bf16[4,48,512]{2,1,0:T(8,128)(2,1)S(1)}, u32[]{:S(2)}, u32[]{:S(2)}) %all-to-all-start.1) | async-done | bytes 196640 | tf_op jit(solution)/shard_map/all_to_all | solution.py:163
  25.3 0.1 reshape_squeeze.2
  25.4 0.1 copy.62
  25.5 0.2 mul.92
  25.7 0.1 mul.93
  25.9 0.2 fusion.15
  26.2 0.0 copy-start.1
  26.2 3.7 %fusion.7 = bf16[8,512,32]{1,2,0:T(8,128)(2,1)} fusion(bf16[32,512,1]{1,0,2:T(8,128)(2,1)S(1)} %reshape.321, bf16[64,8,8,512]{3,2,1,0:T(8,128)(2,1)} %bitcast.139), kind=kOutput, calls=%fused_computation.9 | convolution fusion | flops 134348800 | bytes 4489216 | tf_op jit(solution)/shard_map/dot_general | solution.py:204
  29.9 10.3 %all-to-all-start.2 = ((bf16[8,512,32]{1,2,0:T(8,128)(2,1)}), bf16[8,512,32]{1,2,0:T(8,128)(2,1)S(1)}, u32[]{:S(2)}, u32[]{:S(2)}) async-start(bf16[8,512,32]{1,2,0:T(8,128)(2,1)} %fusion.7), calls=%async_computation.2 | async-start | bytes 524288 | tf_op jit(solution)/shard_map/all_to_all | solution.py:210
  40.2 0.4 convolution_convert_fusion
  40.6 0.0 copy-done.1
  40.6 0.9 %slice_select_fusion = (bf16[576,128]{1,0:T(8,128)(2,1)}, bf16[576,128]{1,0:T(8,128)(2,1)}) fusion(bf16[576,128]{1,0:T(8,128)(2,1)S(1)} %copy-done.2, bf16[576,256]{1,0:T(8,128)(2,1)S(1)} %convolution_convert_fusion, pred[576]{0:T(1024)(128)(4,1)S(1)} %get-tuple-element.22, bf16[576,128]{1,0:T(8,128)(2,1)S(1)} %copy-done.1), kind=kLoop, calls=%fused_computation.38 | loop fusion | flops 147456 | bytes 885312 | tf_op jit(solution)/shard_map/jit(_where)/select_n | solution.py:233
  41.5 5.2 %all-to-all-done.2 = bf16[8,512,32]{1,2,0:T(8,128)(2,1)S(1)} async-done(((bf16[8,512,32]{1,2,0:T(8,128)(2,1)}), bf16[8,512,32]{1,2,0:T(8,128)(2,1)S(1)}, u32[]{:S(2)}, u32[]{:S(2)}) %all-to-all-start.2) | async-done | bytes 262176 | tf_op jit(solution)/shard_map/all_to_all | solution.py:210
  46.8 0.0 copy-done.4
  46.8 0.6 %fusion.63 = bf16[1,32,512]{2,1,0:T(8,128)(2,1)} fusion(f32[512,32]{0,1:T(8,128)S(1)} %convert_reduce_fusion, bf16[1,32,512]{2,1,0:T(8,128)(2,1)S(1)} %copy-done.4), kind=kLoop, calls=%fused_computation.79 | loop fusion | flops 49152 | bytes 131072 | tf_op jit(solution)/shard_map/broadcast_in_dim | solution.py:212
  (29 shorter events, 0.4 us)
Async XLA Ops:
  0.6 8.2 %copy-start = (bf16[1,32,128]{2,1,0:T(8,128)(2,1)S(1)}, bf16[1,32,128]{2,1,0:T(8,128)(2,1)}, u32[]{:S(2)}) copy-start(bf16[1,32,128]{2,1,0:T(8,128)(2,1)} %param.13) | copy-start | bytes 24580
  2.1 10.3 %all-to-all-start = ((bf16[4,32,512]{2,1,0:T(8,128)(2,1)}), bf16[4,32,512]{2,1,0:T(8,128)(2,1)S(1)}, u32[]{:S(2)}, u32[]{:S(2)}) async-start(bf16[4,32,512]{2,1,0:T(8,128)(2,1)} %broadcast_in_dim.113), calls=%async_computation | async-start | bytes 262144 | tf_op jit(solution)/shard_map/all_to_all | solution.py:113
  12.4 2.0 %copy-start.2 = (bf16[576,128]{1,0:T(8,128)(2,1)S(1)}, bf16[576,128]{1,0:T(8,128)(2,1)}, u32[]{:S(2)}) copy-start(bf16[576,128]{1,0:T(8,128)(2,1)} %param.15) | copy-start | bytes 442372
  14.4 5.7 %copy-start.3 = (bf16[1,32,512]{2,1,0:T(8,128)(2,1)S(1)}, bf16[1,32,512]{2,1,0:T(8,128)(2,1)}, u32[]{:S(2)}) copy-start(bf16[1,32,512]{2,1,0:T(8,128)(2,1)} %param.11) | copy-start | bytes 98308
  14.4 5.7 %copy-start.5 = (bf16[1,32,128]{2,1,0:T(8,128)(2,1)S(1)}, bf16[1,32,128]{2,1,0:T(8,128)(2,1)}, u32[]{:S(2)}) copy-start(bf16[1,32,128]{2,1,0:T(8,128)(2,1)} %param.12) | copy-start | bytes 24580
  15.8 9.4 %all-to-all-start.1 = ((bf16[4,48,512]{2,1,0:T(8,128)(2,1)}), bf16[4,48,512]{2,1,0:T(8,128)(2,1)S(1)}, u32[]{:S(2)}, u32[]{:S(2)}) async-start(bf16[4,48,512]{2,1,0:T(8,128)(2,1)} %maximum_maximum_fusion), calls=%async_computation.1 | async-start | bytes 393216 | tf_op jit(solution)/shard_map/all_to_all | solution.py:163
  26.2 14.5 %copy-start.1 = (bf16[576,128]{1,0:T(8,128)(2,1)S(1)}, bf16[576,128]{1,0:T(8,128)(2,1)}, u32[]{:S(2)}) copy-start(bf16[576,128]{1,0:T(8,128)(2,1)} %param.14) | copy-start | bytes 442372
  29.9 16.8 %copy-start.4 = (bf16[1,32,512]{2,1,0:T(8,128)(2,1)S(1)}, bf16[1,32,512]{2,1,0:T(8,128)(2,1)}, u32[]{:S(2)}) copy-start(bf16[1,32,512]{2,1,0:T(8,128)(2,1)} %param.16) | copy-start | bytes 98308
  29.9 16.8 %all-to-all-start.2 = ((bf16[8,512,32]{1,2,0:T(8,128)(2,1)}), bf16[8,512,32]{1,2,0:T(8,128)(2,1)S(1)}, u32[]{:S(2)}, u32[]{:S(2)}) async-start(bf16[8,512,32]{1,2,0:T(8,128)(2,1)} %fusion.7), calls=%async_computation.2 | async-start | bytes 524288 | tf_op jit(solution)/shard_map/all_to_all | solution.py:210
